TPU v7x, 256 devices: a whole 4x4x8 slice. The times are simulated.
256 devices in a mesh: row: 32 (over y, x, z_hi), col: 8 (over z_lo, core).
Axes of the slice: x: 4, y: 4, z: 8 (z_hi: 2, z_lo: 4; z = z_hi * 4 + z_lo), core: 2. Of those that a mesh axis runs over, the one named last changes fastest.
Arguments:
- rhs: float32 [32, 8, 12, 192, 128], P('row', 'col'), may hold values from -6 to 6
- smoother: bfloat16 [32, 8, 3, 3, 768], P('row', 'col'), may hold values from -0.375 to 2.375
- blocks: bfloat16 [32, 8, 12, 192, 1536], P('row', 'col'), may hold values from -0.15625 to 0.15625
- col_index: int32 [32, 8, 12, 8], P('row', 'col'), may hold values from 0 to 27, as said below
- send_list: int32 [32, 8, 4, 4], P('row', 'col'), may hold values from 0 to 11, as said below
- agg_id: int32 [32, 8, 12], P('row', 'col'), may hold values from 0 to 3, as said below
- prolong: bfloat16 [32, 8, 6, 2304], P('row', 'col'), may hold values from -0.4375 to 0.4375
- coarse_inverse: bfloat16 [6144, 6144], P('row'), may hold values from -0.078125 to 0.078125
Outputs:
- smoothed_solution: float32 [32, 8, 12, 192, 128], P('row', 'col')
Inputs may be any that keep to these rules, and one draw needn't show every extreme that they name: `col_index`: A value below 12 names a block row of the same device; the value 12 + 4 * g + j names slot j of ghost group g. Every ghost slot is named by some entry of each device. `send_list`: the 4 blocks of one device and group are distinct. `agg_id`: every aggregate of a device holds at least one block row.
All inputs are finite; a program needn't handle non-finite values.
Results may differ from a plain program's by a relative error of at most 0.0029.
Values may be sent and summed in bfloat16 or wider, within the bound.
No kernel may reach another device: no remote copies, remote signals or barrier semaphores. Data moves between devices by JAX's collectives and lax.ppermute only.
A program may use at most 64 MiB of HBM per device.

v0:
```python
import jax
import jax.numpy as jnp
from jax import lax
from jax.sharding import PartitionSpec as P

damping = 0.6


def passed_along(value, axis, steps):
    count = lax.axis_size(axis)
    pairs = [(source, (source + steps) % count) for source in range(count)]
    return lax.ppermute(value, axis, pairs)


def point_smooth(coefficients, vector):
    leading = vector.shape[:2]
    blocks = vector.shape[2]
    grains = vector.shape[3] // 3
    columns = vector.shape[4]
    factors = coefficients.astype(jnp.float32).reshape(leading + (3, 3, blocks, grains))
    pieces = vector.reshape(leading + (blocks, 3, grains, columns))
    outputs = []
    for component in range(3):
        summed = factors[:, :, component, 0, :, :, None] * pieces[:, :, :, 0]
        summed = summed + factors[:, :, component, 1, :, :, None] * pieces[:, :, :, 1]
        summed = summed + factors[:, :, component, 2, :, :, None] * pieces[:, :, :, 2]
        outputs.append(summed)
    return damping * jnp.stack(outputs, axis=3).reshape(vector.shape)


def body(rhs, smoother, blocks, col_index, send_list, agg_id, prolong, coarse_inverse):
    block_count = rhs.shape[2]
    dof_count = rhs.shape[3]
    vectors = rhs.shape[4]
    send_rows = send_list[0, 0]
    coarse_dofs = prolong.shape[2]
    shaped = prolong[0, 0].reshape((coarse_dofs, block_count, dof_count))

    def apply_operator(vector, ready_ghosts=None):
        vector_low = vector.astype(jnp.bfloat16)
        shard_low = vector_low[0, 0]
        ghosts = []
        for offset in (1, -1):
            packed = jnp.take(shard_low, send_rows[0 if offset == 1 else 1], axis=0)
            ghosts.append(passed_along(packed, "row", offset))
        for offset in (1, -1):
            packed = jnp.take(shard_low, send_rows[2 if offset == 1 else 3], axis=0)
            ghosts.append(passed_along(packed, "col", offset))
        source = jnp.concatenate([shard_low] + list(ghosts), axis=0)
        columns = col_index[0, 0]
        picked = jnp.take(source, columns.reshape(-1), axis=0).reshape((block_count, -1, vectors))
        product = jnp.einsum(
            "nde,ner->ndr", blocks[0, 0], picked, preferred_element_type=jnp.float32
        )
        return product[None, None]

    first_iter = point_smooth(smoother, rhs)
    residual_first = rhs - apply_operator(first_iter)
    update_second = point_smooth(smoother, residual_first)
    second_iter = first_iter + update_second
    residual_second = residual_first - apply_operator(update_second)
    coarse_rows = coarse_inverse.shape[1] // (lax.axis_size("row") * lax.axis_size("col"))
    aggregates = coarse_rows // coarse_dofs
    onehot = (agg_id[0, 0][None, :] == jnp.arange(aggregates, dtype=jnp.int32)[:, None]).astype(
        jnp.float32
    )
    local_terms = jnp.einsum(
        "knd,ndr->nkr",
        shaped,
        residual_second[0, 0].astype(jnp.bfloat16),
        preferred_element_type=jnp.float32,
    )
    coarse_residual = jnp.einsum(
        "an,nkr->akr", onehot, local_terms, precision=lax.Precision.HIGHEST
    )
    coarse_rhs = coarse_residual.astype(jnp.bfloat16).reshape((coarse_rows, vectors))
    column_place = lax.axis_index("col") * coarse_rows
    coarse_solution = jnp.dot(
        coarse_inverse,
        lax.all_gather(coarse_rhs, ("row", "col"), axis=0, tiled=True),
        preferred_element_type=jnp.float32,
    )
    coarse_solution = lax.dynamic_slice_in_dim(coarse_solution, column_place, coarse_rows, 0)
    coarse_rounded = coarse_solution.astype(jnp.bfloat16).reshape(
        (aggregates, coarse_dofs, vectors)
    )
    chosen = jnp.einsum(
        "an,akr->nkr",
        onehot.astype(jnp.bfloat16),
        coarse_rounded,
        preferred_element_type=jnp.float32,
    ).astype(jnp.bfloat16)
    correction = jnp.einsum("knd,nkr->ndr", shaped, chosen, preferred_element_type=jnp.float32)[
        None, None
    ]
    after_coarse = second_iter + correction
    residual_third = residual_second - apply_operator(correction)
    return after_coarse + point_smooth(smoother, residual_third)


def solution(mesh):
    placed = (
        P("row", "col", None, None, None),
        P("row", "col", None, None, None),
        P("row", "col", None, None, None),
        P("row", "col", None, None),
        P("row", "col", None, None),
        P("row", "col", None),
        P("row", "col", None, None),
        P("row", None),
    )
    return jax.shard_map(
        body,
        mesh=mesh,
        in_specs=placed,
        out_specs=P("row", "col", None, None, None),
        check_vma=False,
    )
```

profile of v0, /device:TPU:1, one launch (start us, length us, event | category | flops | bytes accessed | tf_op | source)
XLA Modules:
  0.0 296.1 jit_solution(9077023847655563413)
XLA Ops:
  6.5 1.5 compare_and_fusion.1
  9.5 2.9 multiply_add_fusion.8
  15.5 7.7 %collective-permute-start = (bf16[4,192,128]{2,1,0:T(8,128)(2,1)}, bf16[4,192,128]{2,1,0:T(8,128)(2,1)}, u32[]{:S(2)}, u32[]{:S(2)}) collective-permute-start(bf16[4,192,128]{2,1,0:T(8,128)(2,1)} %broadcast_select_fusion.14), channel_id=1, source_target_pairs={{0,8},{8,16},{16,24},{24,32},{32,40},{40,48},{48,56},{56,64},{64,7... | collective-permute-start | bytes 589832 | tf_op jit(solution)/shard_map/ppermute | solution.py:12
  26.6 4.6 %collective-permute-start.1 = (bf16[4,192,128]{2,1,0:T(8,128)(2,1)}, bf16[4,192,128]{2,1,0:T(8,128)(2,1)}, u32[]{:S(2)}, u32[]{:S(2)}) collective-permute-start(bf16[4,192,128]{2,1,0:T(8,128)(2,1)} %broadcast_select_fusion.11), channel_id=1, source_target_pairs={{0,248},{8,0},{16,8},{24,16},{32,24},{40,32},{48,40},{56,48},{64,5... | collective-permute-start | bytes 589832 | tf_op jit(solution)/shard_map/ppermute | solution.py:12
  34.5 1.6 collective-permute-start.2
  44.4 1.5 reshape_squeeze.9
  47.4 1.6 constant_dynamic-update-slice_fusion.3
  49.0 1.6 constant_dynamic-update-slice_fusion.2
  50.6 1.6 constant_dynamic-update-slice_fusion.1
  52.9 4.8 %gather_fusion.4 = bf16[96,192,128]{2,1,0:T(8,128)(2,1)} fusion(bf16[28,192,128]{2,1,0:T(8,128)(2,1)} %constant_dynamic-update-slice_fusion, s32[1024]{0:T(1024)S(1)} %pad_clamp_fusion), kind=kCustom, calls=%fused_computation.1.clone | custom fusion | bytes 9437568 | tf_op jit(solution)/shard_map/jit(_take)/gather | solution.py:51
  57.8 2.9 broadcast_select_fusion.2
  60.8 5.1 %fusion.15 = f32[1,1,12,192,128]{4,3,2,1,0:T(8,128)S(1)} fusion(f32[1,1,12,192,128]{4,3,2,1,0:T(8,128)S(1)} %copy-done.3, bf16[12,1536,128]{2,1,0:T(8,128)(2,1)S(1)} %bitcast.103, bf16[1,1,12,192,1536]{4,3,2,1,0:T(8,128)(2,1)} %param.14), kind=kOutput, calls=%fused_computation.28 | convolution fusion | flops 906264576 | bytes 14155776 | tf_op jit(solution)/shard_map/nde,ner->ndr/dot_general | solution.py:52
  76.5 8.7 %collective-permute-start.5 = (bf16[4,192,128]{2,1,0:T(8,128)(2,1)S(1)}, bf16[4,192,128]{2,1,0:T(8,128)(2,1)S(1)}, u32[]{:S(2)}, u32[]{:S(2)}) collective-permute-start(bf16[4,192,128]{2,1,0:T(8,128)(2,1)S(1)} %broadcast_select_fusion.10), channel_id=1, source_target_pairs={{0,248},{8,0},{16,8},{24,16},{32,24},{40,32},{48,40},{56,48},{64,5... | collective-permute-start | bytes 589832 | tf_op jit(solution)/shard_map/ppermute | solution.py:12
  85.2 2.3 collective-permute-start.6
  91.4 5.1 %collective-permute-done.6 = bf16[4,192,128]{2,1,0:T(8,128)(2,1)S(1)} collective-permute-done((bf16[4,192,128]{2,1,0:T(8,128)(2,1)S(1)}, bf16[4,192,128]{2,1,0:T(8,128)(2,1)S(1)}, u32[]{:S(2)}, u32[]{:S(2)}) %collective-permute-start.6) | collective-permute-done | bytes 196640 | tf_op jit(solution)/shard_map/ppermute | solution.py:12
  97.2 3.3 %collective-permute-done.7 = bf16[4,192,128]{2,1,0:T(8,128)(2,1)S(1)} collective-permute-done((bf16[4,192,128]{2,1,0:T(8,128)(2,1)S(1)}, bf16[4,192,128]{2,1,0:T(8,128)(2,1)S(1)}, u32[]{:S(2)}, u32[]{:S(2)}) %collective-permute-start.7) | collective-permute-done | bytes 196640 | tf_op jit(solution)/shard_map/ppermute | solution.py:12
  101.3 5.0 %gather_fusion.9 = bf16[96,192,128]{2,1,0:T(8,128)(2,1)} fusion(bf16[28,192,128]{2,1,0:T(8,128)(2,1)} %constant_dynamic-update-slice_fusion.5, s32[1024]{0:T(1024)} %copy-done.32), kind=kCustom, calls=%fused_computation.13.clone | custom fusion | bytes 9437568 | tf_op jit(solution)/shard_map/jit(_take)/gather | solution.py:51
  106.2 2.9 broadcast_select_fusion.1
  109.2 5.0 %fusion.18 = f32[1,1,12,192,128]{4,3,2,1,0:T(8,128)S(1)} fusion(f32[1,1,12,192,128]{4,3,2,1,0:T(8,128)S(1)} %copy-done.2, bf16[12,1536,128]{2,1,0:T(8,128)(2,1)S(1)} %bitcast.102, bf16[1,1,12,192,1536]{4,3,2,1,0:T(8,128)(2,1)} %param.14), kind=kOutput, calls=%fused_computation.29 | convolution fusion | flops 906264576 | bytes 14155776 | tf_op jit(solution)/shard_map/nde,ner->ndr/dot_general | solution.py:52
  116.5 102.9 %all-gather.2.cloned.1.call-done = bf16[6144,128]{1,0:T(8,128)(2,1)} async-done(((bf16[24,128]{1,0:T(8,128)(2,1)}), bf16[6144,128]{1,0:T(8,128)(2,1)}) %all-gather.2.cloned.1.call-update) | async-done | bytes 1572880 | tf_op jit(solution)/shard_map/all_gather | solution.py:80
  219.5 2.2 fusion.43
  224.5 2.6 constant_dynamic-update-slice_fusion.14
  227.1 2.4 gather_fusion.13
  229.5 2.4 gather_fusion.12
  232.0 2.4 gather_fusion.11
  234.4 2.5 gather_fusion.10
  239.9 7.6 %collective-permute-start.9 = (bf16[4,192,128]{2,1,0:T(8,128)(2,1)S(1)}, bf16[4,192,128]{2,1,0:T(8,128)(2,1)S(1)}, u32[]{:S(2)}, u32[]{:S(2)}) collective-permute-start(bf16[4,192,128]{2,1,0:T(8,128)(2,1)S(1)} %broadcast_select_fusion.9), channel_id=1, source_target_pairs={{0,248},{8,0},{16,8},{24,16},{32,24},{40,32},{48,40},{56,48},{64,5... | collective-permute-start | bytes 589832 | tf_op jit(solution)/shard_map/ppermute | solution.py:12
  248.5 1.7 collective-permute-start.10
  250.2 19.2 %collective-permute-done.8 = bf16[4,192,128]{2,1,0:T(8,128)(2,1)S(1)} collective-permute-done((bf16[4,192,128]{2,1,0:T(8,128)(2,1)S(1)}, bf16[4,192,128]{2,1,0:T(8,128)(2,1)S(1)}, u32[]{:S(2)}, u32[]{:S(2)}) %collective-permute-start.8) | collective-permute-done | bytes 196640 | tf_op jit(solution)/shard_map/ppermute | solution.py:12
  272.3 5.0 %gather_fusion.14 = bf16[96,192,128]{2,1,0:T(8,128)(2,1)} fusion(bf16[28,192,128]{2,1,0:T(8,128)(2,1)} %constant_dynamic-update-slice_fusion.10, s32[1024]{0:T(1024)} %copy-done.32), kind=kCustom, calls=%fused_computation.14.clone | custom fusion | bytes 9437568 | tf_op jit(solution)/shard_map/jit(_take)/gather | solution.py:51
  277.2 2.8 broadcast_select_fusion
  280.1 5.1 %fusion.21 = f32[1,1,12,192,128]{4,3,2,1,0:T(8,128)S(1)} fusion(f32[1,1,12,192,128]{4,3,2,1,0:T(8,128)S(1)} %fusion.18, bf16[12,1536,128]{2,1,0:T(8,128)(2,1)S(1)} %bitcast.101, bf16[1,1,12,192,1536]{4,3,2,1,0:T(8,128)(2,1)} %param.14), kind=kOutput, calls=%fused_computation.30 | convolution fusion | flops 906264576 | bytes 14155776 | tf_op jit(solution)/shard_map/nde,ner->ndr/dot_general | solution.py:52
  (143 shorter events, 53.4 us)
Async XLA Ops:
  6.5 213.0 %copy-start = (bf16[192,6144]{1,0:T(8,128)(2,1)S(1)}, bf16[192,6144]{1,0:T(8,128)(2,1)}, u32[]{:S(2)}) copy-start(bf16[192,6144]{1,0:T(8,128)(2,1)} %param.19) | copy-start | bytes 7077892
  6.5 212.9 %all-gather.2.cloned.1.call-start = ((), (), s32[]{:S(2)}) async-start(), calls=%async_computation | async-start | bytes 1579008 | tf_op jit(solution)/shard_map/all_gather | solution.py:80
  15.5 31.9 %collective-permute-start = (bf16[4,192,128]{2,1,0:T(8,128)(2,1)}, bf16[4,192,128]{2,1,0:T(8,128)(2,1)}, u32[]{:S(2)}, u32[]{:S(2)}) collective-permute-start(bf16[4,192,128]{2,1,0:T(8,128)(2,1)} %broadcast_select_fusion.14), channel_id=1, source_target_pairs={{0,8},{8,16},{16,24},{24,32},{32,40},{40,48},{48,56},{56,64},{64,7... | collective-permute-start | bytes 589832 | tf_op jit(solution)/shard_map/ppermute | solution.py:12
  26.6 22.4 %collective-permute-start.1 = (bf16[4,192,128]{2,1,0:T(8,128)(2,1)}, bf16[4,192,128]{2,1,0:T(8,128)(2,1)}, u32[]{:S(2)}, u32[]{:S(2)}) collective-permute-start(bf16[4,192,128]{2,1,0:T(8,128)(2,1)} %broadcast_select_fusion.11), channel_id=1, source_target_pairs={{0,248},{8,0},{16,8},{24,16},{32,24},{40,32},{48,40},{56,48},{64,5... | collective-permute-start | bytes 589832 | tf_op jit(solution)/shard_map/ppermute | solution.py:12
  34.5 16.1 %collective-permute-start.2 = (bf16[4,192,128]{2,1,0:T(8,128)(2,1)}, bf16[4,192,128]{2,1,0:T(8,128)(2,1)}, u32[]{:S(2)}, u32[]{:S(2)}) collective-permute-start(bf16[4,192,128]{2,1,0:T(8,128)(2,1)} %broadcast_select_fusion.8), channel_id=1, source_target_pairs={{0,1},{1,2},{2,3},{3,4},{4,5},{5,6},{6,7},{7,0},{8,9},{9,10},{10,1... | collective-permute-start | bytes 589832 | tf_op jit(solution)/shard_map/ppermute | solution.py:12
  39.4 12.8 %collective-permute-start.3 = (bf16[4,192,128]{2,1,0:T(8,128)(2,1)}, bf16[4,192,128]{2,1,0:T(8,128)(2,1)S(1)}, u32[]{:S(2)}, u32[]{:S(2)}) collective-permute-start(bf16[4,192,128]{2,1,0:T(8,128)(2,1)} %broadcast_select_fusion.5), channel_id=1, source_target_pairs={{0,7},{1,0},{2,1},{3,2},{4,3},{5,4},{6,5},{7,6},{8,15},{9,8},{10,9... | collective-permute-start | bytes 589832 | tf_op jit(solution)/shard_map/ppermute | solution.py:12
  47.4 10.4 %copy-start.32 = (s32[1024]{0:T(1024)}, s32[1024]{0:T(1024)S(1)}, u32[]{:S(2)}) copy-start(s32[1024]{0:T(1024)S(1)} %pad_clamp_fusion) | copy-start | bytes 12292
  60.7 5.2 %copy-start.12 = (f32[12,64]{1,0:T(8,128)S(1)}, f32[12,64]{1,0:T(8,128)}, u32[]{:S(2)}) copy-start(f32[12,64]{1,0:T(8,128)} %copy-done.11) | copy-start | bytes 9220
  60.7 5.2 %copy-start.15 = (f32[12,64]{1,0:T(8,128)S(1)}, f32[12,64]{1,0:T(8,128)}, u32[]{:S(2)}) copy-start(f32[12,64]{1,0:T(8,128)} %copy-done.14) | copy-start | bytes 9220
  60.7 5.2 %copy-start.18 = (f32[12,64]{1,0:T(8,128)S(1)}, f32[12,64]{1,0:T(8,128)}, u32[]{:S(2)}) copy-start(f32[12,64]{1,0:T(8,128)} %copy-done.17) | copy-start | bytes 9220
  60.7 5.2 %copy-start.21 = (f32[12,64]{1,0:T(8,128)S(1)}, f32[12,64]{1,0:T(8,128)}, u32[]{:S(2)}) copy-start(f32[12,64]{1,0:T(8,128)} %copy-done.20) | copy-start | bytes 9220
  60.8 5.2 %copy-start.24 = (f32[12,64]{1,0:T(8,128)S(1)}, f32[12,64]{1,0:T(8,128)}, u32[]{:S(2)}) copy-start(f32[12,64]{1,0:T(8,128)} %copy-done.23) | copy-start | bytes 9220
  60.8 5.2 %copy-start.27 = (f32[12,64]{1,0:T(8,128)S(1)}, f32[12,64]{1,0:T(8,128)}, u32[]{:S(2)}) copy-start(f32[12,64]{1,0:T(8,128)} %copy-done.26) | copy-start | bytes 9220
  60.8 5.2 %copy-start.30 = (f32[12,64]{1,0:T(8,128)S(1)}, f32[12,64]{1,0:T(8,128)}, u32[]{:S(2)}) copy-start(f32[12,64]{1,0:T(8,128)} %copy-done.29) | copy-start | bytes 9220
  74.7 14.9 %collective-permute-start.4 = (bf16[4,192,128]{2,1,0:T(8,128)(2,1)S(1)}, bf16[4,192,128]{2,1,0:T(8,128)(2,1)S(1)}, u32[]{:S(2)}, u32[]{:S(2)}) collective-permute-start(bf16[4,192,128]{2,1,0:T(8,128)(2,1)S(1)} %broadcast_select_fusion.13), channel_id=1, source_target_pairs={{0,8},{8,16},{16,24},{24,32},{32,40},{40,48},{48,56},{56,64},{64,7... | collective-permute-start | bytes 589832 | tf_op jit(solution)/shard_map/ppermute | solution.py:12
  76.5 14.2 %collective-permute-start.5 = (bf16[4,192,128]{2,1,0:T(8,128)(2,1)S(1)}, bf16[4,192,128]{2,1,0:T(8,128)(2,1)S(1)}, u32[]{:S(2)}, u32[]{:S(2)}) collective-permute-start(bf16[4,192,128]{2,1,0:T(8,128)(2,1)S(1)} %broadcast_select_fusion.10), channel_id=1, source_target_pairs={{0,248},{8,0},{16,8},{24,16},{32,24},{40,32},{48,40},{56,48},{64,5... | collective-permute-start | bytes 589832 | tf_op jit(solution)/shard_map/ppermute | solution.py:12
  85.2 11.4 %collective-permute-start.6 = (bf16[4,192,128]{2,1,0:T(8,128)(2,1)S(1)}, bf16[4,192,128]{2,1,0:T(8,128)(2,1)S(1)}, u32[]{:S(2)}, u32[]{:S(2)}) collective-permute-start(bf16[4,192,128]{2,1,0:T(8,128)(2,1)S(1)} %broadcast_select_fusion.7), channel_id=1, source_target_pairs={{0,1},{1,2},{2,3},{3,4},{4,5},{5,6},{6,7},{7,0},{8,9},{9,10},{10,1... | collective-permute-start | bytes 589832 | tf_op jit(solution)/shard_map/ppermute | solution.py:12
  87.5 13.1 %collective-permute-start.7 = (bf16[4,192,128]{2,1,0:T(8,128)(2,1)S(1)}, bf16[4,192,128]{2,1,0:T(8,128)(2,1)S(1)}, u32[]{:S(2)}, u32[]{:S(2)}) collective-permute-start(bf16[4,192,128]{2,1,0:T(8,128)(2,1)S(1)} %broadcast_select_fusion.4), channel_id=1, source_target_pairs={{0,7},{1,0},{2,1},{3,2},{4,3},{5,4},{6,5},{7,6},{8,15},{9,8},{10,9... | collective-permute-start | bytes 589832 | tf_op jit(solution)/shard_map/ppermute | solution.py:12
  101.3 5.0 %copy-start.34 = (pred[96]{0:T(512)(128)(4,1)S(1)}, pred[96]{0:T(512)(128)(4,1)}, u32[]{:S(2)}) copy-start(pred[96]{0:T(512)(128)(4,1)} %compare_and_fusion) | copy-start | bytes 292
  109.2 5.0 %copy-start.10 = (bf16[6,12,192]{2,1,0:T(8,128)(2,1)S(1)}, bf16[6,12,192]{2,1,0:T(8,128)(2,1)}, u32[]{:S(2)}) copy-start(bf16[6,12,192]{2,1,0:T(8,128)(2,1)} %reshape_squeeze.9) | copy-start | bytes 82948
  109.2 5.3 %copy-start.35 = (s32[1,1,12]{2,1,0:T(1,128)S(1)}, s32[1,1,12]{2,1,0:T(1,128)}, u32[]{:S(2)}) copy-start(s32[1,1,12]{2,1,0:T(1,128)} %param.17) | copy-start | bytes 148
  239.9 30.3 %collective-permute-start.9 = (bf16[4,192,128]{2,1,0:T(8,128)(2,1)S(1)}, bf16[4,192,128]{2,1,0:T(8,128)(2,1)S(1)}, u32[]{:S(2)}, u32[]{:S(2)}) collective-permute-start(bf16[4,192,128]{2,1,0:T(8,128)(2,1)S(1)} %broadcast_select_fusion.9), channel_id=1, source_target_pairs={{0,248},{8,0},{16,8},{24,16},{32,24},{40,32},{48,40},{56,48},{64,5... | collective-permute-start | bytes 589832 | tf_op jit(solution)/shard_map/ppermute | solution.py:12
  247.5 22.0 %collective-permute-start.8 = (bf16[4,192,128]{2,1,0:T(8,128)(2,1)S(1)}, bf16[4,192,128]{2,1,0:T(8,128)(2,1)S(1)}, u32[]{:S(2)}, u32[]{:S(2)}) collective-permute-start(bf16[4,192,128]{2,1,0:T(8,128)(2,1)S(1)} %broadcast_select_fusion.12), channel_id=1, source_target_pairs={{0,8},{8,16},{16,24},{24,32},{32,40},{40,48},{48,56},{56,64},{64,7... | collective-permute-start | bytes 589832 | tf_op jit(solution)/shard_map/ppermute | solution.py:12
  248.5 22.3 %collective-permute-start.10 = (bf16[4,192,128]{2,1,0:T(8,128)(2,1)S(1)}, bf16[4,192,128]{2,1,0:T(8,128)(2,1)S(1)}, u32[]{:S(2)}, u32[]{:S(2)}) collective-permute-start(bf16[4,192,128]{2,1,0:T(8,128)(2,1)S(1)} %broadcast_select_fusion.6), channel_id=1, source_target_pairs={{0,1},{1,2},{2,3},{3,4},{4,5},{5,6},{6,7},{7,0},{8,9},{9,10},{10,1... | collective-permute-start | bytes 589832 | tf_op jit(solution)/shard_map/ppermute | solution.py:12
  250.2 21.3 %collective-permute-start.11 = (bf16[4,192,128]{2,1,0:T(8,128)(2,1)S(1)}, bf16[4,192,128]{2,1,0:T(8,128)(2,1)S(1)}, u32[]{:S(2)}, u32[]{:S(2)}) collective-permute-start(bf16[4,192,128]{2,1,0:T(8,128)(2,1)S(1)} %broadcast_select_fusion.3), channel_id=1, source_target_pairs={{0,7},{1,0},{2,1},{3,2},{4,3},{5,4},{6,5},{7,6},{8,15},{9,8},{10,9... | collective-permute-start | bytes 589832 | tf_op jit(solution)/shard_map/ppermute | solution.py:12
  280.0 5.1 %copy-start.13 = (f32[12,64]{1,0:T(8,128)S(1)}, f32[12,64]{1,0:T(8,128)}, u32[]{:S(2)}) copy-start(f32[12,64]{1,0:T(8,128)} %copy-done.11) | copy-start | bytes 9220
  280.1 5.1 %copy-start.16 = (f32[12,64]{1,0:T(8,128)S(1)}, f32[12,64]{1,0:T(8,128)}, u32[]{:S(2)}) copy-start(f32[12,64]{1,0:T(8,128)} %copy-done.14) | copy-start | bytes 9220
  280.1 5.1 %copy-start.19 = (f32[12,64]{1,0:T(8,128)S(1)}, f32[12,64]{1,0:T(8,128)}, u32[]{:S(2)}) copy-start(f32[12,64]{1,0:T(8,128)} %copy-done.17) | copy-start | bytes 9220
  280.1 5.1 %copy-start.22 = (f32[12,64]{1,0:T(8,128)S(1)}, f32[12,64]{1,0:T(8,128)}, u32[]{:S(2)}) copy-start(f32[12,64]{1,0:T(8,128)} %copy-done.20) | copy-start | bytes 9220
  280.1 5.1 %copy-start.25 = (f32[12,64]{1,0:T(8,128)S(1)}, f32[12,64]{1,0:T(8,128)}, u32[]{:S(2)}) copy-start(f32[12,64]{1,0:T(8,128)} %copy-done.23) | copy-start | bytes 9220
  280.1 5.1 %copy-start.28 = (f32[12,64]{1,0:T(8,128)S(1)}, f32[12,64]{1,0:T(8,128)}, u32[]{:S(2)}) copy-start(f32[12,64]{1,0:T(8,128)} %copy-done.26) | copy-start | bytes 9220
  280.1 5.1 %copy-start.31 = (f32[12,64]{1,0:T(8,128)S(1)}, f32[12,64]{1,0:T(8,128)}, u32[]{:S(2)}) copy-start(f32[12,64]{1,0:T(8,128)} %copy-done.29) | copy-start | bytes 9220
  (17 other events, 48.2 us)
Sparse Core Ops, SparseCore 0:
  116.7 102.7 all-gather.1
where the time goes:
time: 297 us; the launch traced here: 296 us
  waiting for transfers between devices  131 us (44%)
  local copies, waits for them, and re-layouts  54.9 us (18%)
  other arithmetic  38.2 us (13%)
  starting transfers between devices  36.5 us (12%)
  matrix products  21.3 us (7%)
  between operations  14.1 us (5%)
    all_gather x1, waiting for transfers between devices, body(): lax.all_gather(coarse_rhs, ('row', 'col'), axis=0, tiled=True)  103 us
    ppermute x12, starting transfers between devices, passed_along(): return lax.ppermute(value, axis, pairs)  36.5 us
    ppermute x12, waiting for transfers between devices, passed_along(): return lax.ppermute(value, axis, pairs)  28.2 us
    dot_general x3, matrix products, apply_operator(): jnp.einsum('nde,ner->ndr', blocks[0, 0], picked, preferred_element_type=j...  15.1 us
    gather x3, local copies, waits for them, and re-layouts, apply_operator(): jnp.take(source, columns.reshape(-1), axis=0)  14.7 us
    unnamed x84, local copies, waits for them, and re-layouts  14.6 us
    select_n x4, other arithmetic, apply_operator(): jnp.take(source, columns.reshape(-1), axis=0)  9.78 us
    gather x6, local copies, waits for them, and re-layouts, apply_operator(): packed = jnp.take(shard_low, send_rows[2 if offset == 1 else 3], axis=0)  8.34 us
  transfers between devices with their start and end apart: 13, of which 5 were waited for; matrix products, arithmetic and copies ran while one was open for 10% of the time, Pallas kernels for 0%

commit v1 on v0

--- a/solution.py
+++ b/solution.py
@@ -1,6 +1,10 @@
+import functools
+
 import jax
 import jax.numpy as jnp
 from jax import lax
+from jax.experimental import pallas as pl
+from jax.experimental.pallas import tpu as pltpu
 from jax.sharding import PartitionSpec as P
 
 damping = 0.6
@@ -28,6 +32,45 @@
     return damping * jnp.stack(outputs, axis=3).reshape(vector.shape)
 
 
+def product_kernel(stored, columns_ref, blocks_ref, source_ref, out_ref, picked):
+    n = pl.program_id(0)
+    dof = source_ref.shape[1]
+    for k in range(stored):
+        picked[k * dof:(k + 1) * dof, :] = source_ref[columns_ref[n * stored + k]]
+    out_ref[0] = jnp.dot(blocks_ref[0], picked[...], preferred_element_type=jnp.float32)
+
+
+def block_product(blocks, columns, source):
+    block_count, dof, width = blocks.shape
+    stored = width // dof
+    vectors = source.shape[-1]
+    grid_spec = pltpu.PrefetchScalarGridSpec(
+        num_scalar_prefetch=1,
+        grid=(block_count,),
+        in_specs=[
+            pl.BlockSpec((1, dof, width), lambda n, c: (n, 0, 0)),
+            pl.BlockSpec(source.shape, lambda n, c: (0, 0, 0)),
+        ],
+        out_specs=pl.BlockSpec((1, dof, vectors), lambda n, c: (n, 0, 0)),
+        scratch_shapes=[pltpu.VMEM((width, vectors), source.dtype)],
+    )
+    flops = 2 * block_count * dof * width * vectors
+    moved = blocks.size * 2 + source.size * 2 + block_count * dof * vectors * 4
+    return pl.pallas_call(
+        functools.partial(product_kernel, stored),
+        grid_spec=grid_spec,
+        out_shape=jax.ShapeDtypeStruct((block_count, dof, vectors), jnp.float32),
+        cost_estimate=pl.CostEstimate(flops=flops, bytes_accessed=moved, transcendentals=0),
+    )(columns.reshape(-1), blocks, source)
+
+
+def gathered_copies(value, axis):
+    count = lax.axis_size(axis)
+    repeated = jnp.broadcast_to(value[None], (count,) + value.shape)
+    repeated = repeated.reshape((count * value.shape[0],) + value.shape[1:])
+    return lax.all_to_all(repeated, axis, 0, 0, tiled=True)
+
+
 def body(rhs, smoother, blocks, col_index, send_list, agg_id, prolong, coarse_inverse):
     block_count = rhs.shape[2]
     dof_count = rhs.shape[3]
@@ -35,8 +78,10 @@
     send_rows = send_list[0, 0]
     coarse_dofs = prolong.shape[2]
     shaped = prolong[0, 0].reshape((coarse_dofs, block_count, dof_count))
+    local_blocks = blocks[0, 0]
+    columns = col_index[0, 0]
 
-    def apply_operator(vector, ready_ghosts=None):
+    def apply_operator(vector):
         vector_low = vector.astype(jnp.bfloat16)
         shard_low = vector_low[0, 0]
         ghosts = []
@@ -47,19 +92,16 @@
             packed = jnp.take(shard_low, send_rows[2 if offset == 1 else 3], axis=0)
             ghosts.append(passed_along(packed, "col", offset))
         source = jnp.concatenate([shard_low] + list(ghosts), axis=0)
-        columns = col_index[0, 0]
-        picked = jnp.take(source, columns.reshape(-1), axis=0).reshape((block_count, -1, vectors))
-        product = jnp.einsum(
-            "nde,ner->ndr", blocks[0, 0], picked, preferred_element_type=jnp.float32
-        )
-        return product[None, None]
+        return block_product(local_blocks, columns, source)[None, None]
 
     first_iter = point_smooth(smoother, rhs)
     residual_first = rhs - apply_operator(first_iter)
     update_second = point_smooth(smoother, residual_first)
     second_iter = first_iter + update_second
     residual_second = residual_first - apply_operator(update_second)
-    coarse_rows = coarse_inverse.shape[1] // (lax.axis_size("row") * lax.axis_size("col"))
+    row_count = lax.axis_size("row")
+    col_count = lax.axis_size("col")
+    coarse_rows = coarse_inverse.shape[1] // (row_count * col_count)
     aggregates = coarse_rows // coarse_dofs
     onehot = (agg_id[0, 0][None, :] == jnp.arange(aggregates, dtype=jnp.int32)[:, None]).astype(
         jnp.float32
@@ -74,13 +116,13 @@
         "an,nkr->akr", onehot, local_terms, precision=lax.Precision.HIGHEST
     )
     coarse_rhs = coarse_residual.astype(jnp.bfloat16).reshape((coarse_rows, vectors))
-    column_place = lax.axis_index("col") * coarse_rows
-    coarse_solution = jnp.dot(
-        coarse_inverse,
-        lax.all_gather(coarse_rhs, ("row", "col"), axis=0, tiled=True),
-        preferred_element_type=jnp.float32,
-    )
-    coarse_solution = lax.dynamic_slice_in_dim(coarse_solution, column_place, coarse_rows, 0)
+    column_part = gathered_copies(coarse_rhs, "row")
+    held = coarse_inverse.reshape((coarse_inverse.shape[0], row_count, col_count, coarse_rows))
+    held = lax.dynamic_slice_in_dim(held, lax.axis_index("col"), 1, 2)
+    held = held.reshape((coarse_inverse.shape[0], row_count * coarse_rows))
+    partial = jnp.dot(held, column_part, preferred_element_type=jnp.float32)
+    partial = lax.all_to_all(partial, "col", 0, 0, tiled=True)
+    coarse_solution = partial.reshape((col_count, coarse_rows, vectors)).sum(axis=0)
     coarse_rounded = coarse_solution.astype(jnp.bfloat16).reshape(
         (aggregates, coarse_dofs, vectors)
     )

time: 297 us -> 186 us (0.63)
  waiting for transfers between devices: 131 us -> 47 us
  Pallas kernels: 0 us -> 33.8 us
  local copies, waits for them, and re-layouts: 54.9 us -> 25.8 us
  other arithmetic: 38.2 us -> 15.2 us
  matrix products: 21.3 us -> 4.79 us
  between operations: 14.1 us -> 0.86 us
  blocking collectives: 0 us -> 12 us
  starting transfers between devices: 36.5 us -> 43.8 us
    all_gather x1 -> x0, waiting for transfers between devices: 103 us -> none  [body(): lax.all_gather(coarse_rhs, ('row', 'col'), axis=0, tiled=True)]
    pallas_call x0 -> x3, Pallas kernels: none -> 33.8 us  [block_product(): pl.pallas_call(functools.partial(product_kernel, stored), grid_spec=grid_...]
    dot_general x4 -> x1, matrix products: 17.3 us -> 1.51 us  [body(): partial = jnp.dot(held, column_part, preferred_element_type=jnp.float32)]
    gather x3 -> x0, local copies, waits for them, and re-layouts: 14.7 us -> none  [apply_operator(): jnp.take(source, columns.reshape(-1), axis=0)]
    all_to_all x0 -> x1, blocking collectives: none -> 12 us  [body(): partial = lax.all_to_all(partial, 'col', 0, 0, tiled=True)]
    ppermute x12, waiting for transfers between devices: 28.2 us -> 40 us  [passed_along(): return lax.ppermute(value, axis, pairs)]
    all_to_all x0 -> x1, starting transfers between devices: none -> 10.9 us  [gathered_copies(): return lax.all_to_all(repeated, axis, 0, 0, tiled=True)]
    select_n x4 -> x0, other arithmetic: 9.78 us -> none  [apply_operator(): jnp.take(source, columns.reshape(-1), axis=0)]
  transfers between devices with their start and end apart: 13 -> 13, of which waited for: 5 -> 9; matrix products, arithmetic and copies ran while one was open for 10% -> 6% of each run, Pallas kernels for 0% -> 0%
where the time goes in v1:
time: 186 us; the launch traced here: 183 us
  waiting for transfers between devices  47 us (25%)
  starting transfers between devices  43.8 us (24%)
  Pallas kernels  33.8 us (18%)
  local copies, waits for them, and re-layouts  25.8 us (14%)
  other arithmetic  15.2 us (8%)
  blocking collectives  12 us (6%)
  matrix products  4.79 us (3%)
    ppermute x12, waiting for transfers between devices, passed_along(): return lax.ppermute(value, axis, pairs)  40 us
    pallas_call x3, Pallas kernels, block_product(): pl.pallas_call(functools.partial(product_kernel, stored), grid_spec=grid_...  33.8 us
    ppermute x12, starting transfers between devices, passed_along(): return lax.ppermute(value, axis, pairs)  33 us
    all_to_all x1, blocking collectives, body(): partial = lax.all_to_all(partial, 'col', 0, 0, tiled=True)  12 us
    all_to_all x1, starting transfers between devices, gathered_copies(): return lax.all_to_all(repeated, axis, 0, 0, tiled=True)  10.9 us
    unnamed x103, local copies, waits for them, and re-layouts  8.65 us
    all_to_all x1, waiting for transfers between devices, gathered_copies(): return lax.all_to_all(repeated, axis, 0, 0, tiled=True)  6.94 us
    add x3, other arithmetic, point_smooth(): summed + factors[:, :, component, 2, :, :, None] * pieces[:, :, :, 2]  5.3 us
  transfers between devices with their start and end apart: 13, of which 9 were waited for; matrix products, arithmetic and copies ran while one was open for 6% of the time, Pallas kernels for 0%

profile of v1, /device:TPU:1, one launch (start us, length us, event | category | flops | bytes accessed | tf_op | source)
XLA Modules:
  0.0 183.3 jit_solution(6689511953574966885)
XLA Ops:
  1.8 2.9 %multiply_add_fusion.8 = (f32[1,1,12,1,64,128]{5,4,3,2,1,0:T(8,128)S(1)}, f32[1,1,12,1,64,128]{5,4,3,2,1,0:T(8,128)S(1)}, f32[1,1,12,1,64,128]{5,4,3,2,1,0:T(8,128)S(1)}) fusion(f32[1,1,12,3,64,128]{5,4,3,2,1,0:T(8,128)} %bitcast.89, f32[12,64]{1,0:T(8,128)S(1)} %get-tuple-element.34, f32[12,64]{1,0:T(8,128)S(1)} %get-tuple-element.35, ...), kind=kLoop, calls=%fused_computation.37 | loop fusion | flops 1474560 | bytes 2386944 | tf_op jit(solution)/shard_map/add | solution.py:30
  5.7 7.8 %collective-permute-start = (bf16[4,192,128]{2,1,0:T(8,128)(2,1)S(1)}, bf16[4,192,128]{2,1,0:T(8,128)(2,1)S(1)}, u32[]{:S(2)}, u32[]{:S(2)}) collective-permute-start(bf16[4,192,128]{2,1,0:T(8,128)(2,1)S(1)} %broadcast_select_fusion.11), channel_id=1, source_target_pairs={{0,8},{8,16},{16,24},{24,32},{32,40},{40,48},{48,56},{56,64},{64,7... | collective-permute-start | bytes 589832 | tf_op jit(solution)/shard_map/ppermute | solution.py:16
  14.2 4.8 %collective-permute-start.1 = (bf16[4,192,128]{2,1,0:T(8,128)(2,1)S(1)}, bf16[4,192,128]{2,1,0:T(8,128)(2,1)S(1)}, u32[]{:S(2)}, u32[]{:S(2)}) collective-permute-start(bf16[4,192,128]{2,1,0:T(8,128)(2,1)S(1)} %broadcast_select_fusion.8), channel_id=1, source_target_pairs={{0,248},{8,0},{16,8},{24,16},{32,24},{40,32},{48,40},{56,48},{64,5... | collective-permute-start | bytes 589832 | tf_op jit(solution)/shard_map/ppermute | solution.py:16
  19.6 1.7 collective-permute-start.2
  23.7 3.4 %collective-permute-done.1 = bf16[4,192,128]{2,1,0:T(8,128)(2,1)S(1)} collective-permute-done((bf16[4,192,128]{2,1,0:T(8,128)(2,1)S(1)}, bf16[4,192,128]{2,1,0:T(8,128)(2,1)S(1)}, u32[]{:S(2)}, u32[]{:S(2)}) %collective-permute-start.1) | collective-permute-done | bytes 196640 | tf_op jit(solution)/shard_map/ppermute | solution.py:16
  27.1 7.7 %collective-permute-done.2 = bf16[4,192,128]{2,1,0:T(8,128)(2,1)S(1)} collective-permute-done((bf16[4,192,128]{2,1,0:T(8,128)(2,1)S(1)}, bf16[4,192,128]{2,1,0:T(8,128)(2,1)S(1)}, u32[]{:S(2)}, u32[]{:S(2)}) %collective-permute-start.2) | collective-permute-done | bytes 196640 | tf_op jit(solution)/shard_map/ppermute | solution.py:16
  34.8 1.6 collective-permute-done.3
  37.6 11.3 %shard_map.82 = f32[12,192,128]{2,1,0:T(8,128)} custom-call(s32[96]{0:T(128)} %reshape_squeeze.8.columns_ref, bf16[12,192,1536]{2,1,0:T(8,128)(2,1)} %bitcast.75, bf16[28,192,128]{2,1,0:T(8,128)(2,1)} %copy-done.3), custom_call_target="tpu_custom_call" | custom-call | flops 905969664 | bytes 9633792 | tf_op jit(solution)/shard_map/pallas_call | solution.py:59
  48.9 1.4 bitcast_subtract_fusion.2
  51.6 1.3 fusion.3
  56.4 9.6 %collective-permute-start.5 = (bf16[4,192,128]{2,1,0:T(8,128)(2,1)S(1)}, bf16[4,192,128]{2,1,0:T(8,128)(2,1)S(1)}, u32[]{:S(2)}, u32[]{:S(2)}) collective-permute-start(bf16[4,192,128]{2,1,0:T(8,128)(2,1)S(1)} %broadcast_select_fusion.7), channel_id=1, source_target_pairs={{0,248},{8,0},{16,8},{24,16},{32,24},{40,32},{48,40},{56,48},{64,5... | collective-permute-start | bytes 589832 | tf_op jit(solution)/shard_map/ppermute | solution.py:16
  66.1 1.4 collective-permute-start.6
  67.6 5.3 %collective-permute-done.4 = bf16[4,192,128]{2,1,0:T(8,128)(2,1)S(1)} collective-permute-done((bf16[4,192,128]{2,1,0:T(8,128)(2,1)S(1)}, bf16[4,192,128]{2,1,0:T(8,128)(2,1)S(1)}, u32[]{:S(2)}, u32[]{:S(2)}) %collective-permute-start.4) | collective-permute-done | bytes 196640 | tf_op jit(solution)/shard_map/ppermute | solution.py:16
  72.9 6.9 %collective-permute-done.5 = bf16[4,192,128]{2,1,0:T(8,128)(2,1)S(1)} collective-permute-done((bf16[4,192,128]{2,1,0:T(8,128)(2,1)S(1)}, bf16[4,192,128]{2,1,0:T(8,128)(2,1)S(1)}, u32[]{:S(2)}, u32[]{:S(2)}) %collective-permute-start.5) | collective-permute-done | bytes 196640 | tf_op jit(solution)/shard_map/ppermute | solution.py:16
  81.4 11.2 %shard_map.83 = f32[12,192,128]{2,1,0:T(8,128)} custom-call(s32[96]{0:T(128)} %reshape_squeeze.8.columns_ref, bf16[12,192,1536]{2,1,0:T(8,128)(2,1)} %bitcast.76, bf16[28,192,128]{2,1,0:T(8,128)(2,1)} %copy-done.4), custom_call_target="tpu_custom_call" | custom-call | flops 905969664 | bytes 9633792 | tf_op jit(solution)/shard_map/pallas_call | solution.py:59
  92.6 1.7 fusion.5
  95.0 1.3 broadcast_in_dim.29
  96.3 1.4 broadcast_in_dim.30
  97.7 10.9 %all-to-all-start = ((bf16[32,24,128]{2,1,0:T(8,128)(2,1)}), bf16[32,24,128]{2,1,0:T(8,128)(2,1)}, u32[]{:S(2)}, u32[]{:S(2)}) async-start(bf16[32,24,128]{2,1,0:T(8,128)(2,1)} %broadcast_in_dim.30), calls=%async_computation | async-start | bytes 393216 | tf_op jit(solution)/shard_map/all_to_all | solution.py:71
  108.6 2.8 %copy.13 = bf16[192,6144]{0,1:T(8,128)(2,1)} copy(bf16[192,6144]{1,0:T(8,128)(2,1)S(1)} %copy-done.5) | data formatting | bytes 4718592 | tf_op args[7]
  113.6 6.9 %all-to-all-done = bf16[32,24,128]{2,1,0:T(8,128)(2,1)} async-done(((bf16[32,24,128]{2,1,0:T(8,128)(2,1)}), bf16[32,24,128]{2,1,0:T(8,128)(2,1)}, u32[]{:S(2)}, u32[]{:S(2)}) %all-to-all-start) | async-done | bytes 196640 | tf_op jit(solution)/shard_map/all_to_all | solution.py:71
  120.5 1.5 fusion
  122.0 12.0 %all_to_all.15 = f32[8,24,128]{2,1,0:T(8,128)S(1)} all-to-all(f32[8,24,128]{2,1,0:T(8,128)S(1)} %fusion), channel_id=1, replica_groups=mesh['row'=32,'col'=8] {'col'}, dimensions={0} | all-to-all | bytes 196608 | tf_op jit(solution)/shard_map/all_to_all | solution.py:124
  134.3 1.3 constant_dynamic-update-slice_fusion.14
  137.7 1.4 gather_fusion.8
  141.5 1.7 collective-permute-start.9
  143.2 3.7 %collective-permute-start.8 = (bf16[4,192,128]{2,1,0:T(8,128)(2,1)S(1)}, bf16[4,192,128]{2,1,0:T(8,128)(2,1)S(1)}, u32[]{:S(2)}, u32[]{:S(2)}) collective-permute-start(bf16[4,192,128]{2,1,0:T(8,128)(2,1)S(1)} %broadcast_select_fusion.9), channel_id=1, source_target_pairs={{0,8},{8,16},{16,24},{24,32},{32,40},{40,48},{48,56},{56,64},{64,7... | collective-permute-start | bytes 589832 | tf_op jit(solution)/shard_map/ppermute | solution.py:16
  147.0 2.0 %collective-permute-start.10 = (bf16[4,192,128]{2,1,0:T(8,128)(2,1)S(1)}, bf16[4,192,128]{2,1,0:T(8,128)(2,1)S(1)}, u32[]{:S(2)}, u32[]{:S(2)}) collective-permute-start(bf16[4,192,128]{2,1,0:T(8,128)(2,1)S(1)} %broadcast_select_fusion.3), channel_id=1, source_target_pairs={{0,1},{1,2},{2,3},{3,4},{4,5},{5,6},{6,7},{7,0},{8,9},{9,10},{10,1... | collective-permute-start | bytes 589832 | tf_op jit(solution)/shard_map/ppermute | solution.py:16
  149.0 13.3 %collective-permute-done.8 = bf16[4,192,128]{2,1,0:T(8,128)(2,1)S(1)} collective-permute-done((bf16[4,192,128]{2,1,0:T(8,128)(2,1)S(1)}, bf16[4,192,128]{2,1,0:T(8,128)(2,1)S(1)}, u32[]{:S(2)}, u32[]{:S(2)}) %collective-permute-start.8) | collective-permute-done | bytes 196640 | tf_op jit(solution)/shard_map/ppermute | solution.py:16
  164.4 1.5 collective-permute-done.11
  166.6 11.3 %shard_map.84 = f32[12,192,128]{2,1,0:T(8,128)} custom-call(s32[96]{0:T(128)} %reshape_squeeze.8.columns_ref, bf16[12,192,1536]{2,1,0:T(8,128)(2,1)} %bitcast.77, bf16[28,192,128]{2,1,0:T(8,128)(2,1)} %constant_dynamic-update-slice_fusion.10.source_ref), custom_call_target="tpu_custom_call" | custom-call | flops 905969664 | bytes 9633792 | tf_op jit(solution)/shard_map/pallas_call | solution.py:59
  177.9 1.5 bitcast_subtract_fusion
  (158 shorter events, 27.9 us)
Async XLA Ops:
  0.8 4.7 %copy-start.34 = (pred[4]{0:T(512)(128)(4,1)}, pred[4]{0:T(512)(128)(4,1)S(1)}, u32[]{:S(2)}) copy-start(pred[4]{0:T(512)(128)(4,1)S(1)} %get-tuple-element.38) | copy-start | bytes 16
  0.9 13.2 %copy-start.32 = (pred[4]{0:T(512)(128)(4,1)}, pred[4]{0:T(512)(128)(4,1)S(1)}, u32[]{:S(2)}) copy-start(pred[4]{0:T(512)(128)(4,1)S(1)} %get-tuple-element.36) | copy-start | bytes 16
  0.9 18.7 %copy-start.29 = (pred[4]{0:T(512)(128)(4,1)}, pred[4]{0:T(512)(128)(4,1)S(1)}, u32[]{:S(2)}) copy-start(pred[4]{0:T(512)(128)(4,1)S(1)} %get-tuple-element.40) | copy-start | bytes 16
  0.9 21.0 %copy-start.36 = (pred[4]{0:T(512)(128)(4,1)}, pred[4]{0:T(512)(128)(4,1)S(1)}, u32[]{:S(2)}) copy-start(pred[4]{0:T(512)(128)(4,1)S(1)} %get-tuple-element.8) | copy-start | bytes 16
  0.9 4.1 %copy-start.38 = (s32[1024]{0:T(1024)}, s32[1024]{0:T(1024)S(1)}, u32[]{:S(2)}) copy-start(s32[1024]{0:T(1024)S(1)} %pad_clamp_fusion.3) | copy-start | bytes 12292
  1.7 3.0 %copy-start.7 = (f32[12,64]{1,0:T(8,128)}, f32[12,64]{1,0:T(8,128)S(1)}, u32[]{:S(2)}) copy-start(f32[12,64]{1,0:T(8,128)S(1)} %get-tuple-element.29) | copy-start | bytes 9220
  5.7 18.0 %collective-permute-start = (bf16[4,192,128]{2,1,0:T(8,128)(2,1)S(1)}, bf16[4,192,128]{2,1,0:T(8,128)(2,1)S(1)}, u32[]{:S(2)}, u32[]{:S(2)}) collective-permute-start(bf16[4,192,128]{2,1,0:T(8,128)(2,1)S(1)} %broadcast_select_fusion.11), channel_id=1, source_target_pairs={{0,8},{8,16},{16,24},{24,32},{32,40},{40,48},{48,56},{56,64},{64,7... | collective-permute-start | bytes 589832 | tf_op jit(solution)/shard_map/ppermute | solution.py:16
  13.5 8.5 %copy-start.39 = (s32[1024]{0:T(1024)}, s32[1024]{0:T(1024)S(1)}, u32[]{:S(2)}) copy-start(s32[1024]{0:T(1024)S(1)} %pad_clamp_fusion.2) | copy-start | bytes 12292
  13.5 8.7 %copy-start.42 = (s32[1,1,12,8]{2,3,1,0:T(8,128)S(1)}, s32[1,1,12,8]{2,3,1,0:T(8,128)}, u32[]{:S(2)}) copy-start(s32[1,1,12,8]{2,3,1,0:T(8,128)} %param.13) | copy-start | bytes 1156
  13.5 9.4 %copy-start.28 = (bf16[1,1,6,2304]{3,2,1,0:T(8,128)(2,1)S(1)}, bf16[1,1,6,2304]{3,2,1,0:T(8,128)(2,1)}, u32[]{:S(2)}) copy-start(bf16[1,1,6,2304]{3,2,1,0:T(8,128)(2,1)} %param.16) | copy-start | bytes 82948
  14.2 12.9 %collective-permute-start.1 = (bf16[4,192,128]{2,1,0:T(8,128)(2,1)S(1)}, bf16[4,192,128]{2,1,0:T(8,128)(2,1)S(1)}, u32[]{:S(2)}, u32[]{:S(2)}) collective-permute-start(bf16[4,192,128]{2,1,0:T(8,128)(2,1)S(1)} %broadcast_select_fusion.8), channel_id=1, source_target_pairs={{0,248},{8,0},{16,8},{24,16},{32,24},{40,32},{48,40},{56,48},{64,5... | collective-permute-start | bytes 589832 | tf_op jit(solution)/shard_map/ppermute | solution.py:16
  18.9 3.1 %copy-start.40 = (s32[1024]{0:T(1024)}, s32[1024]{0:T(1024)S(1)}, u32[]{:S(2)}) copy-start(s32[1024]{0:T(1024)S(1)} %pad_clamp_fusion.1) | copy-start | bytes 12292
  19.6 15.1 %collective-permute-start.2 = (bf16[4,192,128]{2,1,0:T(8,128)(2,1)S(1)}, bf16[4,192,128]{2,1,0:T(8,128)(2,1)S(1)}, u32[]{:S(2)}, u32[]{:S(2)}) collective-permute-start(bf16[4,192,128]{2,1,0:T(8,128)(2,1)S(1)} %broadcast_select_fusion.5), channel_id=1, source_target_pairs={{0,1},{1,2},{2,3},{3,4},{4,5},{5,6},{6,7},{7,0},{8,9},{9,10},{10,1... | collective-permute-start | bytes 589832 | tf_op jit(solution)/shard_map/ppermute | solution.py:16
  22.0 14.4 %collective-permute-start.3 = (bf16[4,192,128]{2,1,0:T(8,128)(2,1)S(1)}, bf16[4,192,128]{2,1,0:T(8,128)(2,1)S(1)}, u32[]{:S(2)}, u32[]{:S(2)}) collective-permute-start(bf16[4,192,128]{2,1,0:T(8,128)(2,1)S(1)} %broadcast_select_fusion.2), channel_id=1, source_target_pairs={{0,7},{1,0},{2,1},{3,2},{4,3},{5,4},{6,5},{7,6},{8,15},{9,8},{10,9... | collective-permute-start | bytes 589832 | tf_op jit(solution)/shard_map/ppermute | solution.py:16
  37.6 11.3 %copy-start.1 = (f32[1,1,12,192,128]{4,3,2,1,0:T(8,128)S(1)}, f32[1,1,12,192,128]{4,3,2,1,0:T(8,128)}, u32[]{:S(2)}) copy-start(f32[1,1,12,192,128]{4,3,2,1,0:T(8,128)} %param.10) | copy-start | bytes 3538948
  52.9 3.0 %copy-start.37 = (pred[4]{0:T(512)(128)(4,1)S(1)}, pred[4]{0:T(512)(128)(4,1)}, u32[]{:S(2)}) copy-start(pred[4]{0:T(512)(128)(4,1)} %copy-done.36) | copy-start | bytes 16
  52.9 3.1 %copy-start.30 = (pred[4]{0:T(512)(128)(4,1)S(1)}, pred[4]{0:T(512)(128)(4,1)}, u32[]{:S(2)}) copy-start(pred[4]{0:T(512)(128)(4,1)} %copy-done.29) | copy-start | bytes 16
  52.9 3.2 %copy-start.35 = (pred[4]{0:T(512)(128)(4,1)S(1)}, pred[4]{0:T(512)(128)(4,1)}, u32[]{:S(2)}) copy-start(pred[4]{0:T(512)(128)(4,1)} %copy-done.34) | copy-start | bytes 16
  56.2 16.6 %collective-permute-start.4 = (bf16[4,192,128]{2,1,0:T(8,128)(2,1)S(1)}, bf16[4,192,128]{2,1,0:T(8,128)(2,1)S(1)}, u32[]{:S(2)}, u32[]{:S(2)}) collective-permute-start(bf16[4,192,128]{2,1,0:T(8,128)(2,1)S(1)} %broadcast_select_fusion.10), channel_id=1, source_target_pairs={{0,8},{8,16},{16,24},{24,32},{32,40},{40,48},{48,56},{56,64},{64,7... | collective-permute-start | bytes 589832 | tf_op jit(solution)/shard_map/ppermute | solution.py:16
  56.4 23.4 %collective-permute-start.5 = (bf16[4,192,128]{2,1,0:T(8,128)(2,1)S(1)}, bf16[4,192,128]{2,1,0:T(8,128)(2,1)S(1)}, u32[]{:S(2)}, u32[]{:S(2)}) collective-permute-start(bf16[4,192,128]{2,1,0:T(8,128)(2,1)S(1)} %broadcast_select_fusion.7), channel_id=1, source_target_pairs={{0,248},{8,0},{16,8},{24,16},{32,24},{40,32},{48,40},{56,48},{64,5... | collective-permute-start | bytes 589832 | tf_op jit(solution)/shard_map/ppermute | solution.py:16
  66.1 14.1 %collective-permute-start.6 = (bf16[4,192,128]{2,1,0:T(8,128)(2,1)S(1)}, bf16[4,192,128]{2,1,0:T(8,128)(2,1)S(1)}, u32[]{:S(2)}, u32[]{:S(2)}) collective-permute-start(bf16[4,192,128]{2,1,0:T(8,128)(2,1)S(1)} %broadcast_select_fusion.4), channel_id=1, source_target_pairs={{0,1},{1,2},{2,3},{3,4},{4,5},{5,6},{6,7},{7,0},{8,9},{9,10},{10,1... | collective-permute-start | bytes 589832 | tf_op jit(solution)/shard_map/ppermute | solution.py:16
  67.5 12.7 %collective-permute-start.7 = (bf16[4,192,128]{2,1,0:T(8,128)(2,1)S(1)}, bf16[4,192,128]{2,1,0:T(8,128)(2,1)S(1)}, u32[]{:S(2)}, u32[]{:S(2)}) collective-permute-start(bf16[4,192,128]{2,1,0:T(8,128)(2,1)S(1)} %broadcast_select_fusion.1), channel_id=1, source_target_pairs={{0,7},{1,0},{2,1},{3,2},{4,3},{5,4},{6,5},{7,6},{8,15},{9,8},{10,9... | collective-permute-start | bytes 589832 | tf_op jit(solution)/shard_map/ppermute | solution.py:16
  92.6 16.0 %copy-start.5 = (bf16[192,6144]{1,0:T(8,128)(2,1)S(1)}, bf16[192,6144]{1,0:T(8,128)(2,1)}, u32[]{:S(2)}) copy-start(bf16[192,6144]{1,0:T(8,128)(2,1)} %param.17) | copy-start | bytes 7077892
  97.7 22.8 %all-to-all-start = ((bf16[32,24,128]{2,1,0:T(8,128)(2,1)}), bf16[32,24,128]{2,1,0:T(8,128)(2,1)}, u32[]{:S(2)}, u32[]{:S(2)}) async-start(bf16[32,24,128]{2,1,0:T(8,128)(2,1)} %broadcast_in_dim.30), calls=%async_computation | async-start | bytes 393216 | tf_op jit(solution)/shard_map/all_to_all | solution.py:71
  120.5 13.6 %copy-start.44 = (s32[1,1,12]{2,1,0:T(1,128)S(1)}, s32[1,1,12]{2,1,0:T(1,128)}, u32[]{:S(2)}) copy-start(s32[1,1,12]{2,1,0:T(1,128)} %param.15) | copy-start | bytes 148
  120.5 13.8 %copy-start.6 = (bf16[6,12,192]{2,1,0:T(8,128)(2,1)S(1)}, bf16[6,12,192]{2,1,0:T(8,128)(2,1)}, u32[]{:S(2)}) copy-start(bf16[6,12,192]{2,1,0:T(8,128)(2,1)} %reshape_squeeze.9) | copy-start | bytes 82948
  139.1 7.9 %copy-start.31 = (pred[4]{0:T(512)(128)(4,1)S(1)}, pred[4]{0:T(512)(128)(4,1)}, u32[]{:S(2)}) copy-start(pred[4]{0:T(512)(128)(4,1)} %copy-done.29) | copy-start | bytes 16
  141.5 21.5 %collective-permute-start.9 = (bf16[4,192,128]{2,1,0:T(8,128)(2,1)S(1)}, bf16[4,192,128]{2,1,0:T(8,128)(2,1)S(1)}, u32[]{:S(2)}, u32[]{:S(2)}) collective-permute-start(bf16[4,192,128]{2,1,0:T(8,128)(2,1)S(1)} %broadcast_select_fusion.6), channel_id=1, source_target_pairs={{0,248},{8,0},{16,8},{24,16},{32,24},{40,32},{48,40},{56,48},{64,5... | collective-permute-start | bytes 589832 | tf_op jit(solution)/shard_map/ppermute | solution.py:16
  143.2 19.1 %collective-permute-start.8 = (bf16[4,192,128]{2,1,0:T(8,128)(2,1)S(1)}, bf16[4,192,128]{2,1,0:T(8,128)(2,1)S(1)}, u32[]{:S(2)}, u32[]{:S(2)}) collective-permute-start(bf16[4,192,128]{2,1,0:T(8,128)(2,1)S(1)} %broadcast_select_fusion.9), channel_id=1, source_target_pairs={{0,8},{8,16},{16,24},{24,32},{32,40},{40,48},{48,56},{56,64},{64,7... | collective-permute-start | bytes 589832 | tf_op jit(solution)/shard_map/ppermute | solution.py:16
  147.0 16.7 %collective-permute-start.10 = (bf16[4,192,128]{2,1,0:T(8,128)(2,1)S(1)}, bf16[4,192,128]{2,1,0:T(8,128)(2,1)S(1)}, u32[]{:S(2)}, u32[]{:S(2)}) collective-permute-start(bf16[4,192,128]{2,1,0:T(8,128)(2,1)S(1)} %broadcast_select_fusion.3), channel_id=1, source_target_pairs={{0,1},{1,2},{2,3},{3,4},{4,5},{5,6},{6,7},{7,0},{8,9},{9,10},{10,1... | collective-permute-start | bytes 589832 | tf_op jit(solution)/shard_map/ppermute | solution.py:16
  149.0 16.9 %collective-permute-start.11 = (bf16[4,192,128]{2,1,0:T(8,128)(2,1)S(1)}, bf16[4,192,128]{2,1,0:T(8,128)(2,1)S(1)}, u32[]{:S(2)}, u32[]{:S(2)}) collective-permute-start(bf16[4,192,128]{2,1,0:T(8,128)(2,1)S(1)} %broadcast_select_fusion), channel_id=1, source_target_pairs={{0,7},{1,0},{2,1},{3,2},{4,3},{5,4},{6,5},{7,6},{8,15},{9,8},{10,9... | collective-permute-start | bytes 589832 | tf_op jit(solution)/shard_map/ppermute | solution.py:16
  166.6 11.3 %copy-start = (f32[12,192,128]{2,1,0:T(8,128)S(1)}, f32[12,192,128]{2,1,0:T(8,128)}, u32[]{:S(2)}) copy-start(f32[12,192,128]{2,1,0:T(8,128)} %shard_map.83) | copy-start | bytes 3538948
  (26 other events, 47.9 us)

commit v2 on v1

--- a/solution.py
+++ b/solution.py
@@ -32,32 +32,34 @@
     return damping * jnp.stack(outputs, axis=3).reshape(vector.shape)
 
 
-def product_kernel(stored, columns_ref, blocks_ref, source_ref, out_ref, picked):
+def product_kernel(stored, rows, columns_ref, blocks_ref, source_ref, out_ref, picked):
     n = pl.program_id(0)
     dof = source_ref.shape[1]
-    for k in range(stored):
-        picked[k * dof:(k + 1) * dof, :] = source_ref[columns_ref[n * stored + k]]
-    out_ref[0] = jnp.dot(blocks_ref[0], picked[...], preferred_element_type=jnp.float32)
+    for j in range(rows):
+        for k in range(stored):
+            picked[k * dof:(k + 1) * dof, :] = source_ref[columns_ref[(n * rows + j) * stored + k]]
+        out_ref[j] = jnp.dot(blocks_ref[j], picked[...], preferred_element_type=jnp.float32)
 
 
 def block_product(blocks, columns, source):
     block_count, dof, width = blocks.shape
     stored = width // dof
     vectors = source.shape[-1]
+    rows = 6 if block_count % 6 == 0 else 1
     grid_spec = pltpu.PrefetchScalarGridSpec(
         num_scalar_prefetch=1,
-        grid=(block_count,),
+        grid=(block_count // rows,),
         in_specs=[
-            pl.BlockSpec((1, dof, width), lambda n, c: (n, 0, 0)),
+            pl.BlockSpec((rows, dof, width), lambda n, c: (n, 0, 0)),
             pl.BlockSpec(source.shape, lambda n, c: (0, 0, 0)),
         ],
-        out_specs=pl.BlockSpec((1, dof, vectors), lambda n, c: (n, 0, 0)),
+        out_specs=pl.BlockSpec((rows, dof, vectors), lambda n, c: (n, 0, 0)),
         scratch_shapes=[pltpu.VMEM((width, vectors), source.dtype)],
     )
     flops = 2 * block_count * dof * width * vectors
     moved = blocks.size * 2 + source.size * 2 + block_count * dof * vectors * 4
     return pl.pallas_call(
-        functools.partial(product_kernel, stored),
+        functools.partial(product_kernel, stored, rows),
         grid_spec=grid_spec,
         out_shape=jax.ShapeDtypeStruct((block_count, dof, vectors), jnp.float32),
         cost_estimate=pl.CostEstimate(flops=flops, bytes_accessed=moved, transcendentals=0),
@@ -71,34 +73,25 @@
     return lax.all_to_all(repeated, axis, 0, 0, tiled=True)
 
 
+def exchange(parts):
+    return [
+        passed_along(parts[0], "row", 1),
+        passed_along(parts[1], "row", -1),
+        passed_along(parts[2], "col", 1),
+        passed_along(parts[3], "col", -1),
+    ]
+
+
 def body(rhs, smoother, blocks, col_index, send_list, agg_id, prolong, coarse_inverse):
     block_count = rhs.shape[2]
     dof_count = rhs.shape[3]
     vectors = rhs.shape[4]
     send_rows = send_list[0, 0]
+    groups, ghost_count = send_rows.shape
     coarse_dofs = prolong.shape[2]
     shaped = prolong[0, 0].reshape((coarse_dofs, block_count, dof_count))
     local_blocks = blocks[0, 0]
     columns = col_index[0, 0]
-
-    def apply_operator(vector):
-        vector_low = vector.astype(jnp.bfloat16)
-        shard_low = vector_low[0, 0]
-        ghosts = []
-        for offset in (1, -1):
-            packed = jnp.take(shard_low, send_rows[0 if offset == 1 else 1], axis=0)
-            ghosts.append(passed_along(packed, "row", offset))
-        for offset in (1, -1):
-            packed = jnp.take(shard_low, send_rows[2 if offset == 1 else 3], axis=0)
-            ghosts.append(passed_along(packed, "col", offset))
-        source = jnp.concatenate([shard_low] + list(ghosts), axis=0)
-        return block_product(local_blocks, columns, source)[None, None]
-
-    first_iter = point_smooth(smoother, rhs)
-    residual_first = rhs - apply_operator(first_iter)
-    update_second = point_smooth(smoother, residual_first)
-    second_iter = first_iter + update_second
-    residual_second = residual_first - apply_operator(update_second)
     row_count = lax.axis_size("row")
     col_count = lax.axis_size("col")
     coarse_rows = coarse_inverse.shape[1] // (row_count * col_count)
@@ -106,6 +99,41 @@
     onehot = (agg_id[0, 0][None, :] == jnp.arange(aggregates, dtype=jnp.int32)[:, None]).astype(
         jnp.float32
     )
+
+    def outgoing(vector):
+        shard_low = vector.astype(jnp.bfloat16)[0, 0]
+        packed = jnp.take(shard_low, send_rows.reshape(-1), axis=0)
+        parts = [packed[g * ghost_count:(g + 1) * ghost_count] for g in range(groups)]
+        return shard_low, parts
+
+    def product(shard_low, ghosts):
+        source = jnp.concatenate([shard_low] + list(ghosts), axis=0)
+        return block_product(local_blocks, columns, source)[None, None]
+
+    tables = []
+    for g in range(groups):
+        picked = jnp.take(shaped, send_rows[g], axis=1)
+        member = jnp.take(onehot, send_rows[g], axis=1).astype(jnp.bfloat16)
+        table = member.T[:, :, None, None] * jnp.transpose(picked, (1, 0, 2))[:, None, :, :]
+        tables.append(table.reshape((ghost_count * coarse_rows * dof_count) // vectors, vectors))
+    ghost_rows = ghost_count * dof_count
+
+    first_iter = point_smooth(smoother, rhs)
+    shard_low, parts = outgoing(first_iter)
+    payloads = [
+        jnp.concatenate([parts[g].reshape(ghost_rows, vectors), tables[g]], axis=0)
+        for g in range(groups)
+    ]
+    arrived = exchange(payloads)
+    ghosts = [a[:ghost_rows].reshape((ghost_count, dof_count, vectors)) for a in arrived]
+    neighbour_tables = [
+        a[ghost_rows:].reshape((ghost_count, coarse_rows, dof_count)) for a in arrived
+    ]
+    residual_first = rhs - product(shard_low, ghosts)
+    update_second = point_smooth(smoother, residual_first)
+    second_iter = first_iter + update_second
+    shard_low, parts = outgoing(update_second)
+    residual_second = residual_first - product(shard_low, exchange(parts))
     local_terms = jnp.einsum(
         "knd,ndr->nkr",
         shaped,
@@ -123,9 +151,9 @@
     partial = jnp.dot(held, column_part, preferred_element_type=jnp.float32)
     partial = lax.all_to_all(partial, "col", 0, 0, tiled=True)
     coarse_solution = partial.reshape((col_count, coarse_rows, vectors)).sum(axis=0)
-    coarse_rounded = coarse_solution.astype(jnp.bfloat16).reshape(
-        (aggregates, coarse_dofs, vectors)
-    )
+    coarse_flat = coarse_solution.astype(jnp.bfloat16)
+    coarse_rounded = coarse_flat.reshape((aggregates, coarse_dofs, vectors))
+    neighbour_coarse = exchange([coarse_flat] * groups)
     chosen = jnp.einsum(
         "an,akr->nkr",
         onehot.astype(jnp.bfloat16),
@@ -136,7 +164,15 @@
         None, None
     ]
     after_coarse = second_iter + correction
-    residual_third = residual_second - apply_operator(correction)
+    ghost_corrections = [
+        jnp.einsum(
+            "bjd,jr->bdr", neighbour_tables[g], neighbour_coarse[g],
+            preferred_element_type=jnp.float32,
+        ).astype(jnp.bfloat16)
+        for g in range(groups)
+    ]
+    correction_low = correction.astype(jnp.bfloat16)[0, 0]
+    residual_third = residual_second - product(correction_low, ghost_corrections)
     return after_coarse + point_smooth(smoother, residual_third)
 
 

time: 186 us -> 164 us (0.88); the launches traced: 183 us -> 163 us
  Pallas kernels: 33.8 us -> 18.7 us
  blocking collectives: 12 us -> 0 us
  waiting for transfers between devices: 47 us -> 40.4 us
  starting transfers between devices: 43.8 us -> 48.3 us
  matrix products: 4.79 us -> 9.21 us
  local copies, waits for them, and re-layouts: 25.8 us -> 29.2 us
    pallas_call x3, Pallas kernels: 33.8 us -> 18.7 us  [block_product(): pl.pallas_call(functools.partial(product_kernel, stored, rows), grid_spec...]
    all_to_all x1 -> x0, blocking collectives: 12 us -> none  [body(): partial = lax.all_to_all(partial, 'col', 0, 0, tiled=True)]
    ppermute x12, waiting for transfers between devices: 40 us -> 31.7 us  [passed_along(): return lax.ppermute(value, axis, pairs)]
    all_to_all x0 -> x1, starting transfers between devices: none -> 7.88 us  [body(): partial = lax.all_to_all(partial, 'col', 0, 0, tiled=True)]
    slice x0 -> x10, local copies, waits for them, and re-layouts: none -> 6.96 us  [the longest x4 3.76 us: body(): a[:ghost_rows].reshape((ghost_count, dof_count, vectors))]
    dot_general x0 -> x4, matrix products: none -> 3.69 us  [body(): jnp.einsum('bjd,jr->bdr', neighbour_tables[g], neighbour_coarse[g], prefe...]
    all_to_all x1, starting transfers between devices: 10.9 us -> 7.61 us  [gathered_copies(): return lax.all_to_all(repeated, axis, 0, 0, tiled=True)]
    concatenate x0 -> x4, other arithmetic: none -> 2.83 us  [body(): jnp.concatenate([parts[g].reshape(ghost_rows, vectors), tables[g]], axis=0)]
  transfers between devices with their start and end apart: 13 -> 14, of which waited for: 9 -> 8; matrix products, arithmetic and copies ran while one was open for 6% -> 14% of each run, Pallas kernels for 0% -> 0%
where the time goes in v2:
time: 164 us; the launch traced here: 163 us
  starting transfers between devices  48.3 us (29%)
  waiting for transfers between devices  40.4 us (25%)
  local copies, waits for them, and re-layouts  29.2 us (18%)
  Pallas kernels  18.7 us (11%)
  other arithmetic  16.7 us (10%)
  matrix products  9.21 us (6%)
    ppermute x12, starting transfers between devices, passed_along(): return lax.ppermute(value, axis, pairs)  32.8 us
    ppermute x12, waiting for transfers between devices, passed_along(): return lax.ppermute(value, axis, pairs)  31.7 us
    pallas_call x3, Pallas kernels, block_product(): pl.pallas_call(functools.partial(product_kernel, stored, rows), grid_spec...  18.7 us
    all_to_all x1, starting transfers between devices, body(): partial = lax.all_to_all(partial, 'col', 0, 0, tiled=True)  7.88 us
    all_to_all x1, starting transfers between devices, gathered_copies(): return lax.all_to_all(repeated, axis, 0, 0, tiled=True)  7.61 us
    all_to_all x1, waiting for transfers between devices, gathered_copies(): return lax.all_to_all(repeated, axis, 0, 0, tiled=True)  6.84 us
    unnamed x80, local copies, waits for them, and re-layouts  6.58 us
    add x3, other arithmetic, point_smooth(): summed + factors[:, :, component, 2, :, :, None] * pieces[:, :, :, 2]  5.3 us
  transfers between devices with their start and end apart: 14, of which 8 were waited for; matrix products, arithmetic and copies ran while one was open for 14% of the time, Pallas kernels for 0%

profile of v2, /device:TPU:1, one launch (start us, length us, event | category | flops | bytes accessed | tf_op | source)
XLA Modules:
  0.0 163.3 jit_solution(1531984214597813536)
XLA Ops:
  5.7 2.9 %multiply_add_fusion.8 = (f32[1,1,12,1,64,128]{5,4,3,2,1,0:T(8,128)S(1)}, f32[1,1,12,1,64,128]{5,4,3,2,1,0:T(8,128)S(1)}, f32[1,1,12,1,64,128]{5,4,3,2,1,0:T(8,128)S(1)}) fusion(f32[1,1,12,3,64,128]{5,4,3,2,1,0:T(8,128)} %bitcast.142, f32[12,64]{1,0:T(8,128)S(1)} %get-tuple-element.42, f32[12,64]{1,0:T(8,128)S(1)} %get-tuple-element.43, ...), kind=kLoop, calls=%fused_computation.47 | loop fusion | flops 1474560 | bytes 2386944 | tf_op jit(solution)/shard_map/add | solution.py:30
  10.5 7.7 %collective-permute-start = (bf16[912,128]{1,0:T(8,128)(2,1)}, bf16[912,128]{1,0:T(8,128)(2,1)}, u32[]{:S(2)}, u32[]{:S(2)}) collective-permute-start(bf16[912,128]{1,0:T(8,128)(2,1)} %pad_maximum_fusion), channel_id=1, source_target_pairs={{0,8},{8,16},{16,24},{24,32},{32,40},{40,48},{48,56},{56,64},{64,7... | collective-permute-start | bytes 700424 | tf_op jit(solution)/shard_map/ppermute | solution.py:16
  20.4 4.6 %collective-permute-start.1 = (bf16[912,128]{1,0:T(8,128)(2,1)}, bf16[912,128]{1,0:T(8,128)(2,1)}, u32[]{:S(2)}, u32[]{:S(2)}) collective-permute-start(bf16[912,128]{1,0:T(8,128)(2,1)} %pad_maximum_fusion.1), channel_id=1, source_target_pairs={{0,248},{8,0},{16,8},{24,16},{32,24},{40,32},{48,40},{56,48},{64,5... | collective-permute-start | bytes 700424 | tf_op jit(solution)/shard_map/ppermute | solution.py:16
  27.3 1.6 collective-permute-start.2
  32.8 5.3 %collective-permute-done.1 = bf16[912,128]{1,0:T(8,128)(2,1)} collective-permute-done((bf16[912,128]{1,0:T(8,128)(2,1)}, bf16[912,128]{1,0:T(8,128)(2,1)}, u32[]{:S(2)}, u32[]{:S(2)}) %collective-permute-start.1) | collective-permute-done | bytes 233504 | tf_op jit(solution)/shard_map/ppermute | solution.py:16
  39.1 4.8 %collective-permute-done.2 = bf16[912,128]{1,0:T(8,128)(2,1)} collective-permute-done((bf16[912,128]{1,0:T(8,128)(2,1)}, bf16[912,128]{1,0:T(8,128)(2,1)}, u32[]{:S(2)}, u32[]{:S(2)}) %collective-permute-start.2) | collective-permute-done | bytes 233504 | tf_op jit(solution)/shard_map/ppermute | solution.py:16
  47.7 6.3 %shard_map.82 = f32[12,192,128]{2,1,0:T(8,128)} custom-call(s32[96]{0:T(128)} %reshape_squeeze.12.columns_ref, bf16[12,192,1536]{2,1,0:T(8,128)(2,1)} %bitcast.134, bf16[28,192,128]{2,1,0:T(8,128)(2,1)} %copy-done.3), custom_call_target="tpu_custom_call" | custom-call | flops 905969664 | bytes 9633792 | tf_op jit(solution)/shard_map/pallas_call | solution.py:61
  54.0 1.4 bitcast_subtract_fusion.2
  56.7 1.3 fusion.7
  59.7 3.9 %collective-permute-start.7 = (bf16[4,192,128]{2,1,0:T(8,128)(2,1)S(1)}, bf16[4,192,128]{2,1,0:T(8,128)(2,1)S(1)}, u32[]{:S(2)}, u32[]{:S(2)}) collective-permute-start(bf16[4,192,128]{2,1,0:T(8,128)(2,1)S(1)} %get-tuple-element.27), channel_id=1, source_target_pairs={{0,7},{1,0},{2,1},{3,2},{4,3},{5,4},{6,5},{7,6},{8,15},{9,8},{10,9... | collective-permute-start | bytes 589832 | tf_op jit(solution)/shard_map/ppermute | solution.py:16
  63.6 7.4 %collective-permute-start.5 = (bf16[4,192,128]{2,1,0:T(8,128)(2,1)S(1)}, bf16[4,192,128]{2,1,0:T(8,128)(2,1)S(1)}, u32[]{:S(2)}, u32[]{:S(2)}) collective-permute-start(bf16[4,192,128]{2,1,0:T(8,128)(2,1)S(1)} %get-tuple-element.29), channel_id=1, source_target_pairs={{0,248},{8,0},{16,8},{24,16},{32,24},{40,32},{48,40},{56,48},{64,5... | collective-permute-start | bytes 589832 | tf_op jit(solution)/shard_map/ppermute | solution.py:16
  71.0 5.7 %collective-permute-done.4 = bf16[4,192,128]{2,1,0:T(8,128)(2,1)S(1)} collective-permute-done((bf16[4,192,128]{2,1,0:T(8,128)(2,1)S(1)}, bf16[4,192,128]{2,1,0:T(8,128)(2,1)S(1)}, u32[]{:S(2)}, u32[]{:S(2)}) %collective-permute-start.4) | collective-permute-done | bytes 196640 | tf_op jit(solution)/shard_map/ppermute | solution.py:16
  76.7 9.5 %collective-permute-done.5 = bf16[4,192,128]{2,1,0:T(8,128)(2,1)S(1)} collective-permute-done((bf16[4,192,128]{2,1,0:T(8,128)(2,1)S(1)}, bf16[4,192,128]{2,1,0:T(8,128)(2,1)S(1)}, u32[]{:S(2)}, u32[]{:S(2)}) %collective-permute-start.5) | collective-permute-done | bytes 196640 | tf_op jit(solution)/shard_map/ppermute | solution.py:16
  87.5 6.1 %shard_map.83 = f32[12,192,128]{2,1,0:T(8,128)} custom-call(s32[96]{0:T(128)} %reshape_squeeze.12.columns_ref, bf16[12,192,1536]{2,1,0:T(8,128)(2,1)} %bitcast.135, bf16[28,192,128]{2,1,0:T(8,128)(2,1)} %copy-done.4), custom_call_target="tpu_custom_call" | custom-call | flops 905969664 | bytes 9633792 | tf_op jit(solution)/shard_map/pallas_call | solution.py:61
  93.6 1.7 %convolution_bitcast_fusion.1 = f32[12,6,128]{2,1,0:T(8,128)S(1)} fusion(f32[1,1,12,192,128]{4,3,2,1,0:T(8,128)S(1)} %bitcast_subtract_fusion.2, f32[12,192,128]{2,1,0:T(8,128)} %shard_map.83, bf16[6,12,192]{2,1,0:T(8,128)(2,1)} %copy-done.6), kind=kOutput, calls=%fused_computation.28 | convolution fusion | flops 4128768 | bytes 2423808 | tf_op jit(solution)/shard_map/knd,ndr->nkr/dot_general | solution.py:137
  96.2 1.3 broadcast_in_dim.52
  97.5 1.4 broadcast_in_dim.53
  98.9 7.6 %all-to-all-start = ((bf16[32,24,128]{2,1,0:T(8,128)(2,1)}), bf16[32,24,128]{2,1,0:T(8,128)(2,1)}, u32[]{:S(2)}, u32[]{:S(2)}) async-start(bf16[32,24,128]{2,1,0:T(8,128)(2,1)} %broadcast_in_dim.53), calls=%async_computation | async-start | bytes 393216 | tf_op jit(solution)/shard_map/all_to_all | solution.py:73
  106.5 2.8 %copy.27 = bf16[192,6144]{0,1:T(8,128)(2,1)} copy(bf16[192,6144]{1,0:T(8,128)(2,1)S(1)} %copy-done.5) | data formatting | bytes 4718592 | tf_op args[7]
  111.5 6.8 %all-to-all-done = bf16[32,24,128]{2,1,0:T(8,128)(2,1)} async-done(((bf16[32,24,128]{2,1,0:T(8,128)(2,1)}), bf16[32,24,128]{2,1,0:T(8,128)(2,1)}, u32[]{:S(2)}, u32[]{:S(2)}) %all-to-all-start) | async-done | bytes 196640 | tf_op jit(solution)/shard_map/all_to_all | solution.py:73
  118.3 2.2 %fusion = f32[8,24,128]{2,1,0:T(8,128)} fusion(bf16[768,128,1]{1,0,2:T(8,128)(2,1)} %bitcast.52, bf16[8,24,768]{1,0,2:T(8,128)(2,1)S(1)} %reshape.412), kind=kOutput, calls=%fused_computation.10 | convolution fusion | flops 37748736 | bytes 589824 | tf_op jit(solution)/shard_map/dot_general | solution.py:151
  120.5 7.9 %all-to-all-start.1 = ((f32[8,24,128]{2,1,0:T(8,128)}), f32[8,24,128]{2,1,0:T(8,128)S(1)}, u32[]{:S(2)}, u32[]{:S(2)}) async-start(f32[8,24,128]{2,1,0:T(8,128)} %fusion), calls=%async_computation.1 | async-start | bytes 196608 | tf_op jit(solution)/shard_map/all_to_all | solution.py:152
  131.8 1.9 %all-to-all-done.1 = f32[8,24,128]{2,1,0:T(8,128)S(1)} async-done(((f32[8,24,128]{2,1,0:T(8,128)}), f32[8,24,128]{2,1,0:T(8,128)S(1)}, u32[]{:S(2)}, u32[]{:S(2)}) %all-to-all-start.1) | async-done | bytes 98336 | tf_op jit(solution)/shard_map/all_to_all | solution.py:152
  133.7 1.5 collective-permute-start.10
  135.2 2.2 %collective-permute-start.9 = (bf16[24,128]{1,0:T(8,128)(2,1)S(1)}, bf16[24,128]{1,0:T(8,128)(2,1)S(1)}, u32[]{:S(2)}, u32[]{:S(2)}) collective-permute-start(bf16[24,128]{1,0:T(8,128)(2,1)S(1)} %reduce_sum.9), channel_id=1, source_target_pairs={{0,248},{8,0},{16,8},{24,16},{32,24},{40,32},{48,40},{56,48},{64,5... | collective-permute-start | bytes 18440 | tf_op jit(solution)/shard_map/ppermute | solution.py:16
  137.3 3.2 %collective-permute-start.8 = (bf16[24,128]{1,0:T(8,128)(2,1)S(1)}, bf16[24,128]{1,0:T(8,128)(2,1)S(1)}, u32[]{:S(2)}, u32[]{:S(2)}) collective-permute-start(bf16[24,128]{1,0:T(8,128)(2,1)S(1)} %reduce_sum.9), channel_id=1, source_target_pairs={{0,8},{8,16},{16,24},{24,32},{32,40},{40,48},{48,56},{56,64},{64,7... | collective-permute-start | bytes 18440 | tf_op jit(solution)/shard_map/ppermute | solution.py:16
  141.0 1.2 convert_dynamic-update-slice_fusion
  142.2 5.7 %collective-permute-done.8 = bf16[24,128]{1,0:T(8,128)(2,1)S(1)} collective-permute-done((bf16[24,128]{1,0:T(8,128)(2,1)S(1)}, bf16[24,128]{1,0:T(8,128)(2,1)S(1)}, u32[]{:S(2)}, u32[]{:S(2)}) %collective-permute-start.8) | collective-permute-done | bytes 6176 | tf_op jit(solution)/shard_map/ppermute | solution.py:16
  151.7 6.3 %shard_map.84 = f32[12,192,128]{2,1,0:T(8,128)} custom-call(s32[96]{0:T(128)} %reshape_squeeze.12.columns_ref, bf16[12,192,1536]{2,1,0:T(8,128)(2,1)} %bitcast.136, bf16[28,192,128]{2,1,0:T(8,128)(2,1)} %fusion.2.source_ref), custom_call_target="tpu_custom_call" | custom-call | flops 905969664 | bytes 9633792 | tf_op jit(solution)/shard_map/pallas_call | solution.py:61
  158.0 1.5 bitcast_subtract_fusion
  159.5 1.2 multiply_add_fusion.2
  162.0 1.2 add_bitcast_fusion
  (165 shorter events, 36.4 us)
Async XLA Ops:
  0.8 8.8 %copy-start.31 = (pred[16]{0:T(512)(128)(4,1)}, pred[16]{0:T(512)(128)(4,1)S(1)}, u32[]{:S(2)}) copy-start(pred[16]{0:T(512)(128)(4,1)S(1)} %compare_and_fusion.4) | copy-start | bytes 52
  1.6 7.2 %copy-start.29 = (s32[1024]{0:T(1024)}, s32[1024]{0:T(1024)S(1)}, u32[]{:S(2)}) copy-start(s32[1024]{0:T(1024)S(1)} %pad_clamp_fusion.4) | copy-start | bytes 12292
  3.3 5.3 %copy-start.6 = (bf16[6,12,192]{2,1,0:T(8,128)(2,1)}, bf16[6,12,192]{2,1,0:T(8,128)(2,1)S(1)}, u32[]{:S(2)}) copy-start(bf16[6,12,192]{2,1,0:T(8,128)(2,1)S(1)} %reshape_squeeze.14) | copy-start | bytes 82948
  5.6 3.0 %copy-start.8 = (f32[12,64]{1,0:T(8,128)}, f32[12,64]{1,0:T(8,128)S(1)}, u32[]{:S(2)}) copy-start(f32[12,64]{1,0:T(8,128)S(1)} %get-tuple-element.37) | copy-start | bytes 9220
  5.6 3.0 %copy-start.11 = (f32[12,64]{1,0:T(8,128)}, f32[12,64]{1,0:T(8,128)S(1)}, u32[]{:S(2)}) copy-start(f32[12,64]{1,0:T(8,128)S(1)} %get-tuple-element.38) | copy-start | bytes 9220
  5.6 3.0 %copy-start.14 = (f32[12,64]{1,0:T(8,128)}, f32[12,64]{1,0:T(8,128)S(1)}, u32[]{:S(2)}) copy-start(f32[12,64]{1,0:T(8,128)S(1)} %get-tuple-element.39) | copy-start | bytes 9220
  5.7 3.0 %copy-start.17 = (f32[12,64]{1,0:T(8,128)}, f32[12,64]{1,0:T(8,128)S(1)}, u32[]{:S(2)}) copy-start(f32[12,64]{1,0:T(8,128)S(1)} %get-tuple-element.40) | copy-start | bytes 9220
  5.7 3.0 %copy-start.20 = (f32[12,64]{1,0:T(8,128)}, f32[12,64]{1,0:T(8,128)S(1)}, u32[]{:S(2)}) copy-start(f32[12,64]{1,0:T(8,128)S(1)} %get-tuple-element.41) | copy-start | bytes 9220
  5.7 3.0 %copy-start.23 = (f32[12,64]{1,0:T(8,128)}, f32[12,64]{1,0:T(8,128)S(1)}, u32[]{:S(2)}) copy-start(f32[12,64]{1,0:T(8,128)S(1)} %get-tuple-element.42) | copy-start | bytes 9220
  5.7 3.0 %copy-start.26 = (f32[12,64]{1,0:T(8,128)}, f32[12,64]{1,0:T(8,128)S(1)}, u32[]{:S(2)}) copy-start(f32[12,64]{1,0:T(8,128)S(1)} %get-tuple-element.43) | copy-start | bytes 9220
  10.5 20.6 %copy-start.30 = (s32[1,1,12,8]{2,3,1,0:T(8,128)S(1)}, s32[1,1,12,8]{2,3,1,0:T(8,128)}, u32[]{:S(2)}) copy-start(s32[1,1,12,8]{2,3,1,0:T(8,128)} %param.17) | copy-start | bytes 1156
  10.5 21.3 %collective-permute-start = (bf16[912,128]{1,0:T(8,128)(2,1)}, bf16[912,128]{1,0:T(8,128)(2,1)}, u32[]{:S(2)}, u32[]{:S(2)}) collective-permute-start(bf16[912,128]{1,0:T(8,128)(2,1)} %pad_maximum_fusion), channel_id=1, source_target_pairs={{0,8},{8,16},{16,24},{24,32},{32,40},{40,48},{48,56},{56,64},{64,7... | collective-permute-start | bytes 700424 | tf_op jit(solution)/shard_map/ppermute | solution.py:16
  20.4 17.7 %collective-permute-start.1 = (bf16[912,128]{1,0:T(8,128)(2,1)}, bf16[912,128]{1,0:T(8,128)(2,1)}, u32[]{:S(2)}, u32[]{:S(2)}) collective-permute-start(bf16[912,128]{1,0:T(8,128)(2,1)} %pad_maximum_fusion.1), channel_id=1, source_target_pairs={{0,248},{8,0},{16,8},{24,16},{32,24},{40,32},{48,40},{56,48},{64,5... | collective-permute-start | bytes 700424 | tf_op jit(solution)/shard_map/ppermute | solution.py:16
  27.3 16.6 %collective-permute-start.2 = (bf16[912,128]{1,0:T(8,128)(2,1)}, bf16[912,128]{1,0:T(8,128)(2,1)}, u32[]{:S(2)}, u32[]{:S(2)}) collective-permute-start(bf16[912,128]{1,0:T(8,128)(2,1)} %pad_maximum_fusion.2), channel_id=1, source_target_pairs={{0,1},{1,2},{2,3},{3,4},{4,5},{5,6},{6,7},{7,0},{8,9},{9,10},{10,1... | collective-permute-start | bytes 700424 | tf_op jit(solution)/shard_map/ppermute | solution.py:16
  31.0 14.5 %collective-permute-start.3 = (bf16[912,128]{1,0:T(8,128)(2,1)}, bf16[912,128]{1,0:T(8,128)(2,1)}, u32[]{:S(2)}, u32[]{:S(2)}) collective-permute-start(bf16[912,128]{1,0:T(8,128)(2,1)} %pad_maximum_fusion.3), channel_id=1, source_target_pairs={{0,7},{1,0},{2,1},{3,2},{4,3},{5,4},{6,5},{7,6},{8,15},{9,8},{10,9... | collective-permute-start | bytes 700424 | tf_op jit(solution)/shard_map/ppermute | solution.py:16
  47.7 6.3 %copy-start.1 = (f32[1,1,12,192,128]{4,3,2,1,0:T(8,128)S(1)}, f32[1,1,12,192,128]{4,3,2,1,0:T(8,128)}, u32[]{:S(2)}) copy-start(f32[1,1,12,192,128]{4,3,2,1,0:T(8,128)} %param.14) | copy-start | bytes 3538948
  59.2 17.5 %collective-permute-start.4 = (bf16[4,192,128]{2,1,0:T(8,128)(2,1)S(1)}, bf16[4,192,128]{2,1,0:T(8,128)(2,1)S(1)}, u32[]{:S(2)}, u32[]{:S(2)}) collective-permute-start(bf16[4,192,128]{2,1,0:T(8,128)(2,1)S(1)} %get-tuple-element.30), channel_id=1, source_target_pairs={{0,8},{8,16},{16,24},{24,32},{32,40},{40,48},{48,56},{56,64},{64,7... | collective-permute-start | bytes 589832 | tf_op jit(solution)/shard_map/ppermute | solution.py:16
  59.7 26.6 %collective-permute-start.7 = (bf16[4,192,128]{2,1,0:T(8,128)(2,1)S(1)}, bf16[4,192,128]{2,1,0:T(8,128)(2,1)S(1)}, u32[]{:S(2)}, u32[]{:S(2)}) collective-permute-start(bf16[4,192,128]{2,1,0:T(8,128)(2,1)S(1)} %get-tuple-element.27), channel_id=1, source_target_pairs={{0,7},{1,0},{2,1},{3,2},{4,3},{5,4},{6,5},{7,6},{8,15},{9,8},{10,9... | collective-permute-start | bytes 589832 | tf_op jit(solution)/shard_map/ppermute | solution.py:16
  63.6 22.7 %collective-permute-start.6 = (bf16[4,192,128]{2,1,0:T(8,128)(2,1)S(1)}, bf16[4,192,128]{2,1,0:T(8,128)(2,1)S(1)}, u32[]{:S(2)}, u32[]{:S(2)}) collective-permute-start(bf16[4,192,128]{2,1,0:T(8,128)(2,1)S(1)} %get-tuple-element.28), channel_id=1, source_target_pairs={{0,1},{1,2},{2,3},{3,4},{4,5},{5,6},{6,7},{7,0},{8,9},{9,10},{10,1... | collective-permute-start | bytes 589832 | tf_op jit(solution)/shard_map/ppermute | solution.py:16
  63.6 22.7 %collective-permute-start.5 = (bf16[4,192,128]{2,1,0:T(8,128)(2,1)S(1)}, bf16[4,192,128]{2,1,0:T(8,128)(2,1)S(1)}, u32[]{:S(2)}, u32[]{:S(2)}) collective-permute-start(bf16[4,192,128]{2,1,0:T(8,128)(2,1)S(1)} %get-tuple-element.29), channel_id=1, source_target_pairs={{0,248},{8,0},{16,8},{24,16},{32,24},{40,32},{48,40},{56,48},{64,5... | collective-permute-start | bytes 589832 | tf_op jit(solution)/shard_map/ppermute | solution.py:16
  93.6 1.7 %copy-start.33 = (s32[1,1,12]{2,1,0:T(1,128)S(1)}, s32[1,1,12]{2,1,0:T(1,128)}, u32[]{:S(2)}) copy-start(s32[1,1,12]{2,1,0:T(1,128)} %param.19) | copy-start | bytes 148
  93.6 12.9 %copy-start.5 = (bf16[192,6144]{1,0:T(8,128)(2,1)S(1)}, bf16[192,6144]{1,0:T(8,128)(2,1)}, u32[]{:S(2)}) copy-start(bf16[192,6144]{1,0:T(8,128)(2,1)} %param.21) | copy-start | bytes 7077892
  98.9 19.4 %all-to-all-start = ((bf16[32,24,128]{2,1,0:T(8,128)(2,1)}), bf16[32,24,128]{2,1,0:T(8,128)(2,1)}, u32[]{:S(2)}, u32[]{:S(2)}) async-start(bf16[32,24,128]{2,1,0:T(8,128)(2,1)} %broadcast_in_dim.53), calls=%async_computation | async-start | bytes 393216 | tf_op jit(solution)/shard_map/all_to_all | solution.py:73
  118.3 22.5 %copy-start.34 = (s32[1,1,12]{2,1,0:T(1,128)S(1)}, s32[1,1,12]{2,1,0:T(1,128)}, u32[]{:S(2)}) copy-start(s32[1,1,12]{2,1,0:T(1,128)} %param.19) | copy-start | bytes 148
  118.3 22.7 %copy-start.7 = (bf16[6,12,192]{2,1,0:T(8,128)(2,1)S(1)}, bf16[6,12,192]{2,1,0:T(8,128)(2,1)}, u32[]{:S(2)}) copy-start(bf16[6,12,192]{2,1,0:T(8,128)(2,1)} %copy-done.6) | copy-start | bytes 82948
  120.5 13.2 %all-to-all-start.1 = ((f32[8,24,128]{2,1,0:T(8,128)}), f32[8,24,128]{2,1,0:T(8,128)S(1)}, u32[]{:S(2)}, u32[]{:S(2)}) async-start(f32[8,24,128]{2,1,0:T(8,128)} %fusion), calls=%async_computation.1 | async-start | bytes 196608 | tf_op jit(solution)/shard_map/all_to_all | solution.py:152
  133.7 16.1 %collective-permute-start.10 = (bf16[24,128]{1,0:T(8,128)(2,1)S(1)}, bf16[24,128]{1,0:T(8,128)(2,1)S(1)}, u32[]{:S(2)}, u32[]{:S(2)}) collective-permute-start(bf16[24,128]{1,0:T(8,128)(2,1)S(1)} %reduce_sum.9), channel_id=1, source_target_pairs={{0,1},{1,2},{2,3},{3,4},{4,5},{5,6},{6,7},{7,0},{8,9},{9,10},{10,1... | collective-permute-start | bytes 18440 | tf_op jit(solution)/shard_map/ppermute | solution.py:16
  135.2 13.7 %collective-permute-start.9 = (bf16[24,128]{1,0:T(8,128)(2,1)S(1)}, bf16[24,128]{1,0:T(8,128)(2,1)S(1)}, u32[]{:S(2)}, u32[]{:S(2)}) collective-permute-start(bf16[24,128]{1,0:T(8,128)(2,1)S(1)} %reduce_sum.9), channel_id=1, source_target_pairs={{0,248},{8,0},{16,8},{24,16},{32,24},{40,32},{48,40},{56,48},{64,5... | collective-permute-start | bytes 18440 | tf_op jit(solution)/shard_map/ppermute | solution.py:16
  137.3 10.6 %collective-permute-start.8 = (bf16[24,128]{1,0:T(8,128)(2,1)S(1)}, bf16[24,128]{1,0:T(8,128)(2,1)S(1)}, u32[]{:S(2)}, u32[]{:S(2)}) collective-permute-start(bf16[24,128]{1,0:T(8,128)(2,1)S(1)} %reduce_sum.9), channel_id=1, source_target_pairs={{0,8},{8,16},{16,24},{24,32},{32,40},{40,48},{48,56},{56,64},{64,7... | collective-permute-start | bytes 18440 | tf_op jit(solution)/shard_map/ppermute | solution.py:16
  140.6 10.2 %collective-permute-start.11 = (bf16[24,128]{1,0:T(8,128)(2,1)S(1)}, bf16[24,128]{1,0:T(8,128)(2,1)S(1)}, u32[]{:S(2)}, u32[]{:S(2)}) collective-permute-start(bf16[24,128]{1,0:T(8,128)(2,1)S(1)} %reduce_sum.9), channel_id=1, source_target_pairs={{0,7},{1,0},{2,1},{3,2},{4,3},{5,4},{6,5},{7,6},{8,15},{9,8},{10,9... | collective-permute-start | bytes 18440 | tf_op jit(solution)/shard_map/ppermute | solution.py:16
  151.7 6.3 %copy-start = (f32[12,192,128]{2,1,0:T(8,128)S(1)}, f32[12,192,128]{2,1,0:T(8,128)}, u32[]{:S(2)}) copy-start(f32[12,192,128]{2,1,0:T(8,128)} %shard_map.83) | copy-start | bytes 3538948
  157.9 1.6 copy-start.16
  (17 other events, 24.5 us)

commit v3 on v2

--- a/solution.py
+++ b/solution.py
@@ -32,38 +32,57 @@
     return damping * jnp.stack(outputs, axis=3).reshape(vector.shape)
 
 
-def product_kernel(stored, rows, columns_ref, blocks_ref, source_ref, out_ref, picked):
+def product_kernel(stored, rows, columns_ref, blocks_ref, prev_ref, local_ref, *rest):
+    ghost_refs = rest[:-3]
+    out_ref, source, picked = rest[-3:]
     n = pl.program_id(0)
-    dof = source_ref.shape[1]
+    block_count, dof = local_ref.shape[0], local_ref.shape[1]
+    ghost_count = (source.shape[0] - block_count) // len(ghost_refs)
+
+    @pl.when(n == 0)
+    def _():
+        source[0:block_count] = local_ref[...]
+        for g, ref in enumerate(ghost_refs):
+            for b in range(ghost_count):
+                source[block_count + g * ghost_count + b] = ref[b * dof:(b + 1) * dof, :]
+
     for j in range(rows):
         for k in range(stored):
-            picked[k * dof:(k + 1) * dof, :] = source_ref[columns_ref[(n * rows + j) * stored + k]]
-        out_ref[j] = jnp.dot(blocks_ref[j], picked[...], preferred_element_type=jnp.float32)
-
-
-def block_product(blocks, columns, source):
+            picked[k * dof:(k + 1) * dof, :] = source[columns_ref[(n * rows + j) * stored + k]]
+        out_ref[j] = prev_ref[j] - jnp.dot(
+            blocks_ref[j], picked[...], preferred_element_type=jnp.float32
+        )
+
+
+def block_product(blocks, columns, prev, local, ghosts, ghost_count):
     block_count, dof, width = blocks.shape
     stored = width // dof
-    vectors = source.shape[-1]
+    vectors = local.shape[-1]
     rows = 6 if block_count % 6 == 0 else 1
+    whole = lambda shape: pl.BlockSpec(shape, lambda n, c: (0,) * len(shape))
     grid_spec = pltpu.PrefetchScalarGridSpec(
         num_scalar_prefetch=1,
         grid=(block_count // rows,),
         in_specs=[
             pl.BlockSpec((rows, dof, width), lambda n, c: (n, 0, 0)),
-            pl.BlockSpec(source.shape, lambda n, c: (0, 0, 0)),
+            pl.BlockSpec((rows, dof, vectors), lambda n, c: (n, 0, 0)),
+            whole(local.shape),
+        ]
+        + [whole(g.shape) for g in ghosts],
+        out_specs=pl.BlockSpec((rows, dof, vectors), lambda n, c: (n, 0, 0)),
+        scratch_shapes=[
+            pltpu.VMEM((block_count + len(ghosts) * ghost_count, dof, vectors), local.dtype),
+            pltpu.VMEM((width, vectors), local.dtype),
         ],
-        out_specs=pl.BlockSpec((rows, dof, vectors), lambda n, c: (n, 0, 0)),
-        scratch_shapes=[pltpu.VMEM((width, vectors), source.dtype)],
     )
     flops = 2 * block_count * dof * width * vectors
-    moved = blocks.size * 2 + source.size * 2 + block_count * dof * vectors * 4
+    moved = blocks.size * 2 + local.size * 2 * 3 + prev.size * 8
     return pl.pallas_call(
         functools.partial(product_kernel, stored, rows),
         grid_spec=grid_spec,
         out_shape=jax.ShapeDtypeStruct((block_count, dof, vectors), jnp.float32),
         cost_estimate=pl.CostEstimate(flops=flops, bytes_accessed=moved, transcendentals=0),
-    )(columns.reshape(-1), blocks, source)
+    )(columns.reshape(-1), blocks, prev, local, *ghosts)
 
 
 def gathered_copies(value, axis):
@@ -100,15 +119,19 @@
         jnp.float32
     )
 
+    ghost_rows = ghost_count * dof_count
+
     def outgoing(vector):
         shard_low = vector.astype(jnp.bfloat16)[0, 0]
         packed = jnp.take(shard_low, send_rows.reshape(-1), axis=0)
-        parts = [packed[g * ghost_count:(g + 1) * ghost_count] for g in range(groups)]
+        packed = packed.reshape((groups * ghost_rows, vectors))
+        parts = [packed[g * ghost_rows:(g + 1) * ghost_rows] for g in range(groups)]
         return shard_low, parts
 
-    def product(shard_low, ghosts):
-        source = jnp.concatenate([shard_low] + list(ghosts), axis=0)
-        return block_product(local_blocks, columns, source)[None, None]
+    def residual(prev, shard_low, ghosts):
+        return block_product(local_blocks, columns, prev[0, 0], shard_low, ghosts, ghost_count)[
+            None, None
+        ]
 
     tables = []
     for g in range(groups):
@@ -116,24 +139,19 @@
         member = jnp.take(onehot, send_rows[g], axis=1).astype(jnp.bfloat16)
         table = member.T[:, :, None, None] * jnp.transpose(picked, (1, 0, 2))[:, None, :, :]
         tables.append(table.reshape((ghost_count * coarse_rows * dof_count) // vectors, vectors))
-    ghost_rows = ghost_count * dof_count
 
     first_iter = point_smooth(smoother, rhs)
     shard_low, parts = outgoing(first_iter)
-    payloads = [
-        jnp.concatenate([parts[g].reshape(ghost_rows, vectors), tables[g]], axis=0)
-        for g in range(groups)
-    ]
-    arrived = exchange(payloads)
-    ghosts = [a[:ghost_rows].reshape((ghost_count, dof_count, vectors)) for a in arrived]
-    neighbour_tables = [
-        a[ghost_rows:].reshape((ghost_count, coarse_rows, dof_count)) for a in arrived
-    ]
-    residual_first = rhs - product(shard_low, ghosts)
+    residual_first = residual(rhs, shard_low, exchange(parts))
     update_second = point_smooth(smoother, residual_first)
     second_iter = first_iter + update_second
     shard_low, parts = outgoing(update_second)
-    residual_second = residual_first - product(shard_low, exchange(parts))
+    payloads = [jnp.concatenate([parts[g], tables[g]], axis=0) for g in range(groups)]
+    arrived = exchange(payloads)
+    neighbour_tables = [
+        a[ghost_rows:].reshape((ghost_count, coarse_rows, dof_count)) for a in arrived
+    ]
+    residual_second = residual(residual_first, shard_low, arrived)
     local_terms = jnp.einsum(
         "knd,ndr->nkr",
         shaped,
@@ -168,11 +186,13 @@
         jnp.einsum(
             "bjd,jr->bdr", neighbour_tables[g], neighbour_coarse[g],
             preferred_element_type=jnp.float32,
-        ).astype(jnp.bfloat16)
+        )
+        .astype(jnp.bfloat16)
+        .reshape((ghost_rows, vectors))
         for g in range(groups)
     ]
     correction_low = correction.astype(jnp.bfloat16)[0, 0]
-    residual_third = residual_second - product(correction_low, ghost_corrections)
+    residual_third = residual(residual_second, correction_low, ghost_corrections)
     return after_coarse + point_smooth(smoother, residual_third)
 
 

time: 164 us -> 158 us (0.963)
  local copies, waits for them, and re-layouts: 29.2 us -> 20.7 us
  starting transfers between devices: 48.3 us -> 52.4 us
  other arithmetic: 16.7 us -> 12.7 us
    slice x6 -> x2, local copies, waits for them, and re-layouts: 3.87 us -> 0.11 us  [outgoing(): parts = [packed[g * ghost_rows:(g + 1) * ghost_rows] for g in range(groups)]]
    all_to_all x1, starting transfers between devices: 7.61 us -> 11.2 us  [gathered_copies(): return lax.all_to_all(repeated, axis, 0, 0, tiled=True)]
    add x3, other arithmetic: 5.3 us -> 8.67 us  [point_smooth(): summed + factors[:, :, component, 2, :, :, None] * pieces[:, :, :, 2]]
    sub x2 -> x0, other arithmetic: 2.94 us -> none  [the longest x1 1.5 us: body(): residual_second - product(correction_low, ghost_corrections)]
    concatenate x4, other arithmetic: 2.83 us -> 0.07 us  [body(): jnp.concatenate([parts[g], tables[g]], axis=0)]
    ppermute x12, starting transfers between devices: 32.8 us -> 35.3 us  [passed_along(): return lax.ppermute(value, axis, pairs)]
    slice x4 -> x7, local copies, waits for them, and re-layouts: 3.09 us -> 0.78 us  [body(): a[ghost_rows:].reshape((ghost_count, coarse_rows, dof_count))]
    all_to_all x1, waiting for transfers between devices: 1.87 us -> 4.17 us  [body(): partial = lax.all_to_all(partial, 'col', 0, 0, tiled=True)]
  transfers between devices with their start and end apart: 14 -> 14, of which waited for: 8 -> 9; matrix products, arithmetic and copies ran while one was open for 14% -> 11% of each run, Pallas kernels for 0% -> 0%
where the time goes in v3:
time: 158 us; the launch traced here: 157 us
  starting transfers between devices  52.4 us (33%)
  waiting for transfers between devices  42 us (27%)
  local copies, waits for them, and re-layouts  20.7 us (13%)
  Pallas kernels  19.5 us (12%)
  other arithmetic  12.7 us (8%)
  matrix products  9.12 us (6%)
    ppermute x12, starting transfers between devices, passed_along(): return lax.ppermute(value, axis, pairs)  35.3 us
    ppermute x12, waiting for transfers between devices, passed_along(): return lax.ppermute(value, axis, pairs)  30.9 us
    pallas_call x3, Pallas kernels, block_product(): pl.pallas_call(functools.partial(product_kernel, stored, rows), grid_spec...  19.5 us
    all_to_all x1, starting transfers between devices, gathered_copies(): return lax.all_to_all(repeated, axis, 0, 0, tiled=True)  11.2 us
    add x3, other arithmetic, point_smooth(): summed + factors[:, :, component, 2, :, :, None] * pieces[:, :, :, 2]  8.67 us
    all_to_all x1, waiting for transfers between devices, gathered_copies(): return lax.all_to_all(repeated, axis, 0, 0, tiled=True)  6.91 us
    all_to_all x1, starting transfers between devices, body(): partial = lax.all_to_all(partial, 'col', 0, 0, tiled=True)  5.9 us
    unnamed x66, local copies, waits for them, and re-layouts  4.38 us
  transfers between devices with their start and end apart: 14, of which 9 were waited for; matrix products, arithmetic and copies ran while one was open for 11% of the time, Pallas kernels for 0%

profile of v3, /device:TPU:1, one launch (start us, length us, event | category | flops | bytes accessed | tf_op | source)
XLA Modules:
  0.0 157.2 jit_solution(5866808364149729360)
XLA Ops:
  1.7 2.9 %multiply_add_fusion.8 = (f32[1,1,12,1,64,128]{5,4,3,2,1,0:T(8,128)S(1)}, f32[1,1,12,1,64,128]{5,4,3,2,1,0:T(8,128)S(1)}, f32[1,1,12,1,64,128]{5,4,3,2,1,0:T(8,128)S(1)}) fusion(f32[1,1,12,3,64,128]{5,4,3,2,1,0:T(8,128)} %bitcast.133, f32[12,64]{1,0:T(8,128)S(1)} %get-tuple-element.42, f32[12,64]{1,0:T(8,128)S(1)} %get-tuple-element.43, ...), kind=kLoop, calls=%fused_computation.38 | loop fusion | flops 1474560 | bytes 2386944 | tf_op jit(solution)/shard_map/add | solution.py:30
  4.8 1.5 gather_fusion
  6.3 1.3 broadcast_select_fusion.1
  7.7 3.1 %collective-permute-start.2 = (bf16[768,128]{1,0:T(8,128)(2,1)S(1)}, bf16[768,128]{1,0:T(8,128)(2,1)S(1)}, u32[]{:S(2)}, u32[]{:S(2)}) collective-permute-start(bf16[768,128]{1,0:T(8,128)(2,1)S(1)} %bitcast.150), channel_id=1, source_target_pairs={{0,1},{1,2},{2,3},{3,4},{4,5},{5,6},{6,7},{7,0},{8,9},{9,10},{10,1... | collective-permute-start | bytes 589832 | tf_op jit(solution)/shard_map/ppermute | solution.py:16
  11.1 10.4 %collective-permute-start.1 = (bf16[768,128]{1,0:T(8,128)(2,1)S(1)}, bf16[768,128]{1,0:T(8,128)(2,1)S(1)}, u32[]{:S(2)}, u32[]{:S(2)}) collective-permute-start(bf16[768,128]{1,0:T(8,128)(2,1)S(1)} %bitcast.148), channel_id=1, source_target_pairs={{0,248},{8,0},{16,8},{24,16},{32,24},{40,32},{48,40},{56,48},{64,5... | collective-permute-start | bytes 589832 | tf_op jit(solution)/shard_map/ppermute | solution.py:16
  28.2 12.1 %collective-permute-done.rest_0_ = bf16[768,128]{1,0:T(8,128)(2,1)S(1)} collective-permute-done((bf16[768,128]{1,0:T(8,128)(2,1)S(1)}, bf16[768,128]{1,0:T(8,128)(2,1)S(1)}, u32[]{:S(2)}, u32[]{:S(2)}) %collective-permute-start) | collective-permute-done | bytes 196640 | tf_op jit(solution)/shard_map/ppermute | solution.py:16
  41.0 6.4 %shard_map.82.prev_ref = f32[12,192,128]{2,1,0:T(8,128)} custom-call(s32[96]{0:T(128)} %reshape_squeeze.12.columns_ref, bf16[12,192,1536]{2,1,0:T(8,128)(2,1)} %bitcast.125, f32[12,192,128]{2,1,0:T(8,128)} %bitcast.134, bf16[12,192,128]{2,1,0:T(8,128)(2,1)} %bitcast.132, bf16[768,128]{1,0:T(8,128)(2,1)} %copy-done.11, bf16[768,128]{1,0:T(8,128)(2,1)} %copy-done.10, ...), custom_call_target="tpu_custom_call" | custom-call | flops 905969664 | bytes 11206656 | tf_op jit(solution)/shard_map/pallas_call | solution.py:80
  47.5 2.9 %multiply_add_fusion.5 = (f32[1,1,12,1,64,128]{5,4,3,2,1,0:T(8,128)S(1)}, f32[1,1,12,1,64,128]{5,4,3,2,1,0:T(8,128)S(1)}, f32[1,1,12,1,64,128]{5,4,3,2,1,0:T(8,128)S(1)}) fusion(f32[1,1,12,3,64,128]{5,4,3,2,1,0:T(8,128)} %bitcast.128, f32[12,64]{1,0:T(8,128)S(1)} %get-tuple-element.42, f32[12,64]{1,0:T(8,128)S(1)} %get-tuple-element.43, ...), kind=kLoop, calls=%fused_computation.35 | loop fusion | flops 1474560 | bytes 2386944 | tf_op jit(solution)/shard_map/add | solution.py:30
  51.7 9.7 %collective-permute-start.5 = (bf16[912,128]{1,0:T(8,128)(2,1)S(1)}, bf16[912,128]{1,0:T(8,128)(2,1)S(1)}, u32[]{:S(2)}, u32[]{:S(2)}) collective-permute-start(bf16[912,128]{1,0:T(8,128)(2,1)S(1)} %pad_maximum_fusion.1), channel_id=1, source_target_pairs={{0,248},{8,0},{16,8},{24,16},{32,24},{40,32},{48,40},{56,48},{64,5... | collective-permute-start | bytes 700424 | tf_op jit(solution)/shard_map/ppermute | solution.py:16
  61.4 4.7 %collective-permute-start.6 = (bf16[912,128]{1,0:T(8,128)(2,1)S(1)}, bf16[912,128]{1,0:T(8,128)(2,1)S(1)}, u32[]{:S(2)}, u32[]{:S(2)}) collective-permute-start(bf16[912,128]{1,0:T(8,128)(2,1)S(1)} %pad_maximum_fusion.2), channel_id=1, source_target_pairs={{0,1},{1,2},{2,3},{3,4},{4,5},{5,6},{6,7},{7,0},{8,9},{9,10},{10,1... | collective-permute-start | bytes 700424 | tf_op jit(solution)/shard_map/ppermute | solution.py:16
  68.2 9.1 %collective-permute-done.6.rest_2_ = bf16[912,128]{1,0:T(8,128)(2,1)S(1)} collective-permute-done((bf16[912,128]{1,0:T(8,128)(2,1)S(1)}, bf16[912,128]{1,0:T(8,128)(2,1)S(1)}, u32[]{:S(2)}, u32[]{:S(2)}) %collective-permute-start.6) | collective-permute-done | bytes 233504 | tf_op jit(solution)/shard_map/ppermute | solution.py:16
  78.0 3.4 %collective-permute-done.7.rest_3_ = bf16[912,128]{1,0:T(8,128)(2,1)} collective-permute-done((bf16[912,128]{1,0:T(8,128)(2,1)S(1)}, bf16[912,128]{1,0:T(8,128)(2,1)}, u32[]{:S(2)}, u32[]{:S(2)}) %collective-permute-start.7) | collective-permute-done | bytes 233504 | tf_op jit(solution)/shard_map/ppermute | solution.py:16
  81.4 6.6 %shard_map.83.prev_ref = f32[12,192,128]{2,1,0:T(8,128)} custom-call(s32[96]{0:T(128)} %reshape_squeeze.12.columns_ref, bf16[12,192,1536]{2,1,0:T(8,128)(2,1)} %bitcast.126, f32[12,192,128]{2,1,0:T(8,128)} %shard_map.82.prev_ref, bf16[12,192,128]{2,1,0:T(8,128)(2,1)} %bitcast.130, bf16[912,128]{1,0:T(8,128)(2,1)} %copy-done.5, bf16[912,128]{1,0:T(8,128)(2,1)} %copy-done.6, ...), custom_call_target="tpu_custom_call" | custom-call | flops 905969664 | bytes 11206656 | tf_op jit(solution)/shard_map/pallas_call | solution.py:80
  88.0 1.5 convolution_bitcast_fusion.1
  90.4 1.3 broadcast_in_dim.28
  91.7 1.4 broadcast_in_dim.42
  93.1 11.2 %all-to-all-start = ((bf16[32,24,128]{2,1,0:T(8,128)(2,1)}), bf16[32,24,128]{2,1,0:T(8,128)(2,1)}, u32[]{:S(2)}, u32[]{:S(2)}) async-start(bf16[32,24,128]{2,1,0:T(8,128)(2,1)} %broadcast_in_dim.42), calls=%async_computation | async-start | bytes 393216 | tf_op jit(solution)/shard_map/all_to_all | solution.py:92
  104.4 2.8 %copy.23 = bf16[192,6144]{0,1:T(8,128)(2,1)} copy(bf16[192,6144]{1,0:T(8,128)(2,1)S(1)} %copy-done.2) | data formatting | bytes 4718592 | tf_op args[7]
  108.2 1.1 reshape.397
  109.3 6.9 %all-to-all-done = bf16[32,24,128]{2,1,0:T(8,128)(2,1)} async-done(((bf16[32,24,128]{2,1,0:T(8,128)(2,1)}), bf16[32,24,128]{2,1,0:T(8,128)(2,1)}, u32[]{:S(2)}, u32[]{:S(2)}) %all-to-all-start) | async-done | bytes 196640 | tf_op jit(solution)/shard_map/all_to_all | solution.py:92
  116.3 2.2 %fusion = f32[8,24,128]{2,1,0:T(8,128)} fusion(bf16[768,128,1]{1,0,2:T(8,128)(2,1)} %bitcast.50, bf16[8,24,768]{1,0,2:T(8,128)(2,1)S(1)} %reshape.397), kind=kOutput, calls=%fused_computation.10 | convolution fusion | flops 37748736 | bytes 589824 | tf_op jit(solution)/shard_map/dot_general | solution.py:169
  118.4 5.9 %all-to-all-start.1 = ((f32[8,24,128]{2,1,0:T(8,128)}), f32[8,24,128]{2,1,0:T(8,128)S(1)}, u32[]{:S(2)}, u32[]{:S(2)}) async-start(f32[8,24,128]{2,1,0:T(8,128)} %fusion), calls=%async_computation.1 | async-start | bytes 196608 | tf_op jit(solution)/shard_map/all_to_all | solution.py:170
  125.5 4.2 %all-to-all-done.1 = f32[8,24,128]{2,1,0:T(8,128)S(1)} async-done(((f32[8,24,128]{2,1,0:T(8,128)}), f32[8,24,128]{2,1,0:T(8,128)S(1)}, u32[]{:S(2)}, u32[]{:S(2)}) %all-to-all-start.1) | async-done | bytes 98336 | tf_op jit(solution)/shard_map/all_to_all | solution.py:170
  129.7 1.5 collective-permute-start.10
  131.2 1.6 %collective-permute-start.9 = (bf16[24,128]{1,0:T(8,128)(2,1)S(1)}, bf16[24,128]{1,0:T(8,128)(2,1)S(1)}, u32[]{:S(2)}, u32[]{:S(2)}) collective-permute-start(bf16[24,128]{1,0:T(8,128)(2,1)S(1)} %reduce_sum.9), channel_id=1, source_target_pairs={{0,248},{8,0},{16,8},{24,16},{32,24},{40,32},{48,40},{56,48},{64,5... | collective-permute-start | bytes 18440 | tf_op jit(solution)/shard_map/ppermute | solution.py:16
  132.8 3.7 %collective-permute-start.8 = (bf16[24,128]{1,0:T(8,128)(2,1)S(1)}, bf16[24,128]{1,0:T(8,128)(2,1)S(1)}, u32[]{:S(2)}, u32[]{:S(2)}) collective-permute-start(bf16[24,128]{1,0:T(8,128)(2,1)S(1)} %reduce_sum.9), channel_id=1, source_target_pairs={{0,8},{8,16},{16,24},{24,32},{32,40},{40,48},{48,56},{56,64},{64,7... | collective-permute-start | bytes 18440 | tf_op jit(solution)/shard_map/ppermute | solution.py:16
  137.0 1.2 fusion.28
  138.2 1.4 collective-permute-done.11
  140.5 2.9 %collective-permute-done.8 = bf16[24,128]{1,0:T(8,128)(2,1)S(1)} collective-permute-done((bf16[24,128]{1,0:T(8,128)(2,1)S(1)}, bf16[24,128]{1,0:T(8,128)(2,1)S(1)}, u32[]{:S(2)}, u32[]{:S(2)}) %collective-permute-start.8) | collective-permute-done | bytes 6176 | tf_op jit(solution)/shard_map/ppermute | solution.py:16
  146.3 6.5 %shard_map.84 = f32[12,192,128]{2,1,0:T(8,128)} custom-call(s32[96]{0:T(128)} %reshape_squeeze.12.columns_ref, bf16[12,192,1536]{2,1,0:T(8,128)(2,1)} %bitcast.127, f32[12,192,128]{2,1,0:T(8,128)} %shard_map.83.prev_ref, bf16[12,192,128]{2,1,0:T(8,128)(2,1)} %get-tuple-element.50.local_ref, bf16[768,128]{1,0:T(8,128)(2,1)} %bitcast.144, ...), custom_call_target="tpu_custom_call" | custom-call | flops 905969664 | bytes 11206656 | tf_op jit(solution)/shard_map/pallas_call | solution.py:80
  152.9 2.9 %multiply_add_fusion.2 = (f32[1,1,12,1,64,128]{5,4,3,2,1,0:T(8,128)S(1)}, f32[1,1,12,1,64,128]{5,4,3,2,1,0:T(8,128)S(1)}, f32[1,1,12,1,64,128]{5,4,3,2,1,0:T(8,128)S(1)}) fusion(f32[1,1,12,3,64,128]{5,4,3,2,1,0:T(8,128)} %bitcast.135, f32[12,64]{1,0:T(8,128)S(1)} %copy-done.23, f32[12,64]{1,0:T(8,128)S(1)} %copy-done.25, f32[12,64]{1,0:T(8,128)S(1)} %get-tuple-element.35, ...), kind=kLoop, calls=%fused_computation.32 | loop fusion | flops 1474560 | bytes 2386944 | tf_op jit(solution)/shard_map/add | solution.py:30
  155.9 1.2 add_bitcast_fusion
  (144 shorter events, 21.0 us)
Async XLA Ops:
  1.6 45.8 %copy-start.12 = (f32[12,64]{1,0:T(8,128)}, f32[12,64]{1,0:T(8,128)S(1)}, u32[]{:S(2)}) copy-start(f32[12,64]{1,0:T(8,128)S(1)} %get-tuple-element.37) | copy-start | bytes 9220
  1.6 45.8 %copy-start.14 = (f32[12,64]{1,0:T(8,128)}, f32[12,64]{1,0:T(8,128)S(1)}, u32[]{:S(2)}) copy-start(f32[12,64]{1,0:T(8,128)S(1)} %get-tuple-element.38) | copy-start | bytes 9220
  1.6 45.8 %copy-start.16 = (f32[12,64]{1,0:T(8,128)}, f32[12,64]{1,0:T(8,128)S(1)}, u32[]{:S(2)}) copy-start(f32[12,64]{1,0:T(8,128)S(1)} %get-tuple-element.39) | copy-start | bytes 9220
  1.6 45.8 %copy-start.18 = (f32[12,64]{1,0:T(8,128)}, f32[12,64]{1,0:T(8,128)S(1)}, u32[]{:S(2)}) copy-start(f32[12,64]{1,0:T(8,128)S(1)} %get-tuple-element.40) | copy-start | bytes 9220
  1.7 45.8 %copy-start.20 = (f32[12,64]{1,0:T(8,128)}, f32[12,64]{1,0:T(8,128)S(1)}, u32[]{:S(2)}) copy-start(f32[12,64]{1,0:T(8,128)S(1)} %get-tuple-element.41) | copy-start | bytes 9220
  1.7 45.8 %copy-start.22 = (f32[12,64]{1,0:T(8,128)}, f32[12,64]{1,0:T(8,128)S(1)}, u32[]{:S(2)}) copy-start(f32[12,64]{1,0:T(8,128)S(1)} %get-tuple-element.42) | copy-start | bytes 9220
  1.7 45.8 %copy-start.24 = (f32[12,64]{1,0:T(8,128)}, f32[12,64]{1,0:T(8,128)S(1)}, u32[]{:S(2)}) copy-start(f32[12,64]{1,0:T(8,128)S(1)} %get-tuple-element.43) | copy-start | bytes 9220
  7.6 13.9 %copy-start.27 = (s32[1,1,4,4]{3,2,1,0:T(4,128)S(1)}, s32[1,1,4,4]{3,2,1,0:T(4,128)}, u32[]{:S(2)}) copy-start(s32[1,1,4,4]{3,2,1,0:T(4,128)} %param.18) | copy-start | bytes 196
  7.6 13.9 %copy-start.29 = (s32[1,1,12]{2,1,0:T(1,128)S(1)}, s32[1,1,12]{2,1,0:T(1,128)}, u32[]{:S(2)}) copy-start(s32[1,1,12]{2,1,0:T(1,128)} %param.19) | copy-start | bytes 148
  7.6 15.1 %copy-start.26 = (bf16[1,1,6,2304]{3,2,1,0:T(8,128)(2,1)S(1)}, bf16[1,1,6,2304]{3,2,1,0:T(8,128)(2,1)}, u32[]{:S(2)}) copy-start(bf16[1,1,6,2304]{3,2,1,0:T(8,128)(2,1)} %param.20) | copy-start | bytes 82948
  7.6 18.6 %copy-start.28 = (s32[1,1,12,8]{2,3,1,0:T(8,128)S(1)}, s32[1,1,12,8]{2,3,1,0:T(8,128)}, u32[]{:S(2)}) copy-start(s32[1,1,12,8]{2,3,1,0:T(8,128)} %param.17) | copy-start | bytes 1156
  7.7 20.5 %collective-permute-start.2 = (bf16[768,128]{1,0:T(8,128)(2,1)S(1)}, bf16[768,128]{1,0:T(8,128)(2,1)S(1)}, u32[]{:S(2)}, u32[]{:S(2)}) collective-permute-start(bf16[768,128]{1,0:T(8,128)(2,1)S(1)} %bitcast.150), channel_id=1, source_target_pairs={{0,1},{1,2},{2,3},{3,4},{4,5},{5,6},{6,7},{7,0},{8,9},{9,10},{10,1... | collective-permute-start | bytes 589832 | tf_op jit(solution)/shard_map/ppermute | solution.py:16
  10.8 17.4 %collective-permute-start.3 = (bf16[768,128]{1,0:T(8,128)(2,1)S(1)}, bf16[768,128]{1,0:T(8,128)(2,1)S(1)}, u32[]{:S(2)}, u32[]{:S(2)}) collective-permute-start(bf16[768,128]{1,0:T(8,128)(2,1)S(1)} %bitcast.149), channel_id=1, source_target_pairs={{0,7},{1,0},{2,1},{3,2},{4,3},{5,4},{6,5},{7,6},{8,15},{9,8},{10,9... | collective-permute-start | bytes 589832 | tf_op jit(solution)/shard_map/ppermute | solution.py:16
  11.1 17.2 %collective-permute-start.1 = (bf16[768,128]{1,0:T(8,128)(2,1)S(1)}, bf16[768,128]{1,0:T(8,128)(2,1)S(1)}, u32[]{:S(2)}, u32[]{:S(2)}) collective-permute-start(bf16[768,128]{1,0:T(8,128)(2,1)S(1)} %bitcast.148), channel_id=1, source_target_pairs={{0,248},{8,0},{16,8},{24,16},{32,24},{40,32},{48,40},{56,48},{64,5... | collective-permute-start | bytes 589832 | tf_op jit(solution)/shard_map/ppermute | solution.py:16
  21.4 18.9 %collective-permute-start = (bf16[768,128]{1,0:T(8,128)(2,1)S(1)}, bf16[768,128]{1,0:T(8,128)(2,1)S(1)}, u32[]{:S(2)}, u32[]{:S(2)}) collective-permute-start(bf16[768,128]{1,0:T(8,128)(2,1)S(1)} %bitcast.147), channel_id=1, source_target_pairs={{0,8},{8,16},{16,24},{24,32},{32,40},{40,48},{48,56},{56,64},{64,7... | collective-permute-start | bytes 589832 | tf_op jit(solution)/shard_map/ppermute | solution.py:16
  22.8 24.6 %copy-start.3 = (bf16[6,12,192]{2,1,0:T(8,128)(2,1)}, bf16[6,12,192]{2,1,0:T(8,128)(2,1)S(1)}, u32[]{:S(2)}) copy-start(bf16[6,12,192]{2,1,0:T(8,128)(2,1)S(1)} %reshape_squeeze.14) | copy-start | bytes 82948
  28.2 12.1 %copy-start.8 = (bf16[768,128]{1,0:T(8,128)(2,1)}, bf16[768,128]{1,0:T(8,128)(2,1)S(1)}, u32[]{:S(2)}) copy-start(bf16[768,128]{1,0:T(8,128)(2,1)S(1)} %collective-permute-done.2.rest_2_) | copy-start | bytes 589828
  28.2 12.1 %copy-start.9 = (bf16[768,128]{1,0:T(8,128)(2,1)}, bf16[768,128]{1,0:T(8,128)(2,1)S(1)}, u32[]{:S(2)}) copy-start(bf16[768,128]{1,0:T(8,128)(2,1)S(1)} %collective-permute-done.3.rest_3_) | copy-start | bytes 589828
  51.6 15.6 %collective-permute-start.4 = (bf16[912,128]{1,0:T(8,128)(2,1)S(1)}, bf16[912,128]{1,0:T(8,128)(2,1)S(1)}, u32[]{:S(2)}, u32[]{:S(2)}) collective-permute-start(bf16[912,128]{1,0:T(8,128)(2,1)S(1)} %pad_maximum_fusion), channel_id=1, source_target_pairs={{0,8},{8,16},{16,24},{24,32},{32,40},{40,48},{48,56},{56,64},{64,7... | collective-permute-start | bytes 700424 | tf_op jit(solution)/shard_map/ppermute | solution.py:16
  51.7 16.5 %collective-permute-start.5 = (bf16[912,128]{1,0:T(8,128)(2,1)S(1)}, bf16[912,128]{1,0:T(8,128)(2,1)S(1)}, u32[]{:S(2)}, u32[]{:S(2)}) collective-permute-start(bf16[912,128]{1,0:T(8,128)(2,1)S(1)} %pad_maximum_fusion.1), channel_id=1, source_target_pairs={{0,248},{8,0},{16,8},{24,16},{32,24},{40,32},{48,40},{56,48},{64,5... | collective-permute-start | bytes 700424 | tf_op jit(solution)/shard_map/ppermute | solution.py:16
  61.4 15.9 %collective-permute-start.6 = (bf16[912,128]{1,0:T(8,128)(2,1)S(1)}, bf16[912,128]{1,0:T(8,128)(2,1)S(1)}, u32[]{:S(2)}, u32[]{:S(2)}) collective-permute-start(bf16[912,128]{1,0:T(8,128)(2,1)S(1)} %pad_maximum_fusion.2), channel_id=1, source_target_pairs={{0,1},{1,2},{2,3},{3,4},{4,5},{5,6},{6,7},{7,0},{8,9},{9,10},{10,1... | collective-permute-start | bytes 700424 | tf_op jit(solution)/shard_map/ppermute | solution.py:16
  66.1 15.3 %collective-permute-start.7 = (bf16[912,128]{1,0:T(8,128)(2,1)S(1)}, bf16[912,128]{1,0:T(8,128)(2,1)}, u32[]{:S(2)}, u32[]{:S(2)}) collective-permute-start(bf16[912,128]{1,0:T(8,128)(2,1)S(1)} %pad_maximum_fusion.3), channel_id=1, source_target_pairs={{0,7},{1,0},{2,1},{3,2},{4,3},{5,4},{6,5},{7,6},{8,15},{9,8},{10,9... | collective-permute-start | bytes 700424 | tf_op jit(solution)/shard_map/ppermute | solution.py:16
  81.4 22.9 %copy-start.2 = (bf16[192,6144]{1,0:T(8,128)(2,1)S(1)}, bf16[192,6144]{1,0:T(8,128)(2,1)}, u32[]{:S(2)}) copy-start(bf16[192,6144]{1,0:T(8,128)(2,1)} %param.21) | copy-start | bytes 7077892
  93.1 23.1 %all-to-all-start = ((bf16[32,24,128]{2,1,0:T(8,128)(2,1)}), bf16[32,24,128]{2,1,0:T(8,128)(2,1)}, u32[]{:S(2)}, u32[]{:S(2)}) async-start(bf16[32,24,128]{2,1,0:T(8,128)(2,1)} %broadcast_in_dim.42), calls=%async_computation | async-start | bytes 393216 | tf_op jit(solution)/shard_map/all_to_all | solution.py:92
  109.3 15.0 %slice-start = ((bf16[912,128]{1,0:T(8,128)(2,1)}), bf16[144,128]{1,0:T(8,128)(2,1)S(1)}, s32[]{:S(2)}) async-start(bf16[912,128]{1,0:T(8,128)(2,1)} %copy-done.5), calls=%async_computation.2 | async-start | bytes 73728 | tf_op jit(solution)/shard_map/slice | solution.py:152
  116.3 20.5 %copy-start.31 = (s32[1,1,12]{2,1,0:T(1,128)S(1)}, s32[1,1,12]{2,1,0:T(1,128)}, u32[]{:S(2)}) copy-start(s32[1,1,12]{2,1,0:T(1,128)} %param.19) | copy-start | bytes 148
  116.3 20.7 %copy-start.4 = (bf16[6,12,192]{2,1,0:T(8,128)(2,1)S(1)}, bf16[6,12,192]{2,1,0:T(8,128)(2,1)}, u32[]{:S(2)}) copy-start(bf16[6,12,192]{2,1,0:T(8,128)(2,1)} %copy-done.3) | copy-start | bytes 82948
  118.4 11.3 %all-to-all-start.1 = ((f32[8,24,128]{2,1,0:T(8,128)}), f32[8,24,128]{2,1,0:T(8,128)S(1)}, u32[]{:S(2)}, u32[]{:S(2)}) async-start(f32[8,24,128]{2,1,0:T(8,128)} %fusion), calls=%async_computation.1 | async-start | bytes 196608 | tf_op jit(solution)/shard_map/all_to_all | solution.py:170
  129.7 15.6 %collective-permute-start.10 = (bf16[24,128]{1,0:T(8,128)(2,1)S(1)}, bf16[24,128]{1,0:T(8,128)(2,1)S(1)}, u32[]{:S(2)}, u32[]{:S(2)}) collective-permute-start(bf16[24,128]{1,0:T(8,128)(2,1)S(1)} %reduce_sum.9), channel_id=1, source_target_pairs={{0,1},{1,2},{2,3},{3,4},{4,5},{5,6},{6,7},{7,0},{8,9},{9,10},{10,1... | collective-permute-start | bytes 18440 | tf_op jit(solution)/shard_map/ppermute | solution.py:16
  131.2 13.2 %collective-permute-start.9 = (bf16[24,128]{1,0:T(8,128)(2,1)S(1)}, bf16[24,128]{1,0:T(8,128)(2,1)S(1)}, u32[]{:S(2)}, u32[]{:S(2)}) collective-permute-start(bf16[24,128]{1,0:T(8,128)(2,1)S(1)} %reduce_sum.9), channel_id=1, source_target_pairs={{0,248},{8,0},{16,8},{24,16},{32,24},{40,32},{48,40},{56,48},{64,5... | collective-permute-start | bytes 18440 | tf_op jit(solution)/shard_map/ppermute | solution.py:16
  132.8 10.6 %collective-permute-start.8 = (bf16[24,128]{1,0:T(8,128)(2,1)S(1)}, bf16[24,128]{1,0:T(8,128)(2,1)S(1)}, u32[]{:S(2)}, u32[]{:S(2)}) collective-permute-start(bf16[24,128]{1,0:T(8,128)(2,1)S(1)} %reduce_sum.9), channel_id=1, source_target_pairs={{0,8},{8,16},{16,24},{24,32},{32,40},{40,48},{48,56},{56,64},{64,7... | collective-permute-start | bytes 18440 | tf_op jit(solution)/shard_map/ppermute | solution.py:16
  136.6 3.1 %collective-permute-start.11 = (bf16[24,128]{1,0:T(8,128)(2,1)S(1)}, bf16[24,128]{1,0:T(8,128)(2,1)S(1)}, u32[]{:S(2)}, u32[]{:S(2)}) collective-permute-start(bf16[24,128]{1,0:T(8,128)(2,1)S(1)} %reduce_sum.9), channel_id=1, source_target_pairs={{0,7},{1,0},{2,1},{3,2},{4,3},{5,4},{6,5},{7,6},{8,15},{9,8},{10,9... | collective-permute-start | bytes 18440 | tf_op jit(solution)/shard_map/ppermute | solution.py:16
  (17 other events, 100.5 us)

commit v4 on v3

--- a/solution.py
+++ b/solution.py
@@ -32,9 +32,28 @@
     return damping * jnp.stack(outputs, axis=3).reshape(vector.shape)
 
 
-def product_kernel(stored, rows, columns_ref, blocks_ref, prev_ref, local_ref, *rest):
-    ghost_refs = rest[:-3]
-    out_ref, source, picked = rest[-3:]
+def smoothed(factors_ref, j, vector):
+    grains = vector.shape[0] // 3
+    pieces = [vector[c * grains:(c + 1) * grains] for c in range(3)]
+    outputs = []
+    for component in range(3):
+        weight = [factors_ref[j, component, c].astype(jnp.float32) for c in range(3)]
+        summed = weight[0] * pieces[0]
+        summed = summed + weight[1] * pieces[1]
+        summed = summed + weight[2] * pieces[2]
+        outputs.append(damping * summed)
+    return jnp.concatenate(outputs, axis=0)
+
+
+def product_kernel(stored, rows, mode, ghost_total, columns_ref, blocks_ref, prev_ref, local_ref, *rest):
+    ghost_refs = rest[:ghost_total]
+    rest = rest[ghost_total:]
+    if mode == "plain":
+        (out_ref, source, picked) = rest
+    elif mode == "smooth":
+        (factors_ref, base_ref, out_ref, next_ref, low_ref, source, picked) = rest
+    else:
+        (factors_ref, base_ref, out_ref, source, picked) = rest
     n = pl.program_id(0)
     block_count, dof = local_ref.shape[0], local_ref.shape[1]
     ghost_count = (source.shape[0] - block_count) // len(ghost_refs)
@@ -49,40 +68,59 @@
     for j in range(rows):
         for k in range(stored):
             picked[k * dof:(k + 1) * dof, :] = source[columns_ref[(n * rows + j) * stored + k]]
-        out_ref[j] = prev_ref[j] - jnp.dot(
-            blocks_ref[j], picked[...], preferred_element_type=jnp.float32
-        )
-
-
-def block_product(blocks, columns, prev, local, ghosts, ghost_count):
+        left = prev_ref[j] - jnp.dot(blocks_ref[j], picked[...], preferred_element_type=jnp.float32)
+        if mode == "plain":
+            out_ref[j] = left
+        elif mode == "smooth":
+            out_ref[j] = left
+            update = smoothed(factors_ref, j, left)
+            next_ref[j] = base_ref[j] + update
+            low_ref[j] = update.astype(low_ref.dtype)
+        else:
+            out_ref[j] = base_ref[j] + smoothed(factors_ref, j, left)
+
+
+def block_product(blocks, columns, prev, local, ghosts, ghost_count, mode="plain", factors=None, base=None):
     block_count, dof, width = blocks.shape
     stored = width // dof
     vectors = local.shape[-1]
     rows = 6 if block_count % 6 == 0 else 1
     whole = lambda shape: pl.BlockSpec(shape, lambda n, c: (0,) * len(shape))
+    tile = pl.BlockSpec((rows, dof, vectors), lambda n, c: (n, 0, 0))
+    field = jax.ShapeDtypeStruct((block_count, dof, vectors), jnp.float32)
+    in_specs = [
+        pl.BlockSpec((rows, dof, width), lambda n, c: (n, 0, 0)),
+        tile,
+        whole(local.shape),
+    ] + [whole(g.shape) for g in ghosts]
+    operands = [blocks, prev, local] + list(ghosts)
+    if mode != "plain":
+        in_specs += [pl.BlockSpec((rows,) + factors.shape[1:], lambda n, c: (n, 0, 0, 0, 0)), tile]
+        operands += [factors, base]
+    if mode == "smooth":
+        out_specs = [tile, tile, tile]
+        out_shape = [field, field, jax.ShapeDtypeStruct(field.shape, jnp.bfloat16)]
+    else:
+        out_specs = tile
+        out_shape = field
     grid_spec = pltpu.PrefetchScalarGridSpec(
         num_scalar_prefetch=1,
         grid=(block_count // rows,),
-        in_specs=[
-            pl.BlockSpec((rows, dof, width), lambda n, c: (n, 0, 0)),
-            pl.BlockSpec((rows, dof, vectors), lambda n, c: (n, 0, 0)),
-            whole(local.shape),
-        ]
-        + [whole(g.shape) for g in ghosts],
-        out_specs=pl.BlockSpec((rows, dof, vectors), lambda n, c: (n, 0, 0)),
+        in_specs=in_specs,
+        out_specs=out_specs,
         scratch_shapes=[
             pltpu.VMEM((block_count + len(ghosts) * ghost_count, dof, vectors), local.dtype),
             pltpu.VMEM((width, vectors), local.dtype),
         ],
     )
     flops = 2 * block_count * dof * width * vectors
-    moved = blocks.size * 2 + local.size * 2 * 3 + prev.size * 8
+    moved = blocks.size * 2 + local.size * 2 * 3 + prev.size * 8 * (1 if mode == "plain" else 3)
     return pl.pallas_call(
-        functools.partial(product_kernel, stored, rows),
+        functools.partial(product_kernel, stored, rows, mode, len(ghosts)),
         grid_spec=grid_spec,
-        out_shape=jax.ShapeDtypeStruct((block_count, dof, vectors), jnp.float32),
+        out_shape=out_shape,
         cost_estimate=pl.CostEstimate(flops=flops, bytes_accessed=moved, transcendentals=0),
-    )(columns.reshape(-1), blocks, prev, local, *ghosts)
+    )(columns.reshape(-1), *operands)
 
 
 def gathered_copies(value, axis):
@@ -133,6 +171,10 @@
             None, None
         ]
 
+    grains = dof_count // 3
+    factors = jnp.transpose(smoother[0, 0].reshape((3, 3, block_count, grains)), (2, 0, 1, 3))
+    factors = jnp.broadcast_to(factors[..., None], factors.shape + (vectors,))
+
     tables = []
     for g in range(groups):
         picked = jnp.take(shaped, send_rows[g], axis=1)
@@ -142,10 +184,13 @@
 
     first_iter = point_smooth(smoother, rhs)
     shard_low, parts = outgoing(first_iter)
-    residual_first = residual(rhs, shard_low, exchange(parts))
-    update_second = point_smooth(smoother, residual_first)
-    second_iter = first_iter + update_second
-    shard_low, parts = outgoing(update_second)
+    residual_first, second_iter, update_low = block_product(
+        local_blocks, columns, rhs[0, 0], shard_low, exchange(parts), ghost_count,
+        mode="smooth", factors=factors, base=first_iter[0, 0],
+    )
+    residual_first = residual_first[None, None]
+    second_iter = second_iter[None, None]
+    shard_low, parts = outgoing(update_low[None, None])
     payloads = [jnp.concatenate([parts[g], tables[g]], axis=0) for g in range(groups)]
     arrived = exchange(payloads)
     neighbour_tables = [
@@ -192,8 +237,11 @@
         for g in range(groups)
     ]
     correction_low = correction.astype(jnp.bfloat16)[0, 0]
-    residual_third = residual(residual_second, correction_low, ghost_corrections)
-    return after_coarse + point_smooth(smoother, residual_third)
+    smoothed_solution = block_product(
+        local_blocks, columns, residual_second[0, 0], correction_low, ghost_corrections,
+        ghost_count, mode="final", factors=factors, base=after_coarse[0, 0],
+    )
+    return smoothed_solution[None, None]
 
 
 def solution(mesh):

time: 158 us -> 151 us (0.956)
  other arithmetic: 12.7 us -> 5.61 us
  local copies, waits for them, and re-layouts: 20.7 us -> 18.4 us
  waiting for transfers between devices: 42 us -> 44.2 us
  Pallas kernels: 19.5 us -> 21.4 us
    add x3 -> x1, other arithmetic: 8.67 us -> 2.89 us  [point_smooth(): summed + factors[:, :, component, 2, :, :, None] * pieces[:, :, :, 2]]
    broadcast_in_dim x0 -> x1, local copies, waits for them, and re-layouts: none -> 1.97 us  [body(): factors = jnp.broadcast_to(factors[..., None], factors.shape + (vectors,))]
    broadcast_in_dim x2, local copies, waits for them, and re-layouts: 2.69 us -> 0.72 us  [gathered_copies(): repeated = jnp.broadcast_to(value[None], (count,) + value.shape)]
    pallas_call x3, Pallas kernels: 19.5 us -> 21.4 us  [block_product(): pl.pallas_call(functools.partial(product_kernel, stored, rows, mode, len(...]
    unnamed x66 -> x38, local copies, waits for them, and re-layouts: 4.38 us -> 4.1 us
where the time goes in v4:
time: 151 us; the launch traced here: 150 us
  starting transfers between devices  51.9 us (34%)
  waiting for transfers between devices  44.2 us (29%)
  Pallas kernels  21.4 us (14%)
  local copies, waits for them, and re-layouts  18.4 us (12%)
  matrix products  8.27 us (5%)
  other arithmetic  5.61 us (4%)
    ppermute x12, starting transfers between devices, passed_along(): return lax.ppermute(value, axis, pairs)  35.3 us
    ppermute x12, waiting for transfers between devices, passed_along(): return lax.ppermute(value, axis, pairs)  31 us
    pallas_call x3, Pallas kernels, block_product(): pl.pallas_call(functools.partial(product_kernel, stored, rows, mode, len(...  21.4 us
    all_to_all x1, starting transfers between devices, gathered_copies(): return lax.all_to_all(repeated, axis, 0, 0, tiled=True)  11.1 us
    all_to_all x1, waiting for transfers between devices, gathered_copies(): return lax.all_to_all(repeated, axis, 0, 0, tiled=True)  8.27 us
    all_to_all x1, starting transfers between devices, body(): partial = lax.all_to_all(partial, 'col', 0, 0, tiled=True)  5.42 us
    all_to_all x1, waiting for transfers between devices, body(): partial = lax.all_to_all(partial, 'col', 0, 0, tiled=True)  4.94 us
    unnamed x38, local copies, waits for them, and re-layouts  4.1 us
  transfers between devices with their start and end apart: 14, of which 9 were waited for; matrix products, arithmetic and copies ran while one was open for 11% of the time, Pallas kernels for 0%

profile of v4, /device:TPU:1, one launch (start us, length us, event | category | flops | bytes accessed | tf_op | source)
XLA Modules:
  0.0 150.2 jit_solution(17714807558589166044)
XLA Ops:
  1.6 2.9 %multiply_add_fusion.2 = (f32[1,1,12,1,64,128]{5,4,3,2,1,0:T(8,128)S(1)}, f32[1,1,12,1,64,128]{5,4,3,2,1,0:T(8,128)S(1)}, f32[1,1,12,1,64,128]{5,4,3,2,1,0:T(8,128)S(1)}) fusion(f32[1,1,12,3,64,128]{5,4,3,2,1,0:T(8,128)} %bitcast.127, f32[12,64]{1,0:T(8,128)S(1)} %get-tuple-element.42, f32[12,64]{1,0:T(8,128)S(1)} %get-tuple-element.43, ...), kind=kLoop, calls=%fused_computation.26 | loop fusion | flops 1474560 | bytes 2386944 | tf_op jit(solution)/shard_map/add | solution.py:30
  5.9 3.1 %collective-permute-start.2 = (bf16[768,128]{1,0:T(8,128)(2,1)S(1)}, bf16[768,128]{1,0:T(8,128)(2,1)S(1)}, u32[]{:S(2)}, u32[]{:S(2)}) collective-permute-start(bf16[768,128]{1,0:T(8,128)(2,1)S(1)} %bitcast.141), channel_id=1, source_target_pairs={{0,1},{1,2},{2,3},{3,4},{4,5},{5,6},{6,7},{7,0},{8,9},{9,10},{10,1... | collective-permute-start | bytes 589832 | tf_op jit(solution)/shard_map/ppermute | solution.py:16
  9.3 10.4 %collective-permute-start.1 = (bf16[768,128]{1,0:T(8,128)(2,1)S(1)}, bf16[768,128]{1,0:T(8,128)(2,1)S(1)}, u32[]{:S(2)}, u32[]{:S(2)}) collective-permute-start(bf16[768,128]{1,0:T(8,128)(2,1)S(1)} %bitcast.139), channel_id=1, source_target_pairs={{0,248},{8,0},{16,8},{24,16},{32,24},{40,32},{48,40},{56,48},{64,5... | collective-permute-start | bytes 589832 | tf_op jit(solution)/shard_map/ppermute | solution.py:16
  26.6 12.0 %collective-permute-done.rest_0_ = bf16[768,128]{1,0:T(8,128)(2,1)S(1)} collective-permute-done((bf16[768,128]{1,0:T(8,128)(2,1)S(1)}, bf16[768,128]{1,0:T(8,128)(2,1)S(1)}, u32[]{:S(2)}, u32[]{:S(2)}) %collective-permute-start) | collective-permute-done | bytes 196640 | tf_op jit(solution)/shard_map/ppermute | solution.py:16
  38.6 2.0 %broadcast_in_dim.32.rest_4_ = bf16[12,3,3,64,128]{4,3,2,1,0:T(8,128)(2,1)} broadcast(bf16[12,3,3,64]{3,2,1,0:T(4,128)(2,1)S(1)} %bitcast.142), dimensions={0,1,2,3} | broadcast | bytes 1783296 | tf_op jit(solution)/shard_map/broadcast_in_dim | solution.py:176
  40.6 7.7 %shard_map.82 = (f32[12,192,128]{2,1,0:T(8,128)}, f32[12,192,128]{2,1,0:T(8,128)}, bf16[12,192,128]{2,1,0:T(8,128)(2,1)}) custom-call(s32[96]{0:T(128)} %reshape_squeeze.15.columns_ref, bf16[12,192,1536]{2,1,0:T(8,128)(2,1)} %bitcast.122, f32[12,192,128]{2,1,0:T(8,128)} %bitcast.128, bf16[12,192,128]{2,1,0:T(8,128)(2,1)} %copy-done.1, ...), custom_call_target="tpu_custom_call" | custom-call | flops 905969664 | bytes 15925248 | tf_op jit(solution)/shard_map/pallas_call | solution.py:118
  48.3 1.8 %gather_fusion.1 = bf16[16,192,128]{2,1,0:T(8,128)(2,1)S(1)} fusion(bf16[12,192,128]{2,1,0:T(8,128)(2,1)} %get-tuple-element.12.local_ref, s32[1024]{0:T(1024)S(1)} %pad_clamp_fusion.4), kind=kCustom, calls=%fused_computation.3.clone | custom fusion | bytes 1572928 | tf_op jit(solution)/shard_map/jit(_take)/gather | solution.py:164
  50.4 9.7 %collective-permute-start.5 = (bf16[912,128]{1,0:T(8,128)(2,1)S(1)}, bf16[912,128]{1,0:T(8,128)(2,1)S(1)}, u32[]{:S(2)}, u32[]{:S(2)}) collective-permute-start(bf16[912,128]{1,0:T(8,128)(2,1)S(1)} %pad_maximum_fusion.1), channel_id=1, source_target_pairs={{0,248},{8,0},{16,8},{24,16},{32,24},{40,32},{48,40},{56,48},{64,5... | collective-permute-start | bytes 700424 | tf_op jit(solution)/shard_map/ppermute | solution.py:16
  60.1 4.7 %collective-permute-start.6 = (bf16[912,128]{1,0:T(8,128)(2,1)S(1)}, bf16[912,128]{1,0:T(8,128)(2,1)S(1)}, u32[]{:S(2)}, u32[]{:S(2)}) collective-permute-start(bf16[912,128]{1,0:T(8,128)(2,1)S(1)} %pad_maximum_fusion.2), channel_id=1, source_target_pairs={{0,1},{1,2},{2,3},{3,4},{4,5},{5,6},{6,7},{7,0},{8,9},{9,10},{10,1... | collective-permute-start | bytes 700424 | tf_op jit(solution)/shard_map/ppermute | solution.py:16
  64.9 1.0 collective-permute-done.4.rest_0_
  65.9 1.0 collective-permute-done.5.rest_1_
  66.9 9.1 %collective-permute-done.6.rest_2_ = bf16[912,128]{1,0:T(8,128)(2,1)S(1)} collective-permute-done((bf16[912,128]{1,0:T(8,128)(2,1)S(1)}, bf16[912,128]{1,0:T(8,128)(2,1)S(1)}, u32[]{:S(2)}, u32[]{:S(2)}) %collective-permute-start.6) | collective-permute-done | bytes 233504 | tf_op jit(solution)/shard_map/ppermute | solution.py:16
  76.0 4.1 %collective-permute-done.7.rest_3_ = bf16[912,128]{1,0:T(8,128)(2,1)S(1)} collective-permute-done((bf16[912,128]{1,0:T(8,128)(2,1)S(1)}, bf16[912,128]{1,0:T(8,128)(2,1)S(1)}, u32[]{:S(2)}, u32[]{:S(2)}) %collective-permute-start.7) | collective-permute-done | bytes 233504 | tf_op jit(solution)/shard_map/ppermute | solution.py:16
  80.8 6.5 %shard_map.83.prev_ref = f32[12,192,128]{2,1,0:T(8,128)} custom-call(s32[96]{0:T(128)} %reshape_squeeze.15.columns_ref, bf16[12,192,1536]{2,1,0:T(8,128)(2,1)} %bitcast.123, f32[12,192,128]{2,1,0:T(8,128)} %get-tuple-element.11.prev_ref, bf16[12,192,128]{2,1,0:T(8,128)(2,1)} %get-tuple-element.12.local_ref, bf16[912,128]{1,0:T(8,128)(2,1)} %copy-done.5, ...), custom_call_target="tpu_custom_call" | custom-call | flops 905969664 | bytes 11206656 | tf_op jit(solution)/shard_map/pallas_call | solution.py:118
  87.2 1.5 %convolution_bitcast_fusion.1 = f32[12,6,128]{2,1,0:T(8,128)S(1)} fusion(f32[12,192,128]{2,1,0:T(8,128)} %shard_map.83.prev_ref, bf16[6,12,192]{2,1,0:T(8,128)(2,1)S(1)} %reshape_squeeze.18), kind=kOutput, calls=%fused_computation.18 | convolution fusion | flops 3833856 | bytes 1244160 | tf_op jit(solution)/shard_map/knd,ndr->nkr/dot_general | solution.py:200
  89.8 11.1 %all-to-all-start = ((bf16[32,24,128]{2,1,0:T(8,128)(2,1)}), bf16[32,24,128]{2,1,0:T(8,128)(2,1)}, u32[]{:S(2)}, u32[]{:S(2)}) async-start(bf16[32,24,128]{2,1,0:T(8,128)(2,1)} %broadcast_in_dim.34), calls=%async_computation | async-start | bytes 393216 | tf_op jit(solution)/shard_map/all_to_all | solution.py:130
  100.9 3.0 %copy.30 = bf16[192,6144]{0,1:T(8,128)(2,1)S(1)} copy(bf16[192,6144]{1,0:T(8,128)(2,1)} %param.21) | data formatting | bytes 4718592 | tf_op args[7]
  104.0 1.1 reshape.315
  105.2 8.3 %all-to-all-done = bf16[32,24,128]{2,1,0:T(8,128)(2,1)} async-done(((bf16[32,24,128]{2,1,0:T(8,128)(2,1)}), bf16[32,24,128]{2,1,0:T(8,128)(2,1)}, u32[]{:S(2)}, u32[]{:S(2)}) %all-to-all-start) | async-done | bytes 196640 | tf_op jit(solution)/shard_map/all_to_all | solution.py:130
  113.4 2.2 %fusion = f32[8,24,128]{2,1,0:T(8,128)} fusion(bf16[768,128,1]{1,0,2:T(8,128)(2,1)} %bitcast.48, bf16[8,24,768]{1,0,2:T(8,128)(2,1)S(1)} %reshape.315), kind=kOutput, calls=%fused_computation.10 | convolution fusion | flops 37748736 | bytes 589824 | tf_op jit(solution)/shard_map/dot_general | solution.py:214
  115.6 5.4 %all-to-all-start.1 = ((f32[8,24,128]{2,1,0:T(8,128)}), f32[8,24,128]{2,1,0:T(8,128)S(1)}, u32[]{:S(2)}, u32[]{:S(2)}) async-start(f32[8,24,128]{2,1,0:T(8,128)} %fusion), calls=%async_computation.1 | async-start | bytes 196608 | tf_op jit(solution)/shard_map/all_to_all | solution.py:215
  121.4 4.9 %all-to-all-done.1 = f32[8,24,128]{2,1,0:T(8,128)S(1)} async-done(((f32[8,24,128]{2,1,0:T(8,128)}), f32[8,24,128]{2,1,0:T(8,128)S(1)}, u32[]{:S(2)}, u32[]{:S(2)}) %all-to-all-start.1) | async-done | bytes 98336 | tf_op jit(solution)/shard_map/all_to_all | solution.py:215
  126.4 1.5 collective-permute-start.10
  127.9 1.6 %collective-permute-start.9 = (bf16[24,128]{1,0:T(8,128)(2,1)S(1)}, bf16[24,128]{1,0:T(8,128)(2,1)S(1)}, u32[]{:S(2)}, u32[]{:S(2)}) collective-permute-start(bf16[24,128]{1,0:T(8,128)(2,1)S(1)} %reduce_sum.9), channel_id=1, source_target_pairs={{0,248},{8,0},{16,8},{24,16},{32,24},{40,32},{48,40},{56,48},{64,5... | collective-permute-start | bytes 18440 | tf_op jit(solution)/shard_map/ppermute | solution.py:16
  129.5 3.7 %collective-permute-start.8 = (bf16[24,128]{1,0:T(8,128)(2,1)S(1)}, bf16[24,128]{1,0:T(8,128)(2,1)S(1)}, u32[]{:S(2)}, u32[]{:S(2)}) collective-permute-start(bf16[24,128]{1,0:T(8,128)(2,1)S(1)} %reduce_sum.9), channel_id=1, source_target_pairs={{0,8},{8,16},{16,24},{24,32},{32,40},{40,48},{48,56},{56,64},{64,7... | collective-permute-start | bytes 18440 | tf_op jit(solution)/shard_map/ppermute | solution.py:16
  134.0 1.4 fusion.23
  136.3 0.9 convolution_convert_fusion
  137.2 2.9 %collective-permute-done.8 = bf16[24,128]{1,0:T(8,128)(2,1)S(1)} collective-permute-done((bf16[24,128]{1,0:T(8,128)(2,1)S(1)}, bf16[24,128]{1,0:T(8,128)(2,1)S(1)}, u32[]{:S(2)}, u32[]{:S(2)}) %collective-permute-start.8) | collective-permute-done | bytes 6176 | tf_op jit(solution)/shard_map/ppermute | solution.py:16
  140.1 1.0 convolution_convert_fusion.3
  141.1 0.9 convolution_convert_fusion.2
  142.0 0.9 convolution_convert_fusion.1
  143.0 7.2 %shard_map.84 = f32[12,192,128]{2,1,0:T(8,128)} custom-call(s32[96]{0:T(128)} %reshape_squeeze.15.columns_ref, bf16[12,192,1536]{2,1,0:T(8,128)(2,1)} %bitcast.124, f32[12,192,128]{2,1,0:T(8,128)} %shard_map.83.prev_ref, bf16[12,192,128]{2,1,0:T(8,128)(2,1)} %get-tuple-element.23.local_ref, bf16[768,128]{1,0:T(8,128)(2,1)} %bitcast.135, ...), custom_call_target="tpu_custom_call" | custom-call | flops 905969664 | bytes 15925248 | tf_op jit(solution)/shard_map/pallas_call | solution.py:118
  (117 shorter events, 14.2 us)
Async XLA Ops:
  5.9 13.8 %copy-start.15 = (s32[1,1,4,4]{3,2,1,0:T(4,128)S(1)}, s32[1,1,4,4]{3,2,1,0:T(4,128)}, u32[]{:S(2)}) copy-start(s32[1,1,4,4]{3,2,1,0:T(4,128)} %param.18) | copy-start | bytes 196
  5.9 13.9 %copy-start.13 = (bf16[1,1,3,3,768]{4,3,2,1,0:T(4,128)(2,1)S(1)}, bf16[1,1,3,3,768]{4,3,2,1,0:T(4,128)(2,1)}, u32[]{:S(2)}) copy-start(bf16[1,1,3,3,768]{4,3,2,1,0:T(4,128)(2,1)} %param.15) | copy-start | bytes 41476
  5.9 14.0 %copy-start.17 = (s32[1,1,12]{2,1,0:T(1,128)S(1)}, s32[1,1,12]{2,1,0:T(1,128)}, u32[]{:S(2)}) copy-start(s32[1,1,12]{2,1,0:T(1,128)} %param.19) | copy-start | bytes 148
  5.9 15.2 %copy-start.14 = (bf16[1,1,6,2304]{3,2,1,0:T(8,128)(2,1)S(1)}, bf16[1,1,6,2304]{3,2,1,0:T(8,128)(2,1)}, u32[]{:S(2)}) copy-start(bf16[1,1,6,2304]{3,2,1,0:T(8,128)(2,1)} %param.20) | copy-start | bytes 82948
  5.9 18.7 %copy-start.16 = (s32[1,1,12,8]{2,3,1,0:T(8,128)S(1)}, s32[1,1,12,8]{2,3,1,0:T(8,128)}, u32[]{:S(2)}) copy-start(s32[1,1,12,8]{2,3,1,0:T(8,128)} %param.17) | copy-start | bytes 1156
  5.9 20.6 %collective-permute-start.2 = (bf16[768,128]{1,0:T(8,128)(2,1)S(1)}, bf16[768,128]{1,0:T(8,128)(2,1)S(1)}, u32[]{:S(2)}, u32[]{:S(2)}) collective-permute-start(bf16[768,128]{1,0:T(8,128)(2,1)S(1)} %bitcast.141), channel_id=1, source_target_pairs={{0,1},{1,2},{2,3},{3,4},{4,5},{5,6},{6,7},{7,0},{8,9},{9,10},{10,1... | collective-permute-start | bytes 589832 | tf_op jit(solution)/shard_map/ppermute | solution.py:16
  9.0 17.5 %collective-permute-start.3 = (bf16[768,128]{1,0:T(8,128)(2,1)S(1)}, bf16[768,128]{1,0:T(8,128)(2,1)S(1)}, u32[]{:S(2)}, u32[]{:S(2)}) collective-permute-start(bf16[768,128]{1,0:T(8,128)(2,1)S(1)} %bitcast.140), channel_id=1, source_target_pairs={{0,7},{1,0},{2,1},{3,2},{4,3},{5,4},{6,5},{7,6},{8,15},{9,8},{10,9... | collective-permute-start | bytes 589832 | tf_op jit(solution)/shard_map/ppermute | solution.py:16
  9.3 17.2 %collective-permute-start.1 = (bf16[768,128]{1,0:T(8,128)(2,1)S(1)}, bf16[768,128]{1,0:T(8,128)(2,1)S(1)}, u32[]{:S(2)}, u32[]{:S(2)}) collective-permute-start(bf16[768,128]{1,0:T(8,128)(2,1)S(1)} %bitcast.139), channel_id=1, source_target_pairs={{0,248},{8,0},{16,8},{24,16},{32,24},{40,32},{48,40},{56,48},{64,5... | collective-permute-start | bytes 589832 | tf_op jit(solution)/shard_map/ppermute | solution.py:16
  19.7 18.9 %collective-permute-start = (bf16[768,128]{1,0:T(8,128)(2,1)S(1)}, bf16[768,128]{1,0:T(8,128)(2,1)S(1)}, u32[]{:S(2)}, u32[]{:S(2)}) collective-permute-start(bf16[768,128]{1,0:T(8,128)(2,1)S(1)} %bitcast.138), channel_id=1, source_target_pairs={{0,8},{8,16},{16,24},{24,32},{32,40},{40,48},{48,56},{56,64},{64,7... | collective-permute-start | bytes 589832 | tf_op jit(solution)/shard_map/ppermute | solution.py:16
  21.2 66.1 %copy-start.3 = (bf16[6,12,192]{2,1,0:T(8,128)(2,1)}, bf16[6,12,192]{2,1,0:T(8,128)(2,1)S(1)}, u32[]{:S(2)}) copy-start(bf16[6,12,192]{2,1,0:T(8,128)(2,1)S(1)} %reshape_squeeze.18) | copy-start | bytes 82948
  26.5 14.0 %copy-start.9 = (bf16[768,128]{1,0:T(8,128)(2,1)}, bf16[768,128]{1,0:T(8,128)(2,1)S(1)}, u32[]{:S(2)}) copy-start(bf16[768,128]{1,0:T(8,128)(2,1)S(1)} %collective-permute-done.2.rest_2_) | copy-start | bytes 589828
  26.5 14.0 %copy-start.10 = (bf16[768,128]{1,0:T(8,128)(2,1)}, bf16[768,128]{1,0:T(8,128)(2,1)S(1)}, u32[]{:S(2)}) copy-start(bf16[768,128]{1,0:T(8,128)(2,1)S(1)} %collective-permute-done.3.rest_3_) | copy-start | bytes 589828
  26.6 14.0 %copy-start.11 = (bf16[768,128]{1,0:T(8,128)(2,1)}, bf16[768,128]{1,0:T(8,128)(2,1)S(1)}, u32[]{:S(2)}) copy-start(bf16[768,128]{1,0:T(8,128)(2,1)S(1)} %collective-permute-done.1.rest_1_) | copy-start | bytes 589828
  50.3 15.6 %collective-permute-start.4 = (bf16[912,128]{1,0:T(8,128)(2,1)S(1)}, bf16[912,128]{1,0:T(8,128)(2,1)S(1)}, u32[]{:S(2)}, u32[]{:S(2)}) collective-permute-start(bf16[912,128]{1,0:T(8,128)(2,1)S(1)} %pad_maximum_fusion), channel_id=1, source_target_pairs={{0,8},{8,16},{16,24},{24,32},{32,40},{40,48},{48,56},{56,64},{64,7... | collective-permute-start | bytes 700424 | tf_op jit(solution)/shard_map/ppermute | solution.py:16
  50.4 16.5 %collective-permute-start.5 = (bf16[912,128]{1,0:T(8,128)(2,1)S(1)}, bf16[912,128]{1,0:T(8,128)(2,1)S(1)}, u32[]{:S(2)}, u32[]{:S(2)}) collective-permute-start(bf16[912,128]{1,0:T(8,128)(2,1)S(1)} %pad_maximum_fusion.1), channel_id=1, source_target_pairs={{0,248},{8,0},{16,8},{24,16},{32,24},{40,32},{48,40},{56,48},{64,5... | collective-permute-start | bytes 700424 | tf_op jit(solution)/shard_map/ppermute | solution.py:16
  60.1 15.9 %collective-permute-start.6 = (bf16[912,128]{1,0:T(8,128)(2,1)S(1)}, bf16[912,128]{1,0:T(8,128)(2,1)S(1)}, u32[]{:S(2)}, u32[]{:S(2)}) collective-permute-start(bf16[912,128]{1,0:T(8,128)(2,1)S(1)} %pad_maximum_fusion.2), channel_id=1, source_target_pairs={{0,1},{1,2},{2,3},{3,4},{4,5},{5,6},{6,7},{7,0},{8,9},{9,10},{10,1... | collective-permute-start | bytes 700424 | tf_op jit(solution)/shard_map/ppermute | solution.py:16
  64.8 15.3 %collective-permute-start.7 = (bf16[912,128]{1,0:T(8,128)(2,1)S(1)}, bf16[912,128]{1,0:T(8,128)(2,1)S(1)}, u32[]{:S(2)}, u32[]{:S(2)}) collective-permute-start(bf16[912,128]{1,0:T(8,128)(2,1)S(1)} %pad_maximum_fusion.3), channel_id=1, source_target_pairs={{0,7},{1,0},{2,1},{3,2},{4,3},{5,4},{6,5},{7,6},{8,15},{9,8},{10,9... | collective-permute-start | bytes 700424 | tf_op jit(solution)/shard_map/ppermute | solution.py:16
  65.9 14.2 %copy-start.5 = (bf16[912,128]{1,0:T(8,128)(2,1)}, bf16[912,128]{1,0:T(8,128)(2,1)S(1)}, u32[]{:S(2)}) copy-start(bf16[912,128]{1,0:T(8,128)(2,1)S(1)} %collective-permute-done.4.rest_0_) | copy-start | bytes 700420
  66.9 13.2 %copy-start.6 = (bf16[912,128]{1,0:T(8,128)(2,1)}, bf16[912,128]{1,0:T(8,128)(2,1)S(1)}, u32[]{:S(2)}) copy-start(bf16[912,128]{1,0:T(8,128)(2,1)S(1)} %collective-permute-done.5.rest_1_) | copy-start | bytes 700420
  75.9 4.1 %copy-start.7 = (bf16[912,128]{1,0:T(8,128)(2,1)}, bf16[912,128]{1,0:T(8,128)(2,1)S(1)}, u32[]{:S(2)}) copy-start(bf16[912,128]{1,0:T(8,128)(2,1)S(1)} %collective-permute-done.6.rest_2_) | copy-start | bytes 700420
  89.8 23.6 %all-to-all-start = ((bf16[32,24,128]{2,1,0:T(8,128)(2,1)}), bf16[32,24,128]{2,1,0:T(8,128)(2,1)}, u32[]{:S(2)}, u32[]{:S(2)}) async-start(bf16[32,24,128]{2,1,0:T(8,128)(2,1)} %broadcast_in_dim.34), calls=%async_computation | async-start | bytes 393216 | tf_op jit(solution)/shard_map/all_to_all | solution.py:130
  105.1 15.9 %slice-start = ((bf16[912,128]{1,0:T(8,128)(2,1)}), bf16[144,128]{1,0:T(8,128)(2,1)S(1)}, s32[]{:S(2)}) async-start(bf16[912,128]{1,0:T(8,128)(2,1)} %copy-done.5), calls=%async_computation.2 | async-start | bytes 73728 | tf_op jit(solution)/shard_map/slice | solution.py:197
  113.4 7.7 %slice-start.1 = ((bf16[912,128]{1,0:T(8,128)(2,1)}), bf16[144,128]{1,0:T(8,128)(2,1)S(1)}, s32[]{:S(2)}) async-start(bf16[912,128]{1,0:T(8,128)(2,1)} %copy-done.6), calls=%async_computation.3 | async-start | bytes 73728 | tf_op jit(solution)/shard_map/slice | solution.py:197
  113.4 7.8 %slice-start.2 = ((bf16[912,128]{1,0:T(8,128)(2,1)}), bf16[144,128]{1,0:T(8,128)(2,1)S(1)}, s32[]{:S(2)}) async-start(bf16[912,128]{1,0:T(8,128)(2,1)} %copy-done.7), calls=%async_computation.4 | async-start | bytes 73728 | tf_op jit(solution)/shard_map/slice | solution.py:197
  113.4 7.9 %slice-start.3 = ((bf16[912,128]{1,0:T(8,128)(2,1)}), bf16[144,128]{1,0:T(8,128)(2,1)S(1)}, s32[]{:S(2)}) async-start(bf16[912,128]{1,0:T(8,128)(2,1)} %copy-done.8), calls=%async_computation.5 | async-start | bytes 73728 | tf_op jit(solution)/shard_map/slice | solution.py:197
  113.4 20.2 %copy-start.4 = (bf16[6,12,192]{2,1,0:T(8,128)(2,1)S(1)}, bf16[6,12,192]{2,1,0:T(8,128)(2,1)}, u32[]{:S(2)}) copy-start(bf16[6,12,192]{2,1,0:T(8,128)(2,1)} %copy-done.3) | copy-start | bytes 82948
  115.6 18.4 %copy-start.2 = (f32[12,192,128]{2,1,0:T(8,128)S(1)}, f32[12,192,128]{2,1,0:T(8,128)}, u32[]{:S(2)}) copy-start(f32[12,192,128]{2,1,0:T(8,128)} %get-tuple-element.13) | copy-start | bytes 3538948
  115.6 10.8 %all-to-all-start.1 = ((f32[8,24,128]{2,1,0:T(8,128)}), f32[8,24,128]{2,1,0:T(8,128)S(1)}, u32[]{:S(2)}, u32[]{:S(2)}) async-start(f32[8,24,128]{2,1,0:T(8,128)} %fusion), calls=%async_computation.1 | async-start | bytes 196608 | tf_op jit(solution)/shard_map/all_to_all | solution.py:215
  126.4 15.6 %collective-permute-start.10 = (bf16[24,128]{1,0:T(8,128)(2,1)S(1)}, bf16[24,128]{1,0:T(8,128)(2,1)S(1)}, u32[]{:S(2)}, u32[]{:S(2)}) collective-permute-start(bf16[24,128]{1,0:T(8,128)(2,1)S(1)} %reduce_sum.9), channel_id=1, source_target_pairs={{0,1},{1,2},{2,3},{3,4},{4,5},{5,6},{6,7},{7,0},{8,9},{9,10},{10,1... | collective-permute-start | bytes 18440 | tf_op jit(solution)/shard_map/ppermute | solution.py:16
  127.9 13.2 %collective-permute-start.9 = (bf16[24,128]{1,0:T(8,128)(2,1)S(1)}, bf16[24,128]{1,0:T(8,128)(2,1)S(1)}, u32[]{:S(2)}, u32[]{:S(2)}) collective-permute-start(bf16[24,128]{1,0:T(8,128)(2,1)S(1)} %reduce_sum.9), channel_id=1, source_target_pairs={{0,248},{8,0},{16,8},{24,16},{32,24},{40,32},{48,40},{56,48},{64,5... | collective-permute-start | bytes 18440 | tf_op jit(solution)/shard_map/ppermute | solution.py:16
  129.5 10.6 %collective-permute-start.8 = (bf16[24,128]{1,0:T(8,128)(2,1)S(1)}, bf16[24,128]{1,0:T(8,128)(2,1)S(1)}, u32[]{:S(2)}, u32[]{:S(2)}) collective-permute-start(bf16[24,128]{1,0:T(8,128)(2,1)S(1)} %reduce_sum.9), channel_id=1, source_target_pairs={{0,8},{8,16},{16,24},{24,32},{32,40},{40,48},{48,56},{56,64},{64,7... | collective-permute-start | bytes 18440 | tf_op jit(solution)/shard_map/ppermute | solution.py:16
  133.2 3.1 %collective-permute-start.11 = (bf16[24,128]{1,0:T(8,128)(2,1)S(1)}, bf16[24,128]{1,0:T(8,128)(2,1)S(1)}, u32[]{:S(2)}, u32[]{:S(2)}) collective-permute-start(bf16[24,128]{1,0:T(8,128)(2,1)S(1)} %reduce_sum.9), channel_id=1, source_target_pairs={{0,7},{1,0},{2,1},{3,2},{4,3},{5,4},{6,5},{7,6},{8,15},{9,8},{10,9... | collective-permute-start | bytes 18440 | tf_op jit(solution)/shard_map/ppermute | solution.py:16
  (4 other events, 4.8 us)

commit v5 on v4

--- a/solution.py
+++ b/solution.py
@@ -6,6 +6,7 @@
 from jax.experimental import pallas as pl
 from jax.experimental.pallas import tpu as pltpu
 from jax.sharding import PartitionSpec as P
+
 
 damping = 0.6
 
@@ -139,7 +140,7 @@
     ]
 
 
-def body(rhs, smoother, blocks, col_index, send_list, agg_id, prolong, coarse_inverse):
+def cycle(rhs, smoother, blocks, col_index, send_list, agg_id, prolong, coarse_inverse):
     block_count = rhs.shape[2]
     dof_count = rhs.shape[3]
     vectors = rhs.shape[4]
@@ -172,7 +173,9 @@
         ]
 
     grains = dof_count // 3
-    factors = jnp.transpose(smoother[0, 0].reshape((3, 3, block_count, grains)), (2, 0, 1, 3))
+    factors = jnp.transpose(
+        smoother[0, 0].reshape((3, 3, block_count, grains)), (2, 0, 1, 3)
+    )
     factors = jnp.broadcast_to(factors[..., None], factors.shape + (vectors,))
 
     tables = []
@@ -182,10 +185,19 @@
         table = member.T[:, :, None, None] * jnp.transpose(picked, (1, 0, 2))[:, None, :, :]
         tables.append(table.reshape((ghost_count * coarse_rows * dof_count) // vectors, vectors))
 
+    sent = send_rows.reshape(-1)
+    sent_rhs = jnp.take(rhs, sent, axis=2)
+    sent_factors = jnp.take(
+        smoother.reshape(smoother.shape[:4] + (block_count, grains)), sent, axis=4
+    ).reshape(smoother.shape[:4] + (sent.shape[0] * grains,))
+    sent_low = point_smooth(sent_factors, sent_rhs).astype(jnp.bfloat16)[0, 0]
+    sent_low = sent_low.reshape((groups * ghost_rows, vectors))
+    parts = [sent_low[g * ghost_rows:(g + 1) * ghost_rows] for g in range(groups)]
+    first_ghosts = exchange(parts)
     first_iter = point_smooth(smoother, rhs)
-    shard_low, parts = outgoing(first_iter)
+    shard_low = first_iter.astype(jnp.bfloat16)[0, 0]
     residual_first, second_iter, update_low = block_product(
-        local_blocks, columns, rhs[0, 0], shard_low, exchange(parts), ghost_count,
+        local_blocks, columns, rhs[0, 0], shard_low, first_ghosts, ghost_count,
         mode="smooth", factors=factors, base=first_iter[0, 0],
     )
     residual_first = residual_first[None, None]
@@ -256,7 +268,7 @@
         P("row", None),
     )
     return jax.shard_map(
-        body,
+        cycle,
         mesh=mesh,
         in_specs=placed,
         out_specs=P("row", "col", None, None, None),

time: 151 us -> 151 us (level)
  local copies, waits for them, and re-layouts: 18.4 us -> 22.3 us
  waiting for transfers between devices: 44.2 us -> 40.6 us
    gather x8 -> x10, local copies, waits for them, and re-layouts: 4.44 us -> 6.98 us  [the longest x4 2.25 us: cycle(): member = jnp.take(onehot, send_rows[g], axis=1).astype(jnp.bfloat16)]
    ppermute x12, waiting for transfers between devices: 31 us -> 28.7 us  [passed_along(): return lax.ppermute(value, axis, pairs)]
    all_to_all x1, starting transfers between devices: 11.1 us -> 8.9 us  [gathered_copies(): return lax.all_to_all(repeated, axis, 0, 0, tiled=True)]
    all_to_all x1, starting transfers between devices: 5.42 us -> 7.38 us  [cycle(): partial = lax.all_to_all(partial, 'col', 0, 0, tiled=True)]
    unnamed x38 -> x34, local copies, waits for them, and re-layouts: 4.1 us -> 3.61 us
  transfers between devices with their start and end apart: 14 -> 14, of which waited for: 9 -> 8; matrix products, arithmetic and copies ran while one was open for 11% -> 13% of each run, Pallas kernels for 0% -> 0%
where the time goes in v5:
time: 151 us
  starting transfers between devices  51.7 us (34%)
  waiting for transfers between devices  40.6 us (27%)
  local copies, waits for them, and re-layouts  22.3 us (15%)
  Pallas kernels  21.5 us (14%)
  matrix products  7.33 us (5%)
  other arithmetic  6.88 us (5%)
    ppermute x12, starting transfers between devices, passed_along(): return lax.ppermute(value, axis, pairs)  35.4 us
    ppermute x12, waiting for transfers between devices, passed_along(): return lax.ppermute(value, axis, pairs)  28.7 us
    pallas_call x3, Pallas kernels, block_product(): pl.pallas_call(functools.partial(product_kernel, stored, rows, mode, len(...  21.5 us
    all_to_all x1, starting transfers between devices, gathered_copies(): return lax.all_to_all(repeated, axis, 0, 0, tiled=True)  8.9 us
    all_to_all x1, starting transfers between devices, cycle(): partial = lax.all_to_all(partial, 'col', 0, 0, tiled=True)  7.38 us
    all_to_all x1, waiting for transfers between devices, gathered_copies(): return lax.all_to_all(repeated, axis, 0, 0, tiled=True)  6.9 us
    all_to_all x1, waiting for transfers between devices, cycle(): partial = lax.all_to_all(partial, 'col', 0, 0, tiled=True)  4.97 us
    dot_general x4, matrix products, cycle(): jnp.einsum('bjd,jr->bdr', neighbour_tables[g], neighbour_coarse[g], prefe...  3.74 us
  transfers between devices with their start and end apart: 14, of which 8 were waited for; matrix products, arithmetic and copies ran while one was open for 13% of the time, Pallas kernels for 0%

profile of v5, /device:TPU:1, one launch (start us, length us, event | category | flops | bytes accessed | tf_op | source)
XLA Modules:
  0.0 150.9 jit_solution(6116254529442638048)
XLA Ops:
  3.2 1.9 %gather_fusion.1 = f32[16,192,128]{2,1,0:T(8,128)S(1)} fusion(f32[12,192,128]{2,1,0:T(8,128)} %bitcast.142, s32[1024]{0:T(1024)S(1)} %pad_clamp_fusion.4), kind=kCustom, calls=%fused_computation.9 | custom fusion | bytes 3145792 | tf_op jit(solution)/shard_map/jit(_take)/gather | solution.py:189
  5.3 1.6 %multiply_add_fusion.2 = (f32[1,1,16,1,64,128]{5,4,3,2,1,0:T(8,128)S(1)}, f32[1,1,16,1,64,128]{5,4,3,2,1,0:T(8,128)S(1)}, f32[1,1,16,1,64,128]{5,4,3,2,1,0:T(8,128)S(1)}) fusion(f32[1,1,16,3,64,128]{5,4,3,2,1,0:T(8,128)S(1)} %broadcast_select_fusion, f32[16,64]{1,0:T(8,128)S(1)} %bitcast.170, f32[16,64]{1,0:T(8,128)S(1)} %bitcast.171, ...), kind=kLoop, calls=%fused_computation.29 | loop fusion | flops 1966080 | bytes 3182592 | tf_op jit(solution)/shard_map/add | solution.py:31
  8.0 3.0 %collective-permute-start.2 = (bf16[768,128]{1,0:T(8,128)(2,1)}, bf16[768,128]{1,0:T(8,128)(2,1)}, u32[]{:S(2)}, u32[]{:S(2)}) collective-permute-start(bf16[768,128]{1,0:T(8,128)(2,1)} %bitcast.29), channel_id=1, source_target_pairs={{0,1},{1,2},{2,3},{3,4},{4,5},{5,6},{6,7},{7,0},{8,9},{9,10},{10,1... | collective-permute-start | bytes 589832 | tf_op jit(solution)/shard_map/ppermute | solution.py:17
  11.2 10.5 %collective-permute-start.1 = (bf16[768,128]{1,0:T(8,128)(2,1)S(1)}, bf16[768,128]{1,0:T(8,128)(2,1)}, u32[]{:S(2)}, u32[]{:S(2)}) collective-permute-start(bf16[768,128]{1,0:T(8,128)(2,1)S(1)} %bitcast.160), channel_id=1, source_target_pairs={{0,248},{8,0},{16,8},{24,16},{32,24},{40,32},{48,40},{56,48},{64,5... | collective-permute-start | bytes 589832 | tf_op jit(solution)/shard_map/ppermute | solution.py:17
  27.2 1.2 multiply_add_fusion.5
  29.9 1.1 convert_element_type.83.local_ref
  31.0 9.6 %collective-permute-done.rest_0_ = bf16[768,128]{1,0:T(8,128)(2,1)} collective-permute-done((bf16[768,128]{1,0:T(8,128)(2,1)S(1)}, bf16[768,128]{1,0:T(8,128)(2,1)}, u32[]{:S(2)}, u32[]{:S(2)}) %collective-permute-start) | collective-permute-done | bytes 196640 | tf_op jit(solution)/shard_map/ppermute | solution.py:17
  40.5 2.0 %broadcast_in_dim.76.rest_4_ = bf16[12,3,3,64,128]{4,3,2,1,0:T(8,128)(2,1)} broadcast(bf16[12,3,3,64]{3,2,1,0:T(4,128)(2,1)S(1)} %copy.26), dimensions={0,1,2,3} | broadcast | bytes 1783296 | tf_op jit(solution)/shard_map/broadcast_in_dim | solution.py:179
  42.5 7.7 %shard_map.82 = (f32[12,192,128]{2,1,0:T(8,128)}, f32[12,192,128]{2,1,0:T(8,128)}, bf16[12,192,128]{2,1,0:T(8,128)(2,1)}) custom-call(s32[96]{0:T(128)} %reshape_squeeze.18.columns_ref, bf16[12,192,1536]{2,1,0:T(8,128)(2,1)} %bitcast.139, f32[12,192,128]{2,1,0:T(8,128)} %bitcast.143, bf16[12,192,128]{2,1,0:T(8,128)(2,1)} %convert_element_type.83.local_ref, ...), custom_call_target="tpu_custom_call" | custom-call | flops 905969664 | bytes 15925248 | tf_op jit(solution)/shard_map/pallas_call | solution.py:119
  50.2 1.8 %gather_fusion.2 = bf16[16,192,128]{2,1,0:T(8,128)(2,1)S(1)} fusion(bf16[12,192,128]{2,1,0:T(8,128)(2,1)} %get-tuple-element.11.local_ref, s32[1024]{0:T(1024)S(1)} %pad_clamp_fusion.4), kind=kCustom, calls=%fused_computation.10 | custom fusion | bytes 1572928 | tf_op jit(solution)/shard_map/jit(_take)/gather | solution.py:165
  52.3 9.7 %collective-permute-start.5 = (bf16[912,128]{1,0:T(8,128)(2,1)S(1)}, bf16[912,128]{1,0:T(8,128)(2,1)S(1)}, u32[]{:S(2)}, u32[]{:S(2)}) collective-permute-start(bf16[912,128]{1,0:T(8,128)(2,1)S(1)} %pad_maximum_fusion.1), channel_id=1, source_target_pairs={{0,248},{8,0},{16,8},{24,16},{32,24},{40,32},{48,40},{56,48},{64,5... | collective-permute-start | bytes 700424 | tf_op jit(solution)/shard_map/ppermute | solution.py:17
  62.0 4.7 %collective-permute-start.6 = (bf16[912,128]{1,0:T(8,128)(2,1)S(1)}, bf16[912,128]{1,0:T(8,128)(2,1)S(1)}, u32[]{:S(2)}, u32[]{:S(2)}) collective-permute-start(bf16[912,128]{1,0:T(8,128)(2,1)S(1)} %pad_maximum_fusion.2), channel_id=1, source_target_pairs={{0,1},{1,2},{2,3},{3,4},{4,5},{5,6},{6,7},{7,0},{8,9},{9,10},{10,1... | collective-permute-start | bytes 700424 | tf_op jit(solution)/shard_map/ppermute | solution.py:17
  67.0 1.8 %collective-permute-done.5.rest_1_ = bf16[912,128]{1,0:T(8,128)(2,1)S(1)} collective-permute-done((bf16[912,128]{1,0:T(8,128)(2,1)S(1)}, bf16[912,128]{1,0:T(8,128)(2,1)S(1)}, u32[]{:S(2)}, u32[]{:S(2)}) %collective-permute-start.5) | collective-permute-done | bytes 233504 | tf_op jit(solution)/shard_map/ppermute | solution.py:17
  68.9 9.4 %collective-permute-done.6.rest_2_ = bf16[912,128]{1,0:T(8,128)(2,1)S(1)} collective-permute-done((bf16[912,128]{1,0:T(8,128)(2,1)S(1)}, bf16[912,128]{1,0:T(8,128)(2,1)S(1)}, u32[]{:S(2)}, u32[]{:S(2)}) %collective-permute-start.6) | collective-permute-done | bytes 233504 | tf_op jit(solution)/shard_map/ppermute | solution.py:17
  78.2 4.1 %collective-permute-done.7.rest_3_ = bf16[912,128]{1,0:T(8,128)(2,1)S(1)} collective-permute-done((bf16[912,128]{1,0:T(8,128)(2,1)S(1)}, bf16[912,128]{1,0:T(8,128)(2,1)S(1)}, u32[]{:S(2)}, u32[]{:S(2)}) %collective-permute-start.7) | collective-permute-done | bytes 233504 | tf_op jit(solution)/shard_map/ppermute | solution.py:17
  83.0 6.6 %shard_map.83.prev_ref = f32[12,192,128]{2,1,0:T(8,128)} custom-call(s32[96]{0:T(128)} %reshape_squeeze.18.columns_ref, bf16[12,192,1536]{2,1,0:T(8,128)(2,1)} %bitcast.140, f32[12,192,128]{2,1,0:T(8,128)} %get-tuple-element.10.prev_ref, bf16[12,192,128]{2,1,0:T(8,128)(2,1)} %get-tuple-element.11.local_ref, bf16[912,128]{1,0:T(8,128)(2,1)} %copy-done.7, ...), custom_call_target="tpu_custom_call" | custom-call | flops 905969664 | bytes 11206656 | tf_op jit(solution)/shard_map/pallas_call | solution.py:119
  89.6 1.5 %convolution_bitcast_fusion.1 = f32[12,6,128]{2,1,0:T(8,128)S(1)} fusion(f32[12,192,128]{2,1,0:T(8,128)} %shard_map.83.prev_ref, bf16[6,12,192]{2,1,0:T(8,128)(2,1)S(1)} %copy-done.5), kind=kOutput, calls=%fused_computation.21 | convolution fusion | flops 3833856 | bytes 1244160 | tf_op jit(solution)/shard_map/knd,ndr->nkr/dot_general | solution.py:212
  92.2 8.9 %all-to-all-start = ((bf16[32,24,128]{2,1,0:T(8,128)(2,1)}), bf16[32,24,128]{2,1,0:T(8,128)(2,1)S(1)}, u32[]{:S(2)}, u32[]{:S(2)}) async-start(bf16[32,24,128]{2,1,0:T(8,128)(2,1)} %broadcast_in_dim.80), calls=%async_computation | async-start | bytes 393216 | tf_op jit(solution)/shard_map/all_to_all | solution.py:131
  101.1 2.7 %copy.31 = bf16[192,6144]{0,1:T(8,128)(2,1)} copy(bf16[192,6144]{1,0:T(8,128)(2,1)S(1)} %copy-done.2) | data formatting | bytes 4718592 | tf_op args[7]
  103.9 1.0 constant_dynamic-slice_fusion
  104.9 1.1 reshape.473
  106.1 6.9 %all-to-all-done = bf16[32,24,128]{2,1,0:T(8,128)(2,1)S(1)} async-done(((bf16[32,24,128]{2,1,0:T(8,128)(2,1)}), bf16[32,24,128]{2,1,0:T(8,128)(2,1)S(1)}, u32[]{:S(2)}, u32[]{:S(2)}) %all-to-all-start) | async-done | bytes 196640 | tf_op jit(solution)/shard_map/all_to_all | solution.py:131
  113.0 1.2 fusion.1
  114.2 7.4 %all-to-all-start.1 = ((f32[8,24,128]{2,1,0:T(8,128)}), f32[8,24,128]{2,1,0:T(8,128)S(1)}, u32[]{:S(2)}, u32[]{:S(2)}) async-start(f32[8,24,128]{2,1,0:T(8,128)} %fusion.1), calls=%async_computation.1 | async-start | bytes 196608 | tf_op jit(solution)/shard_map/all_to_all | solution.py:227
  122.0 5.0 %all-to-all-done.1 = f32[8,24,128]{2,1,0:T(8,128)S(1)} async-done(((f32[8,24,128]{2,1,0:T(8,128)}), f32[8,24,128]{2,1,0:T(8,128)S(1)}, u32[]{:S(2)}, u32[]{:S(2)}) %all-to-all-start.1) | async-done | bytes 98336 | tf_op jit(solution)/shard_map/all_to_all | solution.py:227
  127.0 1.5 collective-permute-start.10
  128.5 1.8 %collective-permute-start.9 = (bf16[24,128]{1,0:T(8,128)(2,1)S(1)}, bf16[24,128]{1,0:T(8,128)(2,1)S(1)}, u32[]{:S(2)}, u32[]{:S(2)}) collective-permute-start(bf16[24,128]{1,0:T(8,128)(2,1)S(1)} %reduce_sum.9), channel_id=1, source_target_pairs={{0,248},{8,0},{16,8},{24,16},{32,24},{40,32},{48,40},{56,48},{64,5... | collective-permute-start | bytes 18440 | tf_op jit(solution)/shard_map/ppermute | solution.py:17
  130.3 3.6 %collective-permute-start.8 = (bf16[24,128]{1,0:T(8,128)(2,1)S(1)}, bf16[24,128]{1,0:T(8,128)(2,1)S(1)}, u32[]{:S(2)}, u32[]{:S(2)}) collective-permute-start(bf16[24,128]{1,0:T(8,128)(2,1)S(1)} %reduce_sum.9), channel_id=1, source_target_pairs={{0,8},{8,16},{16,24},{24,32},{32,40},{40,48},{48,56},{56,64},{64,7... | collective-permute-start | bytes 18440 | tf_op jit(solution)/shard_map/ppermute | solution.py:17
  134.7 1.4 fusion.26
  137.9 3.0 %collective-permute-done.8 = bf16[24,128]{1,0:T(8,128)(2,1)S(1)} collective-permute-done((bf16[24,128]{1,0:T(8,128)(2,1)S(1)}, bf16[24,128]{1,0:T(8,128)(2,1)S(1)}, u32[]{:S(2)}, u32[]{:S(2)}) %collective-permute-start.8) | collective-permute-done | bytes 6176 | tf_op jit(solution)/shard_map/ppermute | solution.py:17
  141.8 0.9 convolution_convert_fusion.2
  143.7 7.2 %shard_map.84 = f32[12,192,128]{2,1,0:T(8,128)} custom-call(s32[96]{0:T(128)} %reshape_squeeze.18.columns_ref, bf16[12,192,1536]{2,1,0:T(8,128)(2,1)} %bitcast.141, f32[12,192,128]{2,1,0:T(8,128)} %shard_map.83.prev_ref, bf16[12,192,128]{2,1,0:T(8,128)(2,1)} %get-tuple-element.25.local_ref, bf16[768,128]{1,0:T(8,128)(2,1)} %bitcast.155, ...), custom_call_target="tpu_custom_call" | custom-call | flops 905969664 | bytes 15925248 | tf_op jit(solution)/shard_map/pallas_call | solution.py:119
  (120 shorter events, 18.6 us)
Async XLA Ops:
  6.9 14.7 %copy-start.13 = (s32[1,1,4,4]{3,2,1,0:T(4,128)S(1)}, s32[1,1,4,4]{3,2,1,0:T(4,128)}, u32[]{:S(2)}) copy-start(s32[1,1,4,4]{3,2,1,0:T(4,128)} %param.16) | copy-start | bytes 196
  6.9 14.7 %copy-start.15 = (s32[1,1,12]{2,1,0:T(1,128)S(1)}, s32[1,1,12]{2,1,0:T(1,128)}, u32[]{:S(2)}) copy-start(s32[1,1,12]{2,1,0:T(1,128)} %param.17) | copy-start | bytes 148
  6.9 16.0 %copy-start.12 = (bf16[1,1,6,2304]{3,2,1,0:T(8,128)(2,1)S(1)}, bf16[1,1,6,2304]{3,2,1,0:T(8,128)(2,1)}, u32[]{:S(2)}) copy-start(bf16[1,1,6,2304]{3,2,1,0:T(8,128)(2,1)} %param.18) | copy-start | bytes 82948
  6.9 19.5 %copy-start.11 = (bf16[1,1,3,3,768]{4,3,2,1,0:T(4,128)(2,1)S(1)}, bf16[1,1,3,3,768]{4,3,2,1,0:T(4,128)(2,1)}, u32[]{:S(2)}) copy-start(bf16[1,1,3,3,768]{4,3,2,1,0:T(4,128)(2,1)} %param.13) | copy-start | bytes 41476
  7.2 20.0 %copy-start = (f32[1,1,12,192,128]{4,3,2,1,0:T(8,128)S(1)}, f32[1,1,12,192,128]{4,3,2,1,0:T(8,128)}, u32[]{:S(2)}) copy-start(f32[1,1,12,192,128]{4,3,2,1,0:T(8,128)} %param.12) | copy-start | bytes 3538948
  8.0 23.0 %collective-permute-start.2 = (bf16[768,128]{1,0:T(8,128)(2,1)}, bf16[768,128]{1,0:T(8,128)(2,1)}, u32[]{:S(2)}, u32[]{:S(2)}) collective-permute-start(bf16[768,128]{1,0:T(8,128)(2,1)} %bitcast.29), channel_id=1, source_target_pairs={{0,1},{1,2},{2,3},{3,4},{4,5},{5,6},{6,7},{7,0},{8,9},{9,10},{10,1... | collective-permute-start | bytes 589832 | tf_op jit(solution)/shard_map/ppermute | solution.py:17
  11.0 20.0 %collective-permute-start.3 = (bf16[768,128]{1,0:T(8,128)(2,1)S(1)}, bf16[768,128]{1,0:T(8,128)(2,1)}, u32[]{:S(2)}, u32[]{:S(2)}) collective-permute-start(bf16[768,128]{1,0:T(8,128)(2,1)S(1)} %bitcast.161), channel_id=1, source_target_pairs={{0,7},{1,0},{2,1},{3,2},{4,3},{5,4},{6,5},{7,6},{8,15},{9,8},{10,9... | collective-permute-start | bytes 589832 | tf_op jit(solution)/shard_map/ppermute | solution.py:17
  11.2 19.8 %collective-permute-start.1 = (bf16[768,128]{1,0:T(8,128)(2,1)S(1)}, bf16[768,128]{1,0:T(8,128)(2,1)}, u32[]{:S(2)}, u32[]{:S(2)}) collective-permute-start(bf16[768,128]{1,0:T(8,128)(2,1)S(1)} %bitcast.160), channel_id=1, source_target_pairs={{0,248},{8,0},{16,8},{24,16},{32,24},{40,32},{48,40},{56,48},{64,5... | collective-permute-start | bytes 589832 | tf_op jit(solution)/shard_map/ppermute | solution.py:17
  21.7 18.9 %collective-permute-start = (bf16[768,128]{1,0:T(8,128)(2,1)S(1)}, bf16[768,128]{1,0:T(8,128)(2,1)}, u32[]{:S(2)}, u32[]{:S(2)}) collective-permute-start(bf16[768,128]{1,0:T(8,128)(2,1)S(1)} %bitcast.159), channel_id=1, source_target_pairs={{0,8},{8,16},{16,24},{24,32},{32,40},{40,48},{48,56},{56,64},{64,7... | collective-permute-start | bytes 589832 | tf_op jit(solution)/shard_map/ppermute | solution.py:17
  23.0 4.1 %copy-start.4 = (bf16[6,12,192]{2,1,0:T(8,128)(2,1)}, bf16[6,12,192]{2,1,0:T(8,128)(2,1)S(1)}, u32[]{:S(2)}) copy-start(bf16[6,12,192]{2,1,0:T(8,128)(2,1)S(1)} %reshape_squeeze.22) | copy-start | bytes 82948
  29.9 12.7 %copy-start.1 = (f32[1,1,12,3,64,128]{5,4,3,2,1,0:T(8,128)}, f32[1,1,12,3,64,128]{5,4,3,2,1,0:T(8,128)S(1)}, u32[]{:S(2)}) copy-start(f32[1,1,12,3,64,128]{5,4,3,2,1,0:T(8,128)S(1)} %maximum_multiply_fusion.1) | copy-start | bytes 3538948
  52.2 14.8 %collective-permute-start.4 = (bf16[912,128]{1,0:T(8,128)(2,1)S(1)}, bf16[912,128]{1,0:T(8,128)(2,1)S(1)}, u32[]{:S(2)}, u32[]{:S(2)}) collective-permute-start(bf16[912,128]{1,0:T(8,128)(2,1)S(1)} %pad_maximum_fusion), channel_id=1, source_target_pairs={{0,8},{8,16},{16,24},{24,32},{32,40},{40,48},{48,56},{56,64},{64,7... | collective-permute-start | bytes 700424 | tf_op jit(solution)/shard_map/ppermute | solution.py:17
  52.3 16.5 %collective-permute-start.5 = (bf16[912,128]{1,0:T(8,128)(2,1)S(1)}, bf16[912,128]{1,0:T(8,128)(2,1)S(1)}, u32[]{:S(2)}, u32[]{:S(2)}) collective-permute-start(bf16[912,128]{1,0:T(8,128)(2,1)S(1)} %pad_maximum_fusion.1), channel_id=1, source_target_pairs={{0,248},{8,0},{16,8},{24,16},{32,24},{40,32},{48,40},{56,48},{64,5... | collective-permute-start | bytes 700424 | tf_op jit(solution)/shard_map/ppermute | solution.py:17
  62.0 16.2 %collective-permute-start.6 = (bf16[912,128]{1,0:T(8,128)(2,1)S(1)}, bf16[912,128]{1,0:T(8,128)(2,1)S(1)}, u32[]{:S(2)}, u32[]{:S(2)}) collective-permute-start(bf16[912,128]{1,0:T(8,128)(2,1)S(1)} %pad_maximum_fusion.2), channel_id=1, source_target_pairs={{0,1},{1,2},{2,3},{3,4},{4,5},{5,6},{6,7},{7,0},{8,9},{9,10},{10,1... | collective-permute-start | bytes 700424 | tf_op jit(solution)/shard_map/ppermute | solution.py:17
  66.7 15.6 %collective-permute-start.7 = (bf16[912,128]{1,0:T(8,128)(2,1)S(1)}, bf16[912,128]{1,0:T(8,128)(2,1)S(1)}, u32[]{:S(2)}, u32[]{:S(2)}) collective-permute-start(bf16[912,128]{1,0:T(8,128)(2,1)S(1)} %pad_maximum_fusion.3), channel_id=1, source_target_pairs={{0,7},{1,0},{2,1},{3,2},{4,3},{5,4},{6,5},{7,6},{8,15},{9,8},{10,9... | collective-permute-start | bytes 700424 | tf_op jit(solution)/shard_map/ppermute | solution.py:17
  67.0 15.3 %copy-start.7 = (bf16[912,128]{1,0:T(8,128)(2,1)}, bf16[912,128]{1,0:T(8,128)(2,1)S(1)}, u32[]{:S(2)}) copy-start(bf16[912,128]{1,0:T(8,128)(2,1)S(1)} %collective-permute-done.4.rest_0_) | copy-start | bytes 700420
  68.9 13.5 %copy-start.8 = (bf16[912,128]{1,0:T(8,128)(2,1)}, bf16[912,128]{1,0:T(8,128)(2,1)S(1)}, u32[]{:S(2)}) copy-start(bf16[912,128]{1,0:T(8,128)(2,1)S(1)} %collective-permute-done.5.rest_1_) | copy-start | bytes 700420
  78.2 4.1 %copy-start.9 = (bf16[912,128]{1,0:T(8,128)(2,1)}, bf16[912,128]{1,0:T(8,128)(2,1)S(1)}, u32[]{:S(2)}) copy-start(bf16[912,128]{1,0:T(8,128)(2,1)S(1)} %collective-permute-done.6.rest_2_) | copy-start | bytes 700420
  83.0 6.6 %copy-start.5 = (bf16[6,12,192]{2,1,0:T(8,128)(2,1)S(1)}, bf16[6,12,192]{2,1,0:T(8,128)(2,1)}, u32[]{:S(2)}) copy-start(bf16[6,12,192]{2,1,0:T(8,128)(2,1)} %copy-done.4) | copy-start | bytes 82948
  83.0 18.1 %copy-start.2 = (bf16[192,6144]{1,0:T(8,128)(2,1)S(1)}, bf16[192,6144]{1,0:T(8,128)(2,1)}, u32[]{:S(2)}) copy-start(bf16[192,6144]{1,0:T(8,128)(2,1)} %param.19) | copy-start | bytes 7077892
  92.2 20.8 %all-to-all-start = ((bf16[32,24,128]{2,1,0:T(8,128)(2,1)}), bf16[32,24,128]{2,1,0:T(8,128)(2,1)S(1)}, u32[]{:S(2)}, u32[]{:S(2)}) async-start(bf16[32,24,128]{2,1,0:T(8,128)(2,1)} %broadcast_in_dim.80), calls=%async_computation | async-start | bytes 393216 | tf_op jit(solution)/shard_map/all_to_all | solution.py:131
  106.0 15.6 %slice-start = ((bf16[912,128]{1,0:T(8,128)(2,1)}), bf16[144,128]{1,0:T(8,128)(2,1)S(1)}, s32[]{:S(2)}) async-start(bf16[912,128]{1,0:T(8,128)(2,1)} %copy-done.7), calls=%async_computation.2 | async-start | bytes 73728 | tf_op jit(solution)/shard_map/slice | solution.py:209
  106.1 15.7 %slice-start.1 = ((bf16[912,128]{1,0:T(8,128)(2,1)}), bf16[144,128]{1,0:T(8,128)(2,1)S(1)}, s32[]{:S(2)}) async-start(bf16[912,128]{1,0:T(8,128)(2,1)} %copy-done.8), calls=%async_computation.3 | async-start | bytes 73728 | tf_op jit(solution)/shard_map/slice | solution.py:209
  106.1 15.8 %slice-start.2 = ((bf16[912,128]{1,0:T(8,128)(2,1)}), bf16[144,128]{1,0:T(8,128)(2,1)S(1)}, s32[]{:S(2)}) async-start(bf16[912,128]{1,0:T(8,128)(2,1)} %copy-done.9), calls=%async_computation.4 | async-start | bytes 73728 | tf_op jit(solution)/shard_map/slice | solution.py:209
  106.1 15.9 %slice-start.3 = ((bf16[912,128]{1,0:T(8,128)(2,1)}), bf16[144,128]{1,0:T(8,128)(2,1)S(1)}, s32[]{:S(2)}) async-start(bf16[912,128]{1,0:T(8,128)(2,1)} %copy-done.10), calls=%async_computation.5 | async-start | bytes 73728 | tf_op jit(solution)/shard_map/slice | solution.py:209
  106.1 28.2 %copy-start.6 = (bf16[6,12,192]{2,1,0:T(8,128)(2,1)S(1)}, bf16[6,12,192]{2,1,0:T(8,128)(2,1)}, u32[]{:S(2)}) copy-start(bf16[6,12,192]{2,1,0:T(8,128)(2,1)} %copy-done.4) | copy-start | bytes 82948
  114.2 20.4 %copy-start.3 = (f32[12,192,128]{2,1,0:T(8,128)S(1)}, f32[12,192,128]{2,1,0:T(8,128)}, u32[]{:S(2)}) copy-start(f32[12,192,128]{2,1,0:T(8,128)} %get-tuple-element.12) | copy-start | bytes 3538948
  114.2 12.8 %all-to-all-start.1 = ((f32[8,24,128]{2,1,0:T(8,128)}), f32[8,24,128]{2,1,0:T(8,128)S(1)}, u32[]{:S(2)}, u32[]{:S(2)}) async-start(f32[8,24,128]{2,1,0:T(8,128)} %fusion.1), calls=%async_computation.1 | async-start | bytes 196608 | tf_op jit(solution)/shard_map/all_to_all | solution.py:227
  127.0 15.7 %collective-permute-start.10 = (bf16[24,128]{1,0:T(8,128)(2,1)S(1)}, bf16[24,128]{1,0:T(8,128)(2,1)S(1)}, u32[]{:S(2)}, u32[]{:S(2)}) collective-permute-start(bf16[24,128]{1,0:T(8,128)(2,1)S(1)} %reduce_sum.9), channel_id=1, source_target_pairs={{0,1},{1,2},{2,3},{3,4},{4,5},{5,6},{6,7},{7,0},{8,9},{9,10},{10,1... | collective-permute-start | bytes 18440 | tf_op jit(solution)/shard_map/ppermute | solution.py:17
  128.5 13.3 %collective-permute-start.9 = (bf16[24,128]{1,0:T(8,128)(2,1)S(1)}, bf16[24,128]{1,0:T(8,128)(2,1)S(1)}, u32[]{:S(2)}, u32[]{:S(2)}) collective-permute-start(bf16[24,128]{1,0:T(8,128)(2,1)S(1)} %reduce_sum.9), channel_id=1, source_target_pairs={{0,248},{8,0},{16,8},{24,16},{32,24},{40,32},{48,40},{56,48},{64,5... | collective-permute-start | bytes 18440 | tf_op jit(solution)/shard_map/ppermute | solution.py:17
  130.3 10.6 %collective-permute-start.8 = (bf16[24,128]{1,0:T(8,128)(2,1)S(1)}, bf16[24,128]{1,0:T(8,128)(2,1)S(1)}, u32[]{:S(2)}, u32[]{:S(2)}) collective-permute-start(bf16[24,128]{1,0:T(8,128)(2,1)S(1)} %reduce_sum.9), channel_id=1, source_target_pairs={{0,8},{8,16},{16,24},{24,32},{32,40},{40,48},{48,56},{56,64},{64,7... | collective-permute-start | bytes 18440 | tf_op jit(solution)/shard_map/ppermute | solution.py:17
  133.9 3.1 %collective-permute-start.11 = (bf16[24,128]{1,0:T(8,128)(2,1)S(1)}, bf16[24,128]{1,0:T(8,128)(2,1)S(1)}, u32[]{:S(2)}, u32[]{:S(2)}) collective-permute-start(bf16[24,128]{1,0:T(8,128)(2,1)S(1)} %reduce_sum.9), channel_id=1, source_target_pairs={{0,7},{1,0},{2,1},{3,2},{4,3},{5,4},{6,5},{7,6},{8,15},{9,8},{10,9... | collective-permute-start | bytes 18440 | tf_op jit(solution)/shard_map/ppermute | solution.py:17
  (2 other events, 2.7 us)

commit v6 on v5

--- a/solution.py
+++ b/solution.py
@@ -46,13 +46,15 @@
     return jnp.concatenate(outputs, axis=0)
 
 
-def product_kernel(stored, rows, mode, ghost_total, columns_ref, blocks_ref, prev_ref, local_ref, *rest):
+def product_kernel(
+    stored, rows, mode, ghost_total, columns_ref, send_ref, blocks_ref, prev_ref, local_ref, *rest
+):
     ghost_refs = rest[:ghost_total]
     rest = rest[ghost_total:]
     if mode == "plain":
         (out_ref, source, picked) = rest
     elif mode == "smooth":
-        (factors_ref, base_ref, out_ref, next_ref, low_ref, source, picked) = rest
+        (factors_ref, base_ref, out_ref, next_ref, low_ref, sends_ref, source, picked, kept) = rest
     else:
         (factors_ref, base_ref, out_ref, source, picked) = rest
     n = pl.program_id(0)
@@ -76,43 +78,65 @@
             out_ref[j] = left
             update = smoothed(factors_ref, j, left)
             next_ref[j] = base_ref[j] + update
-            low_ref[j] = update.astype(low_ref.dtype)
+            low = update.astype(low_ref.dtype)
+            low_ref[j] = low
+            kept[n * rows + j] = low
         else:
             out_ref[j] = base_ref[j] + smoothed(factors_ref, j, left)
 
-
-def block_product(blocks, columns, prev, local, ghosts, ghost_count, mode="plain", factors=None, base=None):
+    if mode == "smooth":
+
+        @pl.when(n == pl.num_programs(0) - 1)
+        def _():
+            for i in range(sends_ref.shape[0] // dof):
+                sends_ref[i * dof:(i + 1) * dof, :] = kept[send_ref[i]]
+
+
+def block_product(
+    blocks, columns, prev, local, ghosts, ghost_count, mode="plain", factors=None, base=None,
+    send=None,
+):
     block_count, dof, width = blocks.shape
     stored = width // dof
     vectors = local.shape[-1]
     rows = 6 if block_count % 6 == 0 else 1
-    whole = lambda shape: pl.BlockSpec(shape, lambda n, c: (0,) * len(shape))
-    tile = pl.BlockSpec((rows, dof, vectors), lambda n, c: (n, 0, 0))
+    whole = lambda shape: pl.BlockSpec(shape, lambda n, c, s: (0,) * len(shape))
+    tile = pl.BlockSpec((rows, dof, vectors), lambda n, c, s: (n, 0, 0))
     field = jax.ShapeDtypeStruct((block_count, dof, vectors), jnp.float32)
     in_specs = [
-        pl.BlockSpec((rows, dof, width), lambda n, c: (n, 0, 0)),
+        pl.BlockSpec((rows, dof, width), lambda n, c, s: (n, 0, 0)),
         tile,
         whole(local.shape),
     ] + [whole(g.shape) for g in ghosts]
     operands = [blocks, prev, local] + list(ghosts)
     if mode != "plain":
-        in_specs += [pl.BlockSpec((rows,) + factors.shape[1:], lambda n, c: (n, 0, 0, 0, 0)), tile]
+        in_specs += [pl.BlockSpec((rows,) + factors.shape[1:], lambda n, c, s: (n, 0, 0, 0, 0)), tile]
         operands += [factors, base]
+    scratch = [
+        pltpu.VMEM((block_count + len(ghosts) * ghost_count, dof, vectors), local.dtype),
+        pltpu.VMEM((width, vectors), local.dtype),
+    ]
+    if send is None:
+        send = jnp.zeros((1,), jnp.int32)
     if mode == "smooth":
-        out_specs = [tile, tile, tile]
-        out_shape = [field, field, jax.ShapeDtypeStruct(field.shape, jnp.bfloat16)]
+        sends_shape = (send.shape[0] * dof, vectors)
+        out_specs = [tile, tile, tile, whole(sends_shape)]
+        out_shape = [
+            field,
+            field,
+            jax.ShapeDtypeStruct(field.shape, jnp.bfloat16),
+            jax.ShapeDtypeStruct(sends_shape, jnp.bfloat16),
+        ]
+        scratch.append(pltpu.VMEM((block_count, dof, vectors), jnp.bfloat16))
     else:
         out_specs = tile
         out_shape = field
     grid_spec = pltpu.PrefetchScalarGridSpec(
-        num_scalar_prefetch=1,
+        num_scalar_prefetch=2,
         grid=(block_count // rows,),
         in_specs=in_specs,
         out_specs=out_specs,
-        scratch_shapes=[
-            pltpu.VMEM((block_count + len(ghosts) * ghost_count, dof, vectors), local.dtype),
-            pltpu.VMEM((width, vectors), local.dtype),
-        ],
+        scratch_shapes=scratch,
     )
     flops = 2 * block_count * dof * width * vectors
     moved = blocks.size * 2 + local.size * 2 * 3 + prev.size * 8 * (1 if mode == "plain" else 3)
@@ -121,7 +145,7 @@
         grid_spec=grid_spec,
         out_shape=out_shape,
         cost_estimate=pl.CostEstimate(flops=flops, bytes_accessed=moved, transcendentals=0),
-    )(columns.reshape(-1), *operands)
+    )(columns.reshape(-1), send, *operands)
 
 
 def gathered_copies(value, axis):
@@ -160,13 +184,6 @@
 
     ghost_rows = ghost_count * dof_count
 
-    def outgoing(vector):
-        shard_low = vector.astype(jnp.bfloat16)[0, 0]
-        packed = jnp.take(shard_low, send_rows.reshape(-1), axis=0)
-        packed = packed.reshape((groups * ghost_rows, vectors))
-        parts = [packed[g * ghost_rows:(g + 1) * ghost_rows] for g in range(groups)]
-        return shard_low, parts
-
     def residual(prev, shard_low, ghosts):
         return block_product(local_blocks, columns, prev[0, 0], shard_low, ghosts, ghost_count)[
             None, None
@@ -196,13 +213,13 @@
     first_ghosts = exchange(parts)
     first_iter = point_smooth(smoother, rhs)
     shard_low = first_iter.astype(jnp.bfloat16)[0, 0]
-    residual_first, second_iter, update_low = block_product(
+    residual_first, second_iter, shard_low, packed = block_product(
         local_blocks, columns, rhs[0, 0], shard_low, first_ghosts, ghost_count,
-        mode="smooth", factors=factors, base=first_iter[0, 0],
+        mode="smooth", factors=factors, base=first_iter[0, 0], send=sent,
     )
     residual_first = residual_first[None, None]
     second_iter = second_iter[None, None]
-    shard_low, parts = outgoing(update_low[None, None])
+    parts = [packed[g * ghost_rows:(g + 1) * ghost_rows] for g in range(groups)]
     payloads = [jnp.concatenate([parts[g], tables[g]], axis=0) for g in range(groups)]
     arrived = exchange(payloads)
     neighbour_tables = [
@@ -224,11 +241,21 @@
     held = lax.dynamic_slice_in_dim(held, lax.axis_index("col"), 1, 2)
     held = held.reshape((coarse_inverse.shape[0], row_count * coarse_rows))
     partial = jnp.dot(held, column_part, preferred_element_type=jnp.float32)
+    partial = partial.reshape((col_count, coarse_rows, vectors))
+    places = jnp.arange(col_count, dtype=jnp.int32)
+    around = jnp.stack([(places - 1) % col_count, places, (places + 1) % col_count], axis=1)
+    partial = jnp.take(partial, around.reshape(-1), axis=0)
+    partial = partial.reshape((col_count, 3, coarse_rows, vectors))
     partial = lax.all_to_all(partial, "col", 0, 0, tiled=True)
-    coarse_solution = partial.reshape((col_count, coarse_rows, vectors)).sum(axis=0)
-    coarse_flat = coarse_solution.astype(jnp.bfloat16)
+    coarse_solution = partial.sum(axis=0).astype(jnp.bfloat16)
+    coarse_flat = coarse_solution[1]
     coarse_rounded = coarse_flat.reshape((aggregates, coarse_dofs, vectors))
-    neighbour_coarse = exchange([coarse_flat] * groups)
+    neighbour_coarse = [
+        passed_along(coarse_flat, "row", 1),
+        passed_along(coarse_flat, "row", -1),
+        coarse_solution[0],
+        coarse_solution[2],
+    ]
     chosen = jnp.einsum(
         "an,akr->nkr",
         onehot.astype(jnp.bfloat16),

time: 151 us -> 156 us (1.033)
  local copies, waits for them, and re-layouts: 22.3 us -> 26.3 us
  other arithmetic: 6.88 us -> 10.1 us
  waiting for transfers between devices: 40.6 us -> 37.7 us
    ppermute x12 -> x10, waiting for transfers between devices: 28.7 us -> 18.3 us  [passed_along(): return lax.ppermute(value, axis, pairs)]
    all_to_all x1, waiting for transfers between devices: 4.97 us -> 8.91 us  [cycle(): partial = lax.all_to_all(partial, 'col', 0, 0, tiled=True)]
    all_to_all x1, waiting for transfers between devices: 6.9 us -> 10.6 us  [gathered_copies(): return lax.all_to_all(repeated, axis, 0, 0, tiled=True)]
    all_to_all x1, starting transfers between devices: 8.9 us -> 11.7 us  [gathered_copies(): return lax.all_to_all(repeated, axis, 0, 0, tiled=True)]
    mul x4, local copies, waits for them, and re-layouts: 0.5 us -> 2.92 us  [cycle(): member.T[:, :, None, None] * jnp.transpose(picked, (1, 0, 2))[:, None, :, :]]
    ppermute x12 -> x10, starting transfers between devices: 35.4 us -> 33.9 us  [passed_along(): return lax.ppermute(value, axis, pairs)]
    unnamed x34 -> x42, local copies, waits for them, and re-layouts: 3.61 us -> 3.61 us
  transfers between devices with their start and end apart: 14 -> 12, of which waited for: 8 -> 7; matrix products, arithmetic and copies ran while one was open for 13% -> 16% of each run, Pallas kernels for 0% -> 0%
where the time goes in v6:
time: 156 us; the launch traced here: 155 us
  starting transfers between devices  51.9 us (33%)
  waiting for transfers between devices  37.7 us (24%)
  local copies, waits for them, and re-layouts  26.3 us (17%)
  Pallas kernels  21.8 us (14%)
  other arithmetic  10.1 us (6%)
  matrix products  6.65 us (4%)
    ppermute x10, starting transfers between devices, passed_along(): return lax.ppermute(value, axis, pairs)  33.9 us
    pallas_call x3, Pallas kernels, block_product(): pl.pallas_call(functools.partial(product_kernel, stored, rows, mode, len(...  21.8 us
    ppermute x10, waiting for transfers between devices, passed_along(): return lax.ppermute(value, axis, pairs)  18.3 us
    all_to_all x1, starting transfers between devices, gathered_copies(): return lax.all_to_all(repeated, axis, 0, 0, tiled=True)  11.7 us
    all_to_all x1, waiting for transfers between devices, gathered_copies(): return lax.all_to_all(repeated, axis, 0, 0, tiled=True)  10.6 us
    all_to_all x1, waiting for transfers between devices, cycle(): partial = lax.all_to_all(partial, 'col', 0, 0, tiled=True)  8.91 us
    all_to_all x1, starting transfers between devices, cycle(): partial = lax.all_to_all(partial, 'col', 0, 0, tiled=True)  6.31 us
    add x2, other arithmetic, point_smooth(): summed + factors[:, :, component, 2, :, :, None] * pieces[:, :, :, 2]  3.84 us
  transfers between devices with their start and end apart: 12, of which 7 were waited for; matrix products, arithmetic and copies ran while one was open for 16% of the time, Pallas kernels for 0%

profile of v6, /device:TPU:1, one launch (start us, length us, event | category | flops | bytes accessed | tf_op | source)
XLA Modules:
  0.0 155.2 jit_solution(13994052604233251052)
XLA Ops:
  3.2 1.9 %gather_fusion.1 = f32[16,192,128]{2,1,0:T(8,128)S(1)} fusion(f32[12,192,128]{2,1,0:T(8,128)} %bitcast.145, s32[1024]{0:T(1024)S(1)} %pad_clamp_fusion.5), kind=kCustom, calls=%fused_computation.9 | custom fusion | bytes 3145792 | tf_op jit(solution)/shard_map/jit(_take)/gather | solution.py:206
  5.3 1.6 %multiply_add_fusion.2 = (f32[1,1,16,1,64,128]{5,4,3,2,1,0:T(8,128)S(1)}, f32[1,1,16,1,64,128]{5,4,3,2,1,0:T(8,128)S(1)}, f32[1,1,16,1,64,128]{5,4,3,2,1,0:T(8,128)S(1)}) fusion(f32[1,1,16,3,64,128]{5,4,3,2,1,0:T(8,128)S(1)} %broadcast_select_fusion, f32[16,64]{1,0:T(8,128)S(1)} %bitcast.167, f32[16,64]{1,0:T(8,128)S(1)} %bitcast.168, ...), kind=kLoop, calls=%fused_computation.28 | loop fusion | flops 1966080 | bytes 3182592 | tf_op jit(solution)/shard_map/add | solution.py:31
  8.1 3.0 %collective-permute-start.2 = (bf16[768,128]{1,0:T(8,128)(2,1)}, bf16[768,128]{1,0:T(8,128)(2,1)}, u32[]{:S(2)}, u32[]{:S(2)}) collective-permute-start(bf16[768,128]{1,0:T(8,128)(2,1)} %bitcast.29), channel_id=1, source_target_pairs={{0,1},{1,2},{2,3},{3,4},{4,5},{5,6},{6,7},{7,0},{8,9},{9,10},{10,1... | collective-permute-start | bytes 589832 | tf_op jit(solution)/shard_map/ppermute | solution.py:17
  11.3 10.5 %collective-permute-start.1 = (bf16[768,128]{1,0:T(8,128)(2,1)}, bf16[768,128]{1,0:T(8,128)(2,1)}, u32[]{:S(2)}, u32[]{:S(2)}) collective-permute-start(bf16[768,128]{1,0:T(8,128)(2,1)} %bitcast.28), channel_id=1, source_target_pairs={{0,248},{8,0},{16,8},{24,16},{32,24},{40,32},{48,40},{56,48},{64,5... | collective-permute-start | bytes 589832 | tf_op jit(solution)/shard_map/ppermute | solution.py:17
  27.3 2.3 %multiply_add_fusion.5 = (f32[1,1,12,1,64,128]{5,4,3,2,1,0:T(8,128)}, f32[1,1,12,1,64,128]{5,4,3,2,1,0:T(8,128)}, f32[1,1,12,1,64,128]{5,4,3,2,1,0:T(8,128)}) fusion(f32[1,1,12,3,64,128]{5,4,3,2,1,0:T(8,128)S(1)} %bitcast.147, f32[12,64]{1,0:T(8,128)S(1)} %get-tuple-element.57, f32[12,64]{1,0:T(8,128)S(1)} %get-tuple-element.58, ...), kind=kLoop, calls=%fused_computation.31 | loop fusion | flops 1474560 | bytes 2386944 | tf_op jit(solution)/shard_map/add | solution.py:31
  33.9 1.5 maximum_multiply_fusion.1
  35.5 1.0 convert_element_type.79.local_ref
  36.5 2.7 %copy.31 = bf16[192,6144]{0,1:T(8,128)(2,1)} copy(bf16[192,6144]{1,0:T(8,128)(2,1)S(1)} %copy-done.2) | data formatting | bytes 4718592 | tf_op args[7]
  39.3 1.7 %collective-permute-done.rest_0_ = bf16[768,128]{1,0:T(8,128)(2,1)} collective-permute-done((bf16[768,128]{1,0:T(8,128)(2,1)}, bf16[768,128]{1,0:T(8,128)(2,1)}, u32[]{:S(2)}, u32[]{:S(2)}) %collective-permute-start) | collective-permute-done | bytes 196640 | tf_op jit(solution)/shard_map/ppermute | solution.py:17
  40.9 2.7 %broadcast_in_dim.76.rest_4_ = bf16[12,3,3,64,128]{4,3,2,1,0:T(8,128)(2,1)} broadcast(bf16[12,3,3,64]{3,2,1,0:T(4,128)(2,1)} %copy.26), dimensions={0,1,2,3} | broadcast | bytes 1783296 | tf_op jit(solution)/shard_map/broadcast_in_dim | solution.py:196
  43.7 8.0 %shard_map.82 = (f32[12,192,128]{2,1,0:T(8,128)}, f32[12,192,128]{2,1,0:T(8,128)}, bf16[12,192,128]{2,1,0:T(8,128)(2,1)}, bf16[3072,128]{1,0:T(8,128)(2,1)}) custom-call(s32[96]{0:T(128)} %reshape_squeeze.20.columns_ref, s32[16]{0:T(128)} %copy-done.18, bf16[12,192,1536]{2,1,0:T(8,128)(2,1)} %bitcast.142, f32[12,192,128]{2,1,0:T(8,128)} %bitcast.146, ...), custom_call_target="tpu_custom_call" | custom-call | flops 905969664 | bytes 15925248 | tf_op jit(solution)/shard_map/pallas_call | solution.py:143
  51.7 1.3 fusion.34
  53.2 9.6 %collective-permute-start.5 = (bf16[912,128]{1,0:T(8,128)(2,1)S(1)}, bf16[912,128]{1,0:T(8,128)(2,1)S(1)}, u32[]{:S(2)}, u32[]{:S(2)}) collective-permute-start(bf16[912,128]{1,0:T(8,128)(2,1)S(1)} %pad_maximum_fusion.1), channel_id=1, source_target_pairs={{0,248},{8,0},{16,8},{24,16},{32,24},{40,32},{48,40},{56,48},{64,5... | collective-permute-start | bytes 700424 | tf_op jit(solution)/shard_map/ppermute | solution.py:17
  62.9 4.8 %collective-permute-start.6 = (bf16[912,128]{1,0:T(8,128)(2,1)S(1)}, bf16[912,128]{1,0:T(8,128)(2,1)S(1)}, u32[]{:S(2)}, u32[]{:S(2)}) collective-permute-start(bf16[912,128]{1,0:T(8,128)(2,1)S(1)} %pad_maximum_fusion.2), channel_id=1, source_target_pairs={{0,1},{1,2},{2,3},{3,4},{4,5},{5,6},{6,7},{7,0},{8,9},{9,10},{10,1... | collective-permute-start | bytes 700424 | tf_op jit(solution)/shard_map/ppermute | solution.py:17
  67.9 1.0 constant_dynamic-slice_fusion
  69.8 8.8 %collective-permute-done.6.rest_2_ = bf16[912,128]{1,0:T(8,128)(2,1)S(1)} collective-permute-done((bf16[912,128]{1,0:T(8,128)(2,1)S(1)}, bf16[912,128]{1,0:T(8,128)(2,1)S(1)}, u32[]{:S(2)}, u32[]{:S(2)}) %collective-permute-start.6) | collective-permute-done | bytes 233504 | tf_op jit(solution)/shard_map/ppermute | solution.py:17
  78.7 3.8 %collective-permute-done.7.rest_3_ = bf16[912,128]{1,0:T(8,128)(2,1)S(1)} collective-permute-done((bf16[912,128]{1,0:T(8,128)(2,1)S(1)}, bf16[912,128]{1,0:T(8,128)(2,1)S(1)}, u32[]{:S(2)}, u32[]{:S(2)}) %collective-permute-start.7) | collective-permute-done | bytes 233504 | tf_op jit(solution)/shard_map/ppermute | solution.py:17
  83.2 6.6 %shard_map.83.prev_ref = f32[12,192,128]{2,1,0:T(8,128)} custom-call(s32[96]{0:T(128)} %reshape_squeeze.20.columns_ref, s32[1]{0:T(128)} %constant.68.clone.1.send_ref, bf16[12,192,1536]{2,1,0:T(8,128)(2,1)} %bitcast.143, f32[12,192,128]{2,1,0:T(8,128)} %get-tuple-element.11.prev_ref, bf16[12,192,128]{2,1,0:T(8,128)(2,1)} %get-tuple-element.12.local_ref, ...), custom_call_target="tpu_custom_call" | custom-call | flops 905969664 | bytes 11206656 | tf_op jit(solution)/shard_map/pallas_call | solution.py:143
  89.8 1.5 convolution_bitcast_fusion.1
  92.4 11.7 %all-to-all-start = ((bf16[32,24,128]{2,1,0:T(8,128)(2,1)}), bf16[32,24,128]{2,1,0:T(8,128)(2,1)S(1)}, u32[]{:S(2)}, u32[]{:S(2)}) async-start(bf16[32,24,128]{2,1,0:T(8,128)(2,1)} %broadcast_in_dim.79), calls=%async_computation | async-start | bytes 393216 | tf_op jit(solution)/shard_map/all_to_all | solution.py:155
  104.2 1.2 reshape.583
  105.4 10.6 %all-to-all-done = bf16[32,24,128]{2,1,0:T(8,128)(2,1)S(1)} async-done(((bf16[32,24,128]{2,1,0:T(8,128)(2,1)}), bf16[32,24,128]{2,1,0:T(8,128)(2,1)S(1)}, u32[]{:S(2)}, u32[]{:S(2)}) %all-to-all-start) | async-done | bytes 196640 | tf_op jit(solution)/shard_map/all_to_all | solution.py:155
  118.0 6.3 %all-to-all-start.1 = ((f32[8,3,24,128]{3,2,1,0:T(8,128)}), f32[8,3,24,128]{3,2,1,0:T(8,128)S(1)}, u32[]{:S(2)}, u32[]{:S(2)}) async-start(f32[8,3,24,128]{3,2,1,0:T(8,128)} %broadcast_select_fusion.1), calls=%async_computation.1 | async-start | bytes 589824 | tf_op jit(solution)/shard_map/all_to_all | solution.py:249
  124.7 8.9 %all-to-all-done.1 = f32[8,3,24,128]{3,2,1,0:T(8,128)S(1)} async-done(((f32[8,3,24,128]{3,2,1,0:T(8,128)}), f32[8,3,24,128]{3,2,1,0:T(8,128)S(1)}, u32[]{:S(2)}, u32[]{:S(2)}) %all-to-all-start.1) | async-done | bytes 294944 | tf_op jit(solution)/shard_map/all_to_all | solution.py:249
  133.7 1.7 %collective-permute-start.9 = (bf16[24,128]{1,0:T(8,128)(2,1)S(1)}, bf16[24,128]{1,0:T(8,128)(2,1)S(1)}, u32[]{:S(2)}, u32[]{:S(2)}) collective-permute-start(bf16[24,128]{1,0:T(8,128)(2,1)S(1)} %get-tuple-element.59), channel_id=1, source_target_pairs={{0,248},{8,0},{16,8},{24,16},{32,24},{40,32},{48,40},{56,48},{64,5... | collective-permute-start | bytes 18440 | tf_op jit(solution)/shard_map/ppermute | solution.py:17
  135.4 3.7 %collective-permute-start.8 = (bf16[24,128]{1,0:T(8,128)(2,1)S(1)}, bf16[24,128]{1,0:T(8,128)(2,1)S(1)}, u32[]{:S(2)}, u32[]{:S(2)}) collective-permute-start(bf16[24,128]{1,0:T(8,128)(2,1)S(1)} %get-tuple-element.59), channel_id=1, source_target_pairs={{0,8},{8,16},{16,24},{24,32},{32,40},{40,48},{48,56},{56,64},{64,7... | collective-permute-start | bytes 18440 | tf_op jit(solution)/shard_map/ppermute | solution.py:17
  139.3 0.9 convolution_convert_fusion.1
  140.6 1.4 fusion.33
  143.0 3.1 %collective-permute-done.8 = bf16[24,128]{1,0:T(8,128)(2,1)S(1)} collective-permute-done((bf16[24,128]{1,0:T(8,128)(2,1)S(1)}, bf16[24,128]{1,0:T(8,128)(2,1)S(1)}, u32[]{:S(2)}, u32[]{:S(2)}) %collective-permute-start.8) | collective-permute-done | bytes 6176 | tf_op jit(solution)/shard_map/ppermute | solution.py:17
  146.0 0.9 convolution_convert_fusion.3
  147.0 0.9 convolution_convert_fusion.2
  147.9 7.3 %shard_map.84 = f32[12,192,128]{2,1,0:T(8,128)} custom-call(s32[96]{0:T(128)} %reshape_squeeze.20.columns_ref, s32[1]{0:T(128)} %constant.68.clone.1.send_ref, bf16[12,192,1536]{2,1,0:T(8,128)(2,1)} %bitcast.144, f32[12,192,128]{2,1,0:T(8,128)} %shard_map.83.prev_ref, bf16[12,192,128]{2,1,0:T(8,128)(2,1)} %get-tuple-element.29.local_ref, ...), custom_call_target="tpu_custom_call" | custom-call | flops 905969664 | bytes 15925248 | tf_op jit(solution)/shard_map/pallas_call | solution.py:143
  (131 shorter events, 21.4 us)
Async XLA Ops:
  0.8 4.3 %copy-start.18 = (s32[16]{0:T(128)}, s32[16]{0:T(128)S(1)}, u32[]{:S(2)}) copy-start(s32[16]{0:T(128)S(1)} %reshape_squeeze.21.send_ref) | copy-start | bytes 196
  6.9 14.9 %copy-start.16 = (s32[1,1,4,4]{3,2,1,0:T(4,128)S(1)}, s32[1,1,4,4]{3,2,1,0:T(4,128)}, u32[]{:S(2)}) copy-start(s32[1,1,4,4]{3,2,1,0:T(4,128)} %param.16) | copy-start | bytes 196
  6.9 14.9 %copy-start.19 = (s32[1,1,12]{2,1,0:T(1,128)S(1)}, s32[1,1,12]{2,1,0:T(1,128)}, u32[]{:S(2)}) copy-start(s32[1,1,12]{2,1,0:T(1,128)} %param.17) | copy-start | bytes 148
  6.9 16.1 %copy-start.15 = (bf16[1,1,6,2304]{3,2,1,0:T(8,128)(2,1)S(1)}, bf16[1,1,6,2304]{3,2,1,0:T(8,128)(2,1)}, u32[]{:S(2)}) copy-start(bf16[1,1,6,2304]{3,2,1,0:T(8,128)(2,1)} %param.18) | copy-start | bytes 82948
  7.0 19.6 %copy-start.14 = (bf16[1,1,3,3,768]{4,3,2,1,0:T(4,128)(2,1)S(1)}, bf16[1,1,3,3,768]{4,3,2,1,0:T(4,128)(2,1)}, u32[]{:S(2)}) copy-start(bf16[1,1,3,3,768]{4,3,2,1,0:T(4,128)(2,1)} %param.13) | copy-start | bytes 41476
  7.2 20.1 %copy-start = (f32[1,1,12,192,128]{4,3,2,1,0:T(8,128)S(1)}, f32[1,1,12,192,128]{4,3,2,1,0:T(8,128)}, u32[]{:S(2)}) copy-start(f32[1,1,12,192,128]{4,3,2,1,0:T(8,128)} %param.12) | copy-start | bytes 3538948
  8.1 31.1 %collective-permute-start.2 = (bf16[768,128]{1,0:T(8,128)(2,1)}, bf16[768,128]{1,0:T(8,128)(2,1)}, u32[]{:S(2)}, u32[]{:S(2)}) collective-permute-start(bf16[768,128]{1,0:T(8,128)(2,1)} %bitcast.29), channel_id=1, source_target_pairs={{0,1},{1,2},{2,3},{3,4},{4,5},{5,6},{6,7},{7,0},{8,9},{9,10},{10,1... | collective-permute-start | bytes 589832 | tf_op jit(solution)/shard_map/ppermute | solution.py:17
  11.1 28.1 %collective-permute-start.3 = (bf16[768,128]{1,0:T(8,128)(2,1)}, bf16[768,128]{1,0:T(8,128)(2,1)}, u32[]{:S(2)}, u32[]{:S(2)}) collective-permute-start(bf16[768,128]{1,0:T(8,128)(2,1)} %bitcast.30), channel_id=1, source_target_pairs={{0,7},{1,0},{2,1},{3,2},{4,3},{5,4},{6,5},{7,6},{8,15},{9,8},{10,9... | collective-permute-start | bytes 589832 | tf_op jit(solution)/shard_map/ppermute | solution.py:17
  11.3 27.9 %collective-permute-start.1 = (bf16[768,128]{1,0:T(8,128)(2,1)}, bf16[768,128]{1,0:T(8,128)(2,1)}, u32[]{:S(2)}, u32[]{:S(2)}) collective-permute-start(bf16[768,128]{1,0:T(8,128)(2,1)} %bitcast.28), channel_id=1, source_target_pairs={{0,248},{8,0},{16,8},{24,16},{32,24},{40,32},{48,40},{56,48},{64,5... | collective-permute-start | bytes 589832 | tf_op jit(solution)/shard_map/ppermute | solution.py:17
  21.8 19.1 %collective-permute-start = (bf16[768,128]{1,0:T(8,128)(2,1)}, bf16[768,128]{1,0:T(8,128)(2,1)}, u32[]{:S(2)}, u32[]{:S(2)}) collective-permute-start(bf16[768,128]{1,0:T(8,128)(2,1)} %bitcast.27), channel_id=1, source_target_pairs={{0,8},{8,16},{16,24},{24,32},{32,40},{40,48},{48,56},{56,64},{64,7... | collective-permute-start | bytes 589832 | tf_op jit(solution)/shard_map/ppermute | solution.py:17
  23.2 6.4 %copy-start.4 = (bf16[6,12,192]{2,1,0:T(8,128)(2,1)}, bf16[6,12,192]{2,1,0:T(8,128)(2,1)S(1)}, u32[]{:S(2)}) copy-start(bf16[6,12,192]{2,1,0:T(8,128)(2,1)S(1)} %reshape_squeeze.24) | copy-start | bytes 82948
  26.7 3.0 %copy-start.17 = (s32[1,1,12,8]{2,3,1,0:T(8,128)S(1)}, s32[1,1,12,8]{2,3,1,0:T(8,128)}, u32[]{:S(2)}) copy-start(s32[1,1,12,8]{2,3,1,0:T(8,128)} %param.15) | copy-start | bytes 1156
  35.4 3.8 %copy-start.1 = (f32[1,1,12,3,64,128]{5,4,3,2,1,0:T(8,128)}, f32[1,1,12,3,64,128]{5,4,3,2,1,0:T(8,128)S(1)}, u32[]{:S(2)}) copy-start(f32[1,1,12,3,64,128]{5,4,3,2,1,0:T(8,128)S(1)} %maximum_multiply_fusion.1) | copy-start | bytes 3538948
  51.7 11.1 %copy-start.11 = (bf16[144,128]{1,0:T(8,128)(2,1)S(1)}, bf16[144,128]{1,0:T(8,128)(2,1)}, u32[]{:S(2)}) copy-start(bf16[144,128]{1,0:T(8,128)(2,1)} %mul.401) | copy-start | bytes 110596
  51.7 15.9 %copy-start.10 = (bf16[144,128]{1,0:T(8,128)(2,1)S(1)}, bf16[144,128]{1,0:T(8,128)(2,1)}, u32[]{:S(2)}) copy-start(bf16[144,128]{1,0:T(8,128)(2,1)} %mul.405) | copy-start | bytes 110596
  53.1 15.9 %collective-permute-start.4 = (bf16[912,128]{1,0:T(8,128)(2,1)S(1)}, bf16[912,128]{1,0:T(8,128)(2,1)S(1)}, u32[]{:S(2)}, u32[]{:S(2)}) collective-permute-start(bf16[912,128]{1,0:T(8,128)(2,1)S(1)} %pad_maximum_fusion), channel_id=1, source_target_pairs={{0,8},{8,16},{16,24},{24,32},{32,40},{40,48},{48,56},{56,64},{64,7... | collective-permute-start | bytes 700424 | tf_op jit(solution)/shard_map/ppermute | solution.py:17
  53.2 16.6 %collective-permute-start.5 = (bf16[912,128]{1,0:T(8,128)(2,1)S(1)}, bf16[912,128]{1,0:T(8,128)(2,1)S(1)}, u32[]{:S(2)}, u32[]{:S(2)}) collective-permute-start(bf16[912,128]{1,0:T(8,128)(2,1)S(1)} %pad_maximum_fusion.1), channel_id=1, source_target_pairs={{0,248},{8,0},{16,8},{24,16},{32,24},{40,32},{48,40},{56,48},{64,5... | collective-permute-start | bytes 700424 | tf_op jit(solution)/shard_map/ppermute | solution.py:17
  62.9 15.8 %collective-permute-start.6 = (bf16[912,128]{1,0:T(8,128)(2,1)S(1)}, bf16[912,128]{1,0:T(8,128)(2,1)S(1)}, u32[]{:S(2)}, u32[]{:S(2)}) collective-permute-start(bf16[912,128]{1,0:T(8,128)(2,1)S(1)} %pad_maximum_fusion.2), channel_id=1, source_target_pairs={{0,1},{1,2},{2,3},{3,4},{4,5},{5,6},{6,7},{7,0},{8,9},{9,10},{10,1... | collective-permute-start | bytes 700424 | tf_op jit(solution)/shard_map/ppermute | solution.py:17
  67.6 14.9 %collective-permute-start.7 = (bf16[912,128]{1,0:T(8,128)(2,1)S(1)}, bf16[912,128]{1,0:T(8,128)(2,1)S(1)}, u32[]{:S(2)}, u32[]{:S(2)}) collective-permute-start(bf16[912,128]{1,0:T(8,128)(2,1)S(1)} %pad_maximum_fusion.3), channel_id=1, source_target_pairs={{0,7},{1,0},{2,1},{3,2},{4,3},{5,4},{6,5},{7,6},{8,15},{9,8},{10,9... | collective-permute-start | bytes 700424 | tf_op jit(solution)/shard_map/ppermute | solution.py:17
  69.0 13.5 %copy-start.6 = (bf16[912,128]{1,0:T(8,128)(2,1)}, bf16[912,128]{1,0:T(8,128)(2,1)S(1)}, u32[]{:S(2)}) copy-start(bf16[912,128]{1,0:T(8,128)(2,1)S(1)} %collective-permute-done.4.rest_0_) | copy-start | bytes 700420
  69.8 12.7 %copy-start.7 = (bf16[912,128]{1,0:T(8,128)(2,1)}, bf16[912,128]{1,0:T(8,128)(2,1)S(1)}, u32[]{:S(2)}) copy-start(bf16[912,128]{1,0:T(8,128)(2,1)S(1)} %collective-permute-done.5.rest_1_) | copy-start | bytes 700420
  78.7 3.9 %copy-start.8 = (bf16[912,128]{1,0:T(8,128)(2,1)}, bf16[912,128]{1,0:T(8,128)(2,1)S(1)}, u32[]{:S(2)}) copy-start(bf16[912,128]{1,0:T(8,128)(2,1)S(1)} %collective-permute-done.6.rest_2_) | copy-start | bytes 700420
  83.2 6.6 %copy-start.5 = (bf16[6,12,192]{2,1,0:T(8,128)(2,1)S(1)}, bf16[6,12,192]{2,1,0:T(8,128)(2,1)}, u32[]{:S(2)}) copy-start(bf16[6,12,192]{2,1,0:T(8,128)(2,1)} %copy-done.4) | copy-start | bytes 82948
  92.4 23.6 %all-to-all-start = ((bf16[32,24,128]{2,1,0:T(8,128)(2,1)}), bf16[32,24,128]{2,1,0:T(8,128)(2,1)S(1)}, u32[]{:S(2)}, u32[]{:S(2)}) async-start(bf16[32,24,128]{2,1,0:T(8,128)(2,1)} %broadcast_in_dim.79), calls=%async_computation | async-start | bytes 393216 | tf_op jit(solution)/shard_map/all_to_all | solution.py:155
  116.0 8.3 %slice-start = ((bf16[912,128]{1,0:T(8,128)(2,1)}), bf16[144,128]{1,0:T(8,128)(2,1)S(1)}, s32[]{:S(2)}) async-start(bf16[912,128]{1,0:T(8,128)(2,1)} %copy-done.6), calls=%async_computation.2 | async-start | bytes 73728 | tf_op jit(solution)/shard_map/slice | solution.py:226
  116.0 8.4 %slice-start.1 = ((bf16[912,128]{1,0:T(8,128)(2,1)}), bf16[144,128]{1,0:T(8,128)(2,1)S(1)}, s32[]{:S(2)}) async-start(bf16[912,128]{1,0:T(8,128)(2,1)} %copy-done.7), calls=%async_computation.3 | async-start | bytes 73728 | tf_op jit(solution)/shard_map/slice | solution.py:226
  116.6 7.9 %slice-start.2 = ((bf16[912,128]{1,0:T(8,128)(2,1)}), bf16[144,128]{1,0:T(8,128)(2,1)S(1)}, s32[]{:S(2)}) async-start(bf16[912,128]{1,0:T(8,128)(2,1)} %copy-done.8), calls=%async_computation.4 | async-start | bytes 73728 | tf_op jit(solution)/shard_map/slice | solution.py:226
  116.6 8.0 %slice-start.3 = ((bf16[912,128]{1,0:T(8,128)(2,1)}), bf16[144,128]{1,0:T(8,128)(2,1)S(1)}, s32[]{:S(2)}) async-start(bf16[912,128]{1,0:T(8,128)(2,1)} %copy-done.9), calls=%async_computation.5 | async-start | bytes 73728 | tf_op jit(solution)/shard_map/slice | solution.py:226
  118.0 22.6 %copy-start.3 = (f32[12,192,128]{2,1,0:T(8,128)S(1)}, f32[12,192,128]{2,1,0:T(8,128)}, u32[]{:S(2)}) copy-start(f32[12,192,128]{2,1,0:T(8,128)} %get-tuple-element.14) | copy-start | bytes 3538948
  118.0 15.6 %all-to-all-start.1 = ((f32[8,3,24,128]{3,2,1,0:T(8,128)}), f32[8,3,24,128]{3,2,1,0:T(8,128)S(1)}, u32[]{:S(2)}, u32[]{:S(2)}) async-start(f32[8,3,24,128]{3,2,1,0:T(8,128)} %broadcast_select_fusion.1), calls=%async_computation.1 | async-start | bytes 589824 | tf_op jit(solution)/shard_map/all_to_all | solution.py:249
  133.7 13.3 %collective-permute-start.9 = (bf16[24,128]{1,0:T(8,128)(2,1)S(1)}, bf16[24,128]{1,0:T(8,128)(2,1)S(1)}, u32[]{:S(2)}, u32[]{:S(2)}) collective-permute-start(bf16[24,128]{1,0:T(8,128)(2,1)S(1)} %get-tuple-element.59), channel_id=1, source_target_pairs={{0,248},{8,0},{16,8},{24,16},{32,24},{40,32},{48,40},{56,48},{64,5... | collective-permute-start | bytes 18440 | tf_op jit(solution)/shard_map/ppermute | solution.py:17
  135.4 10.6 %collective-permute-start.8 = (bf16[24,128]{1,0:T(8,128)(2,1)S(1)}, bf16[24,128]{1,0:T(8,128)(2,1)S(1)}, u32[]{:S(2)}, u32[]{:S(2)}) collective-permute-start(bf16[24,128]{1,0:T(8,128)(2,1)S(1)} %get-tuple-element.59), channel_id=1, source_target_pairs={{0,8},{8,16},{16,24},{24,32},{32,40},{40,48},{48,56},{56,64},{64,7... | collective-permute-start | bytes 18440 | tf_op jit(solution)/shard_map/ppermute | solution.py:17
  (4 other events, 6.1 us)

commit v7 on v6

--- a/solution.py
+++ b/solution.py
@@ -54,7 +54,11 @@
     if mode == "plain":
         (out_ref, source, picked) = rest
     elif mode == "smooth":
-        (factors_ref, base_ref, out_ref, next_ref, low_ref, sends_ref, source, picked, kept) = rest
+        (factors_ref, base_ref) = rest[:2]
+        table_refs = rest[2:2 + ghost_total]
+        (out_ref, next_ref, low_ref) = rest[2 + ghost_total:5 + ghost_total]
+        payload_refs = rest[5 + ghost_total:5 + 2 * ghost_total]
+        (source, picked, kept) = rest[5 + 2 * ghost_total:]
     else:
         (factors_ref, base_ref, out_ref, source, picked) = rest
     n = pl.program_id(0)
@@ -88,13 +92,15 @@
 
         @pl.when(n == pl.num_programs(0) - 1)
         def _():
-            for i in range(sends_ref.shape[0] // dof):
-                sends_ref[i * dof:(i + 1) * dof, :] = kept[send_ref[i]]
+            for g, ref in enumerate(payload_refs):
+                for b in range(ghost_count):
+                    ref[b * dof:(b + 1) * dof, :] = kept[send_ref[g * ghost_count + b]]
+                ref[ghost_count * dof:, :] = table_refs[g][...]
 
 
 def block_product(
     blocks, columns, prev, local, ghosts, ghost_count, mode="plain", factors=None, base=None,
-    send=None,
+    send=None, tables=(),
 ):
     block_count, dof, width = blocks.shape
     stored = width // dof
@@ -112,6 +118,9 @@
     if mode != "plain":
         in_specs += [pl.BlockSpec((rows,) + factors.shape[1:], lambda n, c, s: (n, 0, 0, 0, 0)), tile]
         operands += [factors, base]
+    if mode == "smooth":
+        in_specs += [whole(t.shape) for t in tables]
+        operands += list(tables)
     scratch = [
         pltpu.VMEM((block_count + len(ghosts) * ghost_count, dof, vectors), local.dtype),
         pltpu.VMEM((width, vectors), local.dtype),
@@ -119,14 +128,13 @@
     if send is None:
         send = jnp.zeros((1,), jnp.int32)
     if mode == "smooth":
-        sends_shape = (send.shape[0] * dof, vectors)
-        out_specs = [tile, tile, tile, whole(sends_shape)]
+        payload = [(ghost_count * dof + t.shape[0], vectors) for t in tables]
+        out_specs = [tile, tile, tile] + [whole(p) for p in payload]
         out_shape = [
             field,
             field,
             jax.ShapeDtypeStruct(field.shape, jnp.bfloat16),
-            jax.ShapeDtypeStruct(sends_shape, jnp.bfloat16),
-        ]
+        ] + [jax.ShapeDtypeStruct(p, jnp.bfloat16) for p in payload]
         scratch.append(pltpu.VMEM((block_count, dof, vectors), jnp.bfloat16))
     else:
         out_specs = tile
@@ -184,6 +192,13 @@
 
     ghost_rows = ghost_count * dof_count
 
+    def outgoing(vector):
+        shard_low = vector.astype(jnp.bfloat16)[0, 0]
+        packed = jnp.take(shard_low, send_rows.reshape(-1), axis=0)
+        packed = packed.reshape((groups * ghost_rows, vectors))
+        parts = [packed[g * ghost_rows:(g + 1) * ghost_rows] for g in range(groups)]
+        return shard_low, parts
+
     def residual(prev, shard_low, ghosts):
         return block_product(local_blocks, columns, prev[0, 0], shard_low, ghosts, ghost_count)[
             None, None
@@ -202,25 +217,17 @@
         table = member.T[:, :, None, None] * jnp.transpose(picked, (1, 0, 2))[:, None, :, :]
         tables.append(table.reshape((ghost_count * coarse_rows * dof_count) // vectors, vectors))
 
-    sent = send_rows.reshape(-1)
-    sent_rhs = jnp.take(rhs, sent, axis=2)
-    sent_factors = jnp.take(
-        smoother.reshape(smoother.shape[:4] + (block_count, grains)), sent, axis=4
-    ).reshape(smoother.shape[:4] + (sent.shape[0] * grains,))
-    sent_low = point_smooth(sent_factors, sent_rhs).astype(jnp.bfloat16)[0, 0]
-    sent_low = sent_low.reshape((groups * ghost_rows, vectors))
-    parts = [sent_low[g * ghost_rows:(g + 1) * ghost_rows] for g in range(groups)]
+    first_iter = point_smooth(smoother, rhs)
+    shard_low, parts = outgoing(first_iter)
     first_ghosts = exchange(parts)
-    first_iter = point_smooth(smoother, rhs)
-    shard_low = first_iter.astype(jnp.bfloat16)[0, 0]
-    residual_first, second_iter, shard_low, packed = block_product(
+    outputs = block_product(
         local_blocks, columns, rhs[0, 0], shard_low, first_ghosts, ghost_count,
-        mode="smooth", factors=factors, base=first_iter[0, 0], send=sent,
-    )
-    residual_first = residual_first[None, None]
-    second_iter = second_iter[None, None]
-    parts = [packed[g * ghost_rows:(g + 1) * ghost_rows] for g in range(groups)]
-    payloads = [jnp.concatenate([parts[g], tables[g]], axis=0) for g in range(groups)]
+        mode="smooth", factors=factors, base=first_iter[0, 0], send=send_rows.reshape(-1),
+        tables=tables,
+    )
+    residual_first, second_iter, shard_low = (o[None, None] for o in outputs[:3])
+    shard_low = shard_low[0, 0]
+    payloads = list(outputs[3:])
     arrived = exchange(payloads)
     neighbour_tables = [
         a[ghost_rows:].reshape((ghost_count, coarse_rows, dof_count)) for a in arrived
@@ -241,21 +248,11 @@
     held = lax.dynamic_slice_in_dim(held, lax.axis_index("col"), 1, 2)
     held = held.reshape((coarse_inverse.shape[0], row_count * coarse_rows))
     partial = jnp.dot(held, column_part, preferred_element_type=jnp.float32)
-    partial = partial.reshape((col_count, coarse_rows, vectors))
-    places = jnp.arange(col_count, dtype=jnp.int32)
-    around = jnp.stack([(places - 1) % col_count, places, (places + 1) % col_count], axis=1)
-    partial = jnp.take(partial, around.reshape(-1), axis=0)
-    partial = partial.reshape((col_count, 3, coarse_rows, vectors))
     partial = lax.all_to_all(partial, "col", 0, 0, tiled=True)
-    coarse_solution = partial.sum(axis=0).astype(jnp.bfloat16)
-    coarse_flat = coarse_solution[1]
+    coarse_solution = partial.reshape((col_count, coarse_rows, vectors)).sum(axis=0)
+    coarse_flat = coarse_solution.astype(jnp.bfloat16)
     coarse_rounded = coarse_flat.reshape((aggregates, coarse_dofs, vectors))
-    neighbour_coarse = [
-        passed_along(coarse_flat, "row", 1),
-        passed_along(coarse_flat, "row", -1),
-        coarse_solution[0],
-        coarse_solution[2],
-    ]
+    neighbour_coarse = exchange([coarse_flat] * groups)
     chosen = jnp.einsum(
         "an,akr->nkr",
         onehot.astype(jnp.bfloat16),

time: 156 us -> 150 us (0.962)
  local copies, waits for them, and re-layouts: 26.3 us -> 19.8 us
  other arithmetic: 10.1 us -> 5.39 us
  waiting for transfers between devices: 37.7 us -> 41.9 us
  matrix products: 6.65 us -> 8.27 us
    ppermute x10 -> x12, waiting for transfers between devices: 18.3 us -> 29 us  [passed_along(): return lax.ppermute(value, axis, pairs)]
    all_to_all x1, waiting for transfers between devices: 8.91 us -> 4.94 us  [cycle(): partial = lax.all_to_all(partial, 'col', 0, 0, tiled=True)]
    all_to_all x1, waiting for transfers between devices: 10.6 us -> 8.01 us  [gathered_copies(): return lax.all_to_all(repeated, axis, 0, 0, tiled=True)]
    gather x3 -> x1, local copies, waits for them, and re-layouts: 3.11 us -> 0.7 us  [outgoing(): packed = jnp.take(shard_low, send_rows.reshape(-1), axis=0)]
    slice x3 -> x1, local copies, waits for them, and re-layouts: 2.26 us -> 0.05 us  [outgoing(): parts = [packed[g * ghost_rows:(g + 1) * ghost_rows] for g in range(groups)]]
    dot_general x1, matrix products: 0.56 us -> 2.16 us  [cycle(): partial = jnp.dot(held, column_part, preferred_element_type=jnp.float32)]
    ppermute x10 -> x12, starting transfers between devices: 33.9 us -> 35.1 us  [passed_along(): return lax.ppermute(value, axis, pairs)]
    add x2 -> x1, other arithmetic: 3.84 us -> 2.89 us  [point_smooth(): summed + factors[:, :, component, 2, :, :, None] * pieces[:, :, :, 2]]
  transfers between devices with their start and end apart: 12 -> 14, of which waited for: 7 -> 8; matrix products, arithmetic and copies ran while one was open for 16% -> 12% of each run, Pallas kernels for 0% -> 0%
where the time goes in v7:
time: 150 us
  starting transfers between devices  52 us (35%)
  waiting for transfers between devices  41.9 us (28%)
  Pallas kernels  21.9 us (15%)
  local copies, waits for them, and re-layouts  19.8 us (13%)
  matrix products  8.27 us (6%)
  other arithmetic  5.39 us (4%)
    ppermute x12, starting transfers between devices, passed_along(): return lax.ppermute(value, axis, pairs)  35.1 us
    ppermute x12, waiting for transfers between devices, passed_along(): return lax.ppermute(value, axis, pairs)  29 us
    pallas_call x3, Pallas kernels, block_product(): pl.pallas_call(functools.partial(product_kernel, stored, rows, mode, len(...  21.9 us
    all_to_all x1, starting transfers between devices, gathered_copies(): return lax.all_to_all(repeated, axis, 0, 0, tiled=True)  11.3 us
    all_to_all x1, waiting for transfers between devices, gathered_copies(): return lax.all_to_all(repeated, axis, 0, 0, tiled=True)  8.01 us
    all_to_all x1, starting transfers between devices, cycle(): partial = lax.all_to_all(partial, 'col', 0, 0, tiled=True)  5.54 us
    all_to_all x1, waiting for transfers between devices, cycle(): partial = lax.all_to_all(partial, 'col', 0, 0, tiled=True)  4.94 us
    unnamed x40, local copies, waits for them, and re-layouts  4.1 us
  transfers between devices with their start and end apart: 14, of which 8 were waited for; matrix products, arithmetic and copies ran while one was open for 12% of the time, Pallas kernels for 0%

profile of v7, /device:TPU:1, one launch (start us, length us, event | category | flops | bytes accessed | tf_op | source)
XLA Modules:
  0.0 149.7 jit_solution(16001360646489646925)
XLA Ops:
  1.6 0.8 reshape.221
  2.4 2.9 %multiply_add_fusion.2 = (f32[1,1,12,1,64,128]{5,4,3,2,1,0:T(8,128)S(1)}, f32[1,1,12,1,64,128]{5,4,3,2,1,0:T(8,128)S(1)}, f32[1,1,12,1,64,128]{5,4,3,2,1,0:T(8,128)S(1)}) fusion(f32[1,1,12,3,64,128]{5,4,3,2,1,0:T(8,128)} %bitcast.125, f32[12,64]{1,0:T(8,128)S(1)} %get-tuple-element.45, f32[12,64]{1,0:T(8,128)S(1)} %get-tuple-element.46, ...), kind=kLoop, calls=%fused_computation.24 | loop fusion | flops 1474560 | bytes 2386944 | tf_op jit(solution)/shard_map/add | solution.py:31
  6.7 3.1 %collective-permute-start.2 = (bf16[768,128]{1,0:T(8,128)(2,1)S(1)}, bf16[768,128]{1,0:T(8,128)(2,1)S(1)}, u32[]{:S(2)}, u32[]{:S(2)}) collective-permute-start(bf16[768,128]{1,0:T(8,128)(2,1)S(1)} %bitcast.135), channel_id=1, source_target_pairs={{0,1},{1,2},{2,3},{3,4},{4,5},{5,6},{6,7},{7,0},{8,9},{9,10},{10,1... | collective-permute-start | bytes 589832 | tf_op jit(solution)/shard_map/ppermute | solution.py:17
  10.1 10.4 %collective-permute-start.1 = (bf16[768,128]{1,0:T(8,128)(2,1)S(1)}, bf16[768,128]{1,0:T(8,128)(2,1)S(1)}, u32[]{:S(2)}, u32[]{:S(2)}) collective-permute-start(bf16[768,128]{1,0:T(8,128)(2,1)S(1)} %bitcast.133), channel_id=1, source_target_pairs={{0,248},{8,0},{16,8},{24,16},{32,24},{40,32},{48,40},{56,48},{64,5... | collective-permute-start | bytes 589832 | tf_op jit(solution)/shard_map/ppermute | solution.py:17
  29.8 9.6 %collective-permute-done.rest_0_ = bf16[768,128]{1,0:T(8,128)(2,1)S(1)} collective-permute-done((bf16[768,128]{1,0:T(8,128)(2,1)S(1)}, bf16[768,128]{1,0:T(8,128)(2,1)S(1)}, u32[]{:S(2)}, u32[]{:S(2)}) %collective-permute-start) | collective-permute-done | bytes 196640 | tf_op jit(solution)/shard_map/ppermute | solution.py:17
  39.4 2.0 %broadcast_in_dim.54.rest_4_ = bf16[12,3,3,64,128]{4,3,2,1,0:T(8,128)(2,1)} broadcast(bf16[12,3,3,64]{3,2,1,0:T(4,128)(2,1)S(1)} %bitcast.136), dimensions={0,1,2,3} | broadcast | bytes 1783296 | tf_op jit(solution)/shard_map/broadcast_in_dim | solution.py:211
  41.4 8.2 %shard_map.82 = (f32[12,192,128]{2,1,0:T(8,128)}, f32[12,192,128]{2,1,0:T(8,128)}, bf16[12,192,128]{2,1,0:T(8,128)(2,1)}, bf16[912,128]{1,0:T(8,128)(2,1)}, bf16...) custom-call(s32[96]{0:T(128)} %reshape_squeeze.17.columns_ref, s32[16]{0:T(128)} %copy-done.17, ...), custom_call_target="tpu_custom_call" | custom-call | flops 905969664 | bytes 15925248 | tf_op jit(solution)/shard_map/pallas_call | solution.py:151
  49.6 9.6 %collective-permute-start.5 = (bf16[912,128]{1,0:T(8,128)(2,1)}, bf16[912,128]{1,0:T(8,128)(2,1)S(1)}, u32[]{:S(2)}, u32[]{:S(2)}) collective-permute-start(bf16[912,128]{1,0:T(8,128)(2,1)} %get-tuple-element.17), channel_id=1, source_target_pairs={{0,248},{8,0},{16,8},{24,16},{32,24},{40,32},{48,40},{56,48},{64,5... | collective-permute-start | bytes 700424 | tf_op jit(solution)/shard_map/ppermute | solution.py:17
  59.2 4.6 %collective-permute-start.6 = (bf16[912,128]{1,0:T(8,128)(2,1)}, bf16[912,128]{1,0:T(8,128)(2,1)S(1)}, u32[]{:S(2)}, u32[]{:S(2)}) collective-permute-start(bf16[912,128]{1,0:T(8,128)(2,1)} %get-tuple-element.18), channel_id=1, source_target_pairs={{0,1},{1,2},{2,3},{3,4},{4,5},{5,6},{6,7},{7,0},{8,9},{9,10},{10,1... | collective-permute-start | bytes 700424 | tf_op jit(solution)/shard_map/ppermute | solution.py:17
  63.8 2.5 %collective-permute-done.5.rest_1_ = bf16[912,128]{1,0:T(8,128)(2,1)S(1)} collective-permute-done((bf16[912,128]{1,0:T(8,128)(2,1)}, bf16[912,128]{1,0:T(8,128)(2,1)S(1)}, u32[]{:S(2)}, u32[]{:S(2)}) %collective-permute-start.5) | collective-permute-done | bytes 233504 | tf_op jit(solution)/shard_map/ppermute | solution.py:17
  66.3 9.2 %collective-permute-done.6.rest_2_ = bf16[912,128]{1,0:T(8,128)(2,1)S(1)} collective-permute-done((bf16[912,128]{1,0:T(8,128)(2,1)}, bf16[912,128]{1,0:T(8,128)(2,1)S(1)}, u32[]{:S(2)}, u32[]{:S(2)}) %collective-permute-start.6) | collective-permute-done | bytes 233504 | tf_op jit(solution)/shard_map/ppermute | solution.py:17
  75.6 3.9 %collective-permute-done.7.rest_3_ = bf16[912,128]{1,0:T(8,128)(2,1)S(1)} collective-permute-done((bf16[912,128]{1,0:T(8,128)(2,1)}, bf16[912,128]{1,0:T(8,128)(2,1)S(1)}, u32[]{:S(2)}, u32[]{:S(2)}) %collective-permute-start.7) | collective-permute-done | bytes 233504 | tf_op jit(solution)/shard_map/ppermute | solution.py:17
  80.2 6.5 %shard_map.83.prev_ref = f32[12,192,128]{2,1,0:T(8,128)} custom-call(s32[96]{0:T(128)} %reshape_squeeze.17.columns_ref, s32[1]{0:T(128)} %constant.9.clone.1.send_ref, bf16[12,192,1536]{2,1,0:T(8,128)(2,1)} %bitcast.121, f32[12,192,128]{2,1,0:T(8,128)} %get-tuple-element.14.prev_ref, bf16[12,192,128]{2,1,0:T(8,128)(2,1)} %get-tuple-element.15.local_ref, ...), custom_call_target="tpu_custom_call" | custom-call | flops 905969664 | bytes 11206656 | tf_op jit(solution)/shard_map/pallas_call | solution.py:151
  86.6 1.5 %convolution_bitcast_fusion.1 = f32[12,6,128]{2,1,0:T(8,128)S(1)} fusion(f32[12,192,128]{2,1,0:T(8,128)} %shard_map.83.prev_ref, bf16[6,12,192]{2,1,0:T(8,128)(2,1)S(1)} %reshape_squeeze.21), kind=kOutput, calls=%fused_computation.17 | convolution fusion | flops 3833856 | bytes 1244160 | tf_op jit(solution)/shard_map/knd,ndr->nkr/dot_general | solution.py:236
  89.2 11.3 %all-to-all-start = ((bf16[32,24,128]{2,1,0:T(8,128)(2,1)}), bf16[32,24,128]{2,1,0:T(8,128)(2,1)}, u32[]{:S(2)}, u32[]{:S(2)}) async-start(bf16[32,24,128]{2,1,0:T(8,128)(2,1)} %broadcast_in_dim.56), calls=%async_computation | async-start | bytes 393216 | tf_op jit(solution)/shard_map/all_to_all | solution.py:163
  100.5 3.0 %copy.30 = bf16[192,6144]{0,1:T(8,128)(2,1)S(1)} copy(bf16[192,6144]{1,0:T(8,128)(2,1)} %param.19) | data formatting | bytes 4718592 | tf_op args[7]
  103.6 1.1 reshape.325
  104.8 8.0 %all-to-all-done = bf16[32,24,128]{2,1,0:T(8,128)(2,1)} async-done(((bf16[32,24,128]{2,1,0:T(8,128)(2,1)}), bf16[32,24,128]{2,1,0:T(8,128)(2,1)}, u32[]{:S(2)}, u32[]{:S(2)}) %all-to-all-start) | async-done | bytes 196640 | tf_op jit(solution)/shard_map/all_to_all | solution.py:163
  112.8 2.2 %fusion = f32[8,24,128]{2,1,0:T(8,128)} fusion(bf16[768,128,1]{1,0,2:T(8,128)(2,1)} %bitcast.45, bf16[8,24,768]{1,0,2:T(8,128)(2,1)S(1)} %reshape.325), kind=kOutput, calls=%fused_computation.9 | convolution fusion | flops 37748736 | bytes 589824 | tf_op jit(solution)/shard_map/dot_general | solution.py:250
  115.0 5.5 %all-to-all-start.1 = ((f32[8,24,128]{2,1,0:T(8,128)}), f32[8,24,128]{2,1,0:T(8,128)S(1)}, u32[]{:S(2)}, u32[]{:S(2)}) async-start(f32[8,24,128]{2,1,0:T(8,128)} %fusion), calls=%async_computation.1 | async-start | bytes 196608 | tf_op jit(solution)/shard_map/all_to_all | solution.py:251
  120.9 4.9 %all-to-all-done.1 = f32[8,24,128]{2,1,0:T(8,128)S(1)} async-done(((f32[8,24,128]{2,1,0:T(8,128)}), f32[8,24,128]{2,1,0:T(8,128)S(1)}, u32[]{:S(2)}, u32[]{:S(2)}) %all-to-all-start.1) | async-done | bytes 98336 | tf_op jit(solution)/shard_map/all_to_all | solution.py:251
  125.9 1.5 collective-permute-start.10
  127.4 1.6 %collective-permute-start.9 = (bf16[24,128]{1,0:T(8,128)(2,1)S(1)}, bf16[24,128]{1,0:T(8,128)(2,1)S(1)}, u32[]{:S(2)}, u32[]{:S(2)}) collective-permute-start(bf16[24,128]{1,0:T(8,128)(2,1)S(1)} %reduce_sum.9), channel_id=1, source_target_pairs={{0,248},{8,0},{16,8},{24,16},{32,24},{40,32},{48,40},{56,48},{64,5... | collective-permute-start | bytes 18440 | tf_op jit(solution)/shard_map/ppermute | solution.py:17
  129.0 3.7 %collective-permute-start.8 = (bf16[24,128]{1,0:T(8,128)(2,1)S(1)}, bf16[24,128]{1,0:T(8,128)(2,1)S(1)}, u32[]{:S(2)}, u32[]{:S(2)}) collective-permute-start(bf16[24,128]{1,0:T(8,128)(2,1)S(1)} %reduce_sum.9), channel_id=1, source_target_pairs={{0,8},{8,16},{16,24},{24,32},{32,40},{40,48},{48,56},{56,64},{64,7... | collective-permute-start | bytes 18440 | tf_op jit(solution)/shard_map/ppermute | solution.py:17
  133.5 1.4 fusion.24
  134.9 0.9 collective-permute-done.11
  135.8 0.9 convolution_convert_fusion
  136.7 2.9 %collective-permute-done.8 = bf16[24,128]{1,0:T(8,128)(2,1)S(1)} collective-permute-done((bf16[24,128]{1,0:T(8,128)(2,1)S(1)}, bf16[24,128]{1,0:T(8,128)(2,1)S(1)}, u32[]{:S(2)}, u32[]{:S(2)}) %collective-permute-start.8) | collective-permute-done | bytes 6176 | tf_op jit(solution)/shard_map/ppermute | solution.py:17
  139.6 1.0 convolution_convert_fusion.3
  140.6 0.9 convolution_convert_fusion.2
  141.5 0.9 convolution_convert_fusion.1
  142.5 7.2 %shard_map.84 = f32[12,192,128]{2,1,0:T(8,128)} custom-call(s32[96]{0:T(128)} %reshape_squeeze.17.columns_ref, s32[1]{0:T(128)} %constant.9.clone.1.send_ref, bf16[12,192,1536]{2,1,0:T(8,128)(2,1)} %bitcast.122, f32[12,192,128]{2,1,0:T(8,128)} %shard_map.83.prev_ref, bf16[12,192,128]{2,1,0:T(8,128)(2,1)} %get-tuple-element.30.local_ref, ...), custom_call_target="tpu_custom_call" | custom-call | flops 905969664 | bytes 15925248 | tf_op jit(solution)/shard_map/pallas_call | solution.py:151
  (113 shorter events, 15.4 us)
Async XLA Ops:
  0.8 4.5 %copy-start.17 = (s32[16]{0:T(128)}, s32[16]{0:T(128)S(1)}, u32[]{:S(2)}) copy-start(s32[16]{0:T(128)S(1)} %reshape_squeeze.18.send_ref) | copy-start | bytes 196
  6.6 13.8 %copy-start.15 = (s32[1,1,4,4]{3,2,1,0:T(4,128)S(1)}, s32[1,1,4,4]{3,2,1,0:T(4,128)}, u32[]{:S(2)}) copy-start(s32[1,1,4,4]{3,2,1,0:T(4,128)} %param.16) | copy-start | bytes 196
  6.6 13.9 %copy-start.13 = (bf16[1,1,3,3,768]{4,3,2,1,0:T(4,128)(2,1)S(1)}, bf16[1,1,3,3,768]{4,3,2,1,0:T(4,128)(2,1)}, u32[]{:S(2)}) copy-start(bf16[1,1,3,3,768]{4,3,2,1,0:T(4,128)(2,1)} %param.13) | copy-start | bytes 41476
  6.6 14.0 %copy-start.18 = (s32[1,1,12]{2,1,0:T(1,128)S(1)}, s32[1,1,12]{2,1,0:T(1,128)}, u32[]{:S(2)}) copy-start(s32[1,1,12]{2,1,0:T(1,128)} %param.17) | copy-start | bytes 148
  6.6 15.2 %copy-start.14 = (bf16[1,1,6,2304]{3,2,1,0:T(8,128)(2,1)S(1)}, bf16[1,1,6,2304]{3,2,1,0:T(8,128)(2,1)}, u32[]{:S(2)}) copy-start(bf16[1,1,6,2304]{3,2,1,0:T(8,128)(2,1)} %param.18) | copy-start | bytes 82948
  6.7 18.7 %copy-start.16 = (s32[1,1,12,8]{2,3,1,0:T(8,128)S(1)}, s32[1,1,12,8]{2,3,1,0:T(8,128)}, u32[]{:S(2)}) copy-start(s32[1,1,12,8]{2,3,1,0:T(8,128)} %param.15) | copy-start | bytes 1156
  6.7 23.0 %collective-permute-start.2 = (bf16[768,128]{1,0:T(8,128)(2,1)S(1)}, bf16[768,128]{1,0:T(8,128)(2,1)S(1)}, u32[]{:S(2)}, u32[]{:S(2)}) collective-permute-start(bf16[768,128]{1,0:T(8,128)(2,1)S(1)} %bitcast.135), channel_id=1, source_target_pairs={{0,1},{1,2},{2,3},{3,4},{4,5},{5,6},{6,7},{7,0},{8,9},{9,10},{10,1... | collective-permute-start | bytes 589832 | tf_op jit(solution)/shard_map/ppermute | solution.py:17
  9.8 19.9 %collective-permute-start.3 = (bf16[768,128]{1,0:T(8,128)(2,1)S(1)}, bf16[768,128]{1,0:T(8,128)(2,1)S(1)}, u32[]{:S(2)}, u32[]{:S(2)}) collective-permute-start(bf16[768,128]{1,0:T(8,128)(2,1)S(1)} %bitcast.134), channel_id=1, source_target_pairs={{0,7},{1,0},{2,1},{3,2},{4,3},{5,4},{6,5},{7,6},{8,15},{9,8},{10,9... | collective-permute-start | bytes 589832 | tf_op jit(solution)/shard_map/ppermute | solution.py:17
  10.1 19.7 %collective-permute-start.1 = (bf16[768,128]{1,0:T(8,128)(2,1)S(1)}, bf16[768,128]{1,0:T(8,128)(2,1)S(1)}, u32[]{:S(2)}, u32[]{:S(2)}) collective-permute-start(bf16[768,128]{1,0:T(8,128)(2,1)S(1)} %bitcast.133), channel_id=1, source_target_pairs={{0,248},{8,0},{16,8},{24,16},{32,24},{40,32},{48,40},{56,48},{64,5... | collective-permute-start | bytes 589832 | tf_op jit(solution)/shard_map/ppermute | solution.py:17
  20.5 18.9 %collective-permute-start = (bf16[768,128]{1,0:T(8,128)(2,1)S(1)}, bf16[768,128]{1,0:T(8,128)(2,1)S(1)}, u32[]{:S(2)}, u32[]{:S(2)}) collective-permute-start(bf16[768,128]{1,0:T(8,128)(2,1)S(1)} %bitcast.132), channel_id=1, source_target_pairs={{0,8},{8,16},{16,24},{24,32},{32,40},{40,48},{48,56},{56,64},{64,7... | collective-permute-start | bytes 589832 | tf_op jit(solution)/shard_map/ppermute | solution.py:17
  22.0 64.7 %copy-start.3 = (bf16[6,12,192]{2,1,0:T(8,128)(2,1)}, bf16[6,12,192]{2,1,0:T(8,128)(2,1)S(1)}, u32[]{:S(2)}) copy-start(bf16[6,12,192]{2,1,0:T(8,128)(2,1)S(1)} %reshape_squeeze.21) | copy-start | bytes 82948
  29.8 11.6 %copy-start.9 = (bf16[768,128]{1,0:T(8,128)(2,1)}, bf16[768,128]{1,0:T(8,128)(2,1)S(1)}, u32[]{:S(2)}) copy-start(bf16[768,128]{1,0:T(8,128)(2,1)S(1)} %collective-permute-done.2.rest_2_) | copy-start | bytes 589828
  29.8 11.6 %copy-start.10 = (bf16[768,128]{1,0:T(8,128)(2,1)}, bf16[768,128]{1,0:T(8,128)(2,1)S(1)}, u32[]{:S(2)}) copy-start(bf16[768,128]{1,0:T(8,128)(2,1)S(1)} %collective-permute-done.3.rest_3_) | copy-start | bytes 589828
  29.8 11.6 %copy-start.11 = (bf16[768,128]{1,0:T(8,128)(2,1)}, bf16[768,128]{1,0:T(8,128)(2,1)S(1)}, u32[]{:S(2)}) copy-start(bf16[768,128]{1,0:T(8,128)(2,1)S(1)} %collective-permute-done.1.rest_1_) | copy-start | bytes 589828
  49.5 14.3 %collective-permute-start.4 = (bf16[912,128]{1,0:T(8,128)(2,1)}, bf16[912,128]{1,0:T(8,128)(2,1)S(1)}, u32[]{:S(2)}, u32[]{:S(2)}) collective-permute-start(bf16[912,128]{1,0:T(8,128)(2,1)} %get-tuple-element.16), channel_id=1, source_target_pairs={{0,8},{8,16},{16,24},{24,32},{32,40},{40,48},{48,56},{56,64},{64,7... | collective-permute-start | bytes 700424 | tf_op jit(solution)/shard_map/ppermute | solution.py:17
  49.6 16.7 %collective-permute-start.5 = (bf16[912,128]{1,0:T(8,128)(2,1)}, bf16[912,128]{1,0:T(8,128)(2,1)S(1)}, u32[]{:S(2)}, u32[]{:S(2)}) collective-permute-start(bf16[912,128]{1,0:T(8,128)(2,1)} %get-tuple-element.17), channel_id=1, source_target_pairs={{0,248},{8,0},{16,8},{24,16},{32,24},{40,32},{48,40},{56,48},{64,5... | collective-permute-start | bytes 700424 | tf_op jit(solution)/shard_map/ppermute | solution.py:17
  59.2 16.4 %collective-permute-start.6 = (bf16[912,128]{1,0:T(8,128)(2,1)}, bf16[912,128]{1,0:T(8,128)(2,1)S(1)}, u32[]{:S(2)}, u32[]{:S(2)}) collective-permute-start(bf16[912,128]{1,0:T(8,128)(2,1)} %get-tuple-element.18), channel_id=1, source_target_pairs={{0,1},{1,2},{2,3},{3,4},{4,5},{5,6},{6,7},{7,0},{8,9},{9,10},{10,1... | collective-permute-start | bytes 700424 | tf_op jit(solution)/shard_map/ppermute | solution.py:17
  63.8 15.6 %collective-permute-start.7 = (bf16[912,128]{1,0:T(8,128)(2,1)}, bf16[912,128]{1,0:T(8,128)(2,1)S(1)}, u32[]{:S(2)}, u32[]{:S(2)}) collective-permute-start(bf16[912,128]{1,0:T(8,128)(2,1)} %get-tuple-element.19), channel_id=1, source_target_pairs={{0,7},{1,0},{2,1},{3,2},{4,3},{5,4},{6,5},{7,6},{8,15},{9,8},{10,9... | collective-permute-start | bytes 700424 | tf_op jit(solution)/shard_map/ppermute | solution.py:17
  63.8 15.6 %copy-start.5 = (bf16[912,128]{1,0:T(8,128)(2,1)}, bf16[912,128]{1,0:T(8,128)(2,1)S(1)}, u32[]{:S(2)}) copy-start(bf16[912,128]{1,0:T(8,128)(2,1)S(1)} %collective-permute-done.4.rest_0_) | copy-start | bytes 700420
  66.3 13.2 %copy-start.6 = (bf16[912,128]{1,0:T(8,128)(2,1)}, bf16[912,128]{1,0:T(8,128)(2,1)S(1)}, u32[]{:S(2)}) copy-start(bf16[912,128]{1,0:T(8,128)(2,1)S(1)} %collective-permute-done.5.rest_1_) | copy-start | bytes 700420
  89.2 23.6 %all-to-all-start = ((bf16[32,24,128]{2,1,0:T(8,128)(2,1)}), bf16[32,24,128]{2,1,0:T(8,128)(2,1)}, u32[]{:S(2)}, u32[]{:S(2)}) async-start(bf16[32,24,128]{2,1,0:T(8,128)(2,1)} %broadcast_in_dim.56), calls=%async_computation | async-start | bytes 393216 | tf_op jit(solution)/shard_map/all_to_all | solution.py:163
  104.8 15.7 %slice-start = ((bf16[912,128]{1,0:T(8,128)(2,1)}), bf16[144,128]{1,0:T(8,128)(2,1)S(1)}, s32[]{:S(2)}) async-start(bf16[912,128]{1,0:T(8,128)(2,1)} %copy-done.5), calls=%async_computation.2 | async-start | bytes 73728 | tf_op jit(solution)/shard_map/slice | solution.py:233
  112.8 7.8 %slice-start.1 = ((bf16[912,128]{1,0:T(8,128)(2,1)}), bf16[144,128]{1,0:T(8,128)(2,1)S(1)}, s32[]{:S(2)}) async-start(bf16[912,128]{1,0:T(8,128)(2,1)} %copy-done.6), calls=%async_computation.3 | async-start | bytes 73728 | tf_op jit(solution)/shard_map/slice | solution.py:233
  112.8 7.9 %slice-start.2 = ((bf16[912,128]{1,0:T(8,128)(2,1)}), bf16[144,128]{1,0:T(8,128)(2,1)S(1)}, s32[]{:S(2)}) async-start(bf16[912,128]{1,0:T(8,128)(2,1)} %copy-done.7), calls=%async_computation.4 | async-start | bytes 73728 | tf_op jit(solution)/shard_map/slice | solution.py:233
  112.8 8.0 %slice-start.3 = ((bf16[912,128]{1,0:T(8,128)(2,1)}), bf16[144,128]{1,0:T(8,128)(2,1)S(1)}, s32[]{:S(2)}) async-start(bf16[912,128]{1,0:T(8,128)(2,1)} %copy-done.8), calls=%async_computation.5 | async-start | bytes 73728 | tf_op jit(solution)/shard_map/slice | solution.py:233
  112.8 20.4 %copy-start.4 = (bf16[6,12,192]{2,1,0:T(8,128)(2,1)S(1)}, bf16[6,12,192]{2,1,0:T(8,128)(2,1)}, u32[]{:S(2)}) copy-start(bf16[6,12,192]{2,1,0:T(8,128)(2,1)} %copy-done.3) | copy-start | bytes 82948
  115.0 18.6 %copy-start.2 = (f32[12,192,128]{2,1,0:T(8,128)S(1)}, f32[12,192,128]{2,1,0:T(8,128)}, u32[]{:S(2)}) copy-start(f32[12,192,128]{2,1,0:T(8,128)} %get-tuple-element.20) | copy-start | bytes 3538948
  115.0 10.9 %all-to-all-start.1 = ((f32[8,24,128]{2,1,0:T(8,128)}), f32[8,24,128]{2,1,0:T(8,128)S(1)}, u32[]{:S(2)}, u32[]{:S(2)}) async-start(f32[8,24,128]{2,1,0:T(8,128)} %fusion), calls=%async_computation.1 | async-start | bytes 196608 | tf_op jit(solution)/shard_map/all_to_all | solution.py:251
  125.9 15.6 %collective-permute-start.10 = (bf16[24,128]{1,0:T(8,128)(2,1)S(1)}, bf16[24,128]{1,0:T(8,128)(2,1)S(1)}, u32[]{:S(2)}, u32[]{:S(2)}) collective-permute-start(bf16[24,128]{1,0:T(8,128)(2,1)S(1)} %reduce_sum.9), channel_id=1, source_target_pairs={{0,1},{1,2},{2,3},{3,4},{4,5},{5,6},{6,7},{7,0},{8,9},{9,10},{10,1... | collective-permute-start | bytes 18440 | tf_op jit(solution)/shard_map/ppermute | solution.py:17
  127.4 13.2 %collective-permute-start.9 = (bf16[24,128]{1,0:T(8,128)(2,1)S(1)}, bf16[24,128]{1,0:T(8,128)(2,1)S(1)}, u32[]{:S(2)}, u32[]{:S(2)}) collective-permute-start(bf16[24,128]{1,0:T(8,128)(2,1)S(1)} %reduce_sum.9), channel_id=1, source_target_pairs={{0,248},{8,0},{16,8},{24,16},{32,24},{40,32},{48,40},{56,48},{64,5... | collective-permute-start | bytes 18440 | tf_op jit(solution)/shard_map/ppermute | solution.py:17
  129.0 10.6 %collective-permute-start.8 = (bf16[24,128]{1,0:T(8,128)(2,1)S(1)}, bf16[24,128]{1,0:T(8,128)(2,1)S(1)}, u32[]{:S(2)}, u32[]{:S(2)}) collective-permute-start(bf16[24,128]{1,0:T(8,128)(2,1)S(1)} %reduce_sum.9), channel_id=1, source_target_pairs={{0,8},{8,16},{16,24},{24,32},{32,40},{40,48},{48,56},{56,64},{64,7... | collective-permute-start | bytes 18440 | tf_op jit(solution)/shard_map/ppermute | solution.py:17
  132.7 3.1 %collective-permute-start.11 = (bf16[24,128]{1,0:T(8,128)(2,1)S(1)}, bf16[24,128]{1,0:T(8,128)(2,1)S(1)}, u32[]{:S(2)}, u32[]{:S(2)}) collective-permute-start(bf16[24,128]{1,0:T(8,128)(2,1)S(1)} %reduce_sum.9), channel_id=1, source_target_pairs={{0,7},{1,0},{2,1},{3,2},{4,3},{5,4},{6,5},{7,6},{8,15},{9,8},{10,9... | collective-permute-start | bytes 18440 | tf_op jit(solution)/shard_map/ppermute | solution.py:17
  (5 other events, 8.7 us)

commit v8 on v7

--- a/solution.py
+++ b/solution.py
@@ -156,6 +156,17 @@
     )(columns.reshape(-1), send, *operands)
 
 
+def coarse_kernel(held_ref, part_ref, out_ref):
+    out_ref[...] = jnp.dot(held_ref[...], part_ref[...], preferred_element_type=jnp.float32)
+
+
+def coarse_product(held, part):
+    return pl.pallas_call(
+        coarse_kernel,
+        out_shape=jax.ShapeDtypeStruct((held.shape[0], part.shape[1]), jnp.float32),
+    )(held, part)
+
+
 def gathered_copies(value, axis):
     count = lax.axis_size(axis)
     repeated = jnp.broadcast_to(value[None], (count,) + value.shape)
@@ -229,6 +240,11 @@
     shard_low = shard_low[0, 0]
     payloads = list(outputs[3:])
     arrived = exchange(payloads)
+    held = coarse_inverse.reshape(
+        (coarse_inverse.shape[0], row_count, col_count, coarse_rows)
+    )
+    held = lax.dynamic_slice_in_dim(held, lax.axis_index("col"), 1, 2)
+    held = held.reshape((coarse_inverse.shape[0], row_count * coarse_rows))
     neighbour_tables = [
         a[ghost_rows:].reshape((ghost_count, coarse_rows, dof_count)) for a in arrived
     ]
@@ -244,10 +260,7 @@
     )
     coarse_rhs = coarse_residual.astype(jnp.bfloat16).reshape((coarse_rows, vectors))
     column_part = gathered_copies(coarse_rhs, "row")
-    held = coarse_inverse.reshape((coarse_inverse.shape[0], row_count, col_count, coarse_rows))
-    held = lax.dynamic_slice_in_dim(held, lax.axis_index("col"), 1, 2)
-    held = held.reshape((coarse_inverse.shape[0], row_count * coarse_rows))
-    partial = jnp.dot(held, column_part, preferred_element_type=jnp.float32)
+    partial = coarse_product(held, column_part)
     partial = lax.all_to_all(partial, "col", 0, 0, tiled=True)
     coarse_solution = partial.reshape((col_count, coarse_rows, vectors)).sum(axis=0)
     coarse_flat = coarse_solution.astype(jnp.bfloat16)

time: 150 us -> 150 us (level)
  matrix products: 8.27 us -> 6.12 us
  Pallas kernels: 21.9 us -> 23.7 us
    dot_general x1 -> x0, matrix products: 2.16 us -> none  [cycle(): partial = jnp.dot(held, column_part, preferred_element_type=jnp.float32)]
    pallas_call x0 -> x1, Pallas kernels: none -> 1.88 us  [coarse_product(): pl.pallas_call(coarse_kernel, out_shape=jax.ShapeDtypeStruct((held.shape[...]
  transfers between devices with their start and end apart: 14 -> 14, of which waited for: 8 -> 8; matrix products, arithmetic and copies ran while one was open for 12% -> 13% of each run, Pallas kernels for 0% -> 0%
where the time goes in v8:
time: 150 us; the launch traced here: 149 us
  starting transfers between devices  52 us (35%)
  waiting for transfers between devices  41.4 us (28%)
  Pallas kernels  23.7 us (16%)
  local copies, waits for them, and re-layouts  20.3 us (14%)
  matrix products  6.12 us (4%)
  other arithmetic  5.39 us (4%)
    ppermute x12, starting transfers between devices, passed_along(): return lax.ppermute(value, axis, pairs)  35.1 us
    ppermute x12, waiting for transfers between devices, passed_along(): return lax.ppermute(value, axis, pairs)  29 us
    pallas_call x3, Pallas kernels, block_product(): pl.pallas_call(functools.partial(product_kernel, stored, rows, mode, len(...  21.8 us
    all_to_all x1, starting transfers between devices, gathered_copies(): return lax.all_to_all(repeated, axis, 0, 0, tiled=True)  11.3 us
    all_to_all x1, waiting for transfers between devices, gathered_copies(): return lax.all_to_all(repeated, axis, 0, 0, tiled=True)  8.28 us
    all_to_all x1, starting transfers between devices, cycle(): partial = lax.all_to_all(partial, 'col', 0, 0, tiled=True)  5.53 us
    all_to_all x1, waiting for transfers between devices, cycle(): partial = lax.all_to_all(partial, 'col', 0, 0, tiled=True)  4.16 us
    unnamed x40, local copies, waits for them, and re-layouts  4.08 us
  transfers between devices with their start and end apart: 14, of which 8 were waited for; matrix products, arithmetic and copies ran while one was open for 13% of the time, Pallas kernels for 0%

profile of v8, /device:TPU:1, one launch (start us, length us, event | category | flops | bytes accessed | tf_op | source)
XLA Modules:
  0.0 149.4 jit_solution(6562899953253064624)
XLA Ops:
  1.6 0.8 reshape.222
  2.4 2.9 %multiply_add_fusion.2 = (f32[1,1,12,1,64,128]{5,4,3,2,1,0:T(8,128)S(1)}, f32[1,1,12,1,64,128]{5,4,3,2,1,0:T(8,128)S(1)}, f32[1,1,12,1,64,128]{5,4,3,2,1,0:T(8,128)S(1)}) fusion(f32[1,1,12,3,64,128]{5,4,3,2,1,0:T(8,128)} %bitcast.120, f32[12,64]{1,0:T(8,128)S(1)} %get-tuple-element.45, f32[12,64]{1,0:T(8,128)S(1)} %get-tuple-element.46, ...), kind=kLoop, calls=%fused_computation.22 | loop fusion | flops 1474560 | bytes 2386944 | tf_op jit(solution)/shard_map/add | solution.py:31
  6.7 3.1 %collective-permute-start.2 = (bf16[768,128]{1,0:T(8,128)(2,1)S(1)}, bf16[768,128]{1,0:T(8,128)(2,1)S(1)}, u32[]{:S(2)}, u32[]{:S(2)}) collective-permute-start(bf16[768,128]{1,0:T(8,128)(2,1)S(1)} %bitcast.132), channel_id=1, source_target_pairs={{0,1},{1,2},{2,3},{3,4},{4,5},{5,6},{6,7},{7,0},{8,9},{9,10},{10,1... | collective-permute-start | bytes 589832 | tf_op jit(solution)/shard_map/ppermute | solution.py:17
  10.1 10.4 %collective-permute-start.1 = (bf16[768,128]{1,0:T(8,128)(2,1)S(1)}, bf16[768,128]{1,0:T(8,128)(2,1)S(1)}, u32[]{:S(2)}, u32[]{:S(2)}) collective-permute-start(bf16[768,128]{1,0:T(8,128)(2,1)S(1)} %bitcast.130), channel_id=1, source_target_pairs={{0,248},{8,0},{16,8},{24,16},{32,24},{40,32},{48,40},{56,48},{64,5... | collective-permute-start | bytes 589832 | tf_op jit(solution)/shard_map/ppermute | solution.py:17
  29.8 9.6 %collective-permute-done.rest_0_ = bf16[768,128]{1,0:T(8,128)(2,1)S(1)} collective-permute-done((bf16[768,128]{1,0:T(8,128)(2,1)S(1)}, bf16[768,128]{1,0:T(8,128)(2,1)S(1)}, u32[]{:S(2)}, u32[]{:S(2)}) %collective-permute-start) | collective-permute-done | bytes 196640 | tf_op jit(solution)/shard_map/ppermute | solution.py:17
  39.4 2.0 %broadcast_in_dim.54.rest_4_ = bf16[12,3,3,64,128]{4,3,2,1,0:T(8,128)(2,1)} broadcast(bf16[12,3,3,64]{3,2,1,0:T(4,128)(2,1)S(1)} %bitcast.133), dimensions={0,1,2,3} | broadcast | bytes 1783296 | tf_op jit(solution)/shard_map/broadcast_in_dim | solution.py:222
  41.3 8.2 %shard_map.82 = (f32[12,192,128]{2,1,0:T(8,128)}, f32[12,192,128]{2,1,0:T(8,128)}, bf16[12,192,128]{2,1,0:T(8,128)(2,1)}, bf16[912,128]{1,0:T(8,128)(2,1)}, bf16...) custom-call(s32[96]{0:T(128)} %reshape_squeeze.17.columns_ref, s32[16]{0:T(128)} %copy-done.17, ...), custom_call_target="tpu_custom_call" | custom-call | flops 905969664 | bytes 15925248 | tf_op jit(solution)/shard_map/pallas_call | solution.py:151
  49.6 9.6 %collective-permute-start.5 = (bf16[912,128]{1,0:T(8,128)(2,1)}, bf16[912,128]{1,0:T(8,128)(2,1)S(1)}, u32[]{:S(2)}, u32[]{:S(2)}) collective-permute-start(bf16[912,128]{1,0:T(8,128)(2,1)} %get-tuple-element.17), channel_id=1, source_target_pairs={{0,248},{8,0},{16,8},{24,16},{32,24},{40,32},{48,40},{56,48},{64,5... | collective-permute-start | bytes 700424 | tf_op jit(solution)/shard_map/ppermute | solution.py:17
  59.2 4.6 %collective-permute-start.6 = (bf16[912,128]{1,0:T(8,128)(2,1)}, bf16[912,128]{1,0:T(8,128)(2,1)S(1)}, u32[]{:S(2)}, u32[]{:S(2)}) collective-permute-start(bf16[912,128]{1,0:T(8,128)(2,1)} %get-tuple-element.18), channel_id=1, source_target_pairs={{0,1},{1,2},{2,3},{3,4},{4,5},{5,6},{6,7},{7,0},{8,9},{9,10},{10,1... | collective-permute-start | bytes 700424 | tf_op jit(solution)/shard_map/ppermute | solution.py:17
  63.8 2.5 %collective-permute-done.5.rest_1_ = bf16[912,128]{1,0:T(8,128)(2,1)S(1)} collective-permute-done((bf16[912,128]{1,0:T(8,128)(2,1)}, bf16[912,128]{1,0:T(8,128)(2,1)S(1)}, u32[]{:S(2)}, u32[]{:S(2)}) %collective-permute-start.5) | collective-permute-done | bytes 233504 | tf_op jit(solution)/shard_map/ppermute | solution.py:17
  66.3 9.2 %collective-permute-done.6.rest_2_ = bf16[912,128]{1,0:T(8,128)(2,1)S(1)} collective-permute-done((bf16[912,128]{1,0:T(8,128)(2,1)}, bf16[912,128]{1,0:T(8,128)(2,1)S(1)}, u32[]{:S(2)}, u32[]{:S(2)}) %collective-permute-start.6) | collective-permute-done | bytes 233504 | tf_op jit(solution)/shard_map/ppermute | solution.py:17
  75.5 3.9 %collective-permute-done.7.rest_3_ = bf16[912,128]{1,0:T(8,128)(2,1)S(1)} collective-permute-done((bf16[912,128]{1,0:T(8,128)(2,1)}, bf16[912,128]{1,0:T(8,128)(2,1)S(1)}, u32[]{:S(2)}, u32[]{:S(2)}) %collective-permute-start.7) | collective-permute-done | bytes 233504 | tf_op jit(solution)/shard_map/ppermute | solution.py:17
  80.1 6.4 %shard_map.83.prev_ref = f32[12,192,128]{2,1,0:T(8,128)} custom-call(s32[96]{0:T(128)} %reshape_squeeze.17.columns_ref, s32[1]{0:T(128)} %constant.9.clone.1.send_ref, bf16[12,192,1536]{2,1,0:T(8,128)(2,1)} %bitcast.116, f32[12,192,128]{2,1,0:T(8,128)} %get-tuple-element.14.prev_ref, bf16[12,192,128]{2,1,0:T(8,128)(2,1)} %get-tuple-element.15.local_ref, ...), custom_call_target="tpu_custom_call" | custom-call | flops 905969664 | bytes 11206656 | tf_op jit(solution)/shard_map/pallas_call | solution.py:151
  86.6 1.5 %convolution_bitcast_fusion.1 = f32[12,6,128]{2,1,0:T(8,128)S(1)} fusion(f32[12,192,128]{2,1,0:T(8,128)} %shard_map.83.prev_ref, bf16[6,12,192]{2,1,0:T(8,128)(2,1)S(1)} %reshape_squeeze.21), kind=kOutput, calls=%fused_computation.15 | convolution fusion | flops 3833856 | bytes 1244160 | tf_op jit(solution)/shard_map/knd,ndr->nkr/dot_general | solution.py:252
  89.1 11.3 %all-to-all-start = ((bf16[32,24,128]{2,1,0:T(8,128)(2,1)}), bf16[32,24,128]{2,1,0:T(8,128)(2,1)}, u32[]{:S(2)}, u32[]{:S(2)}) async-start(bf16[32,24,128]{2,1,0:T(8,128)(2,1)} %broadcast_in_dim.56), calls=%async_computation | async-start | bytes 393216 | tf_op jit(solution)/shard_map/all_to_all | solution.py:174
  100.5 3.0 %copy.30 = bf16[192,6144]{0,1:T(8,128)(2,1)S(1)} copy(bf16[192,6144]{1,0:T(8,128)(2,1)} %param.19) | data formatting | bytes 4718592 | tf_op args[7]
  103.6 0.9 copy.35.held_ref
  104.5 8.3 %all-to-all-done = bf16[32,24,128]{2,1,0:T(8,128)(2,1)} async-done(((bf16[32,24,128]{2,1,0:T(8,128)(2,1)}), bf16[32,24,128]{2,1,0:T(8,128)(2,1)}, u32[]{:S(2)}, u32[]{:S(2)}) %all-to-all-start) | async-done | bytes 196640 | tf_op jit(solution)/shard_map/all_to_all | solution.py:174
  112.8 1.9 %shard_map.84 = f32[192,128]{1,0:T(8,128)} custom-call(bf16[192,768]{1,0:T(8,128)(2,1)} %copy.35.held_ref, bf16[768,128]{1,0:T(8,128)(2,1)} %bitcast.45.part_ref), custom_call_target="tpu_custom_call" | custom-call | tf_op jit(solution)/shard_map/pallas_call | solution.py:164
  114.6 5.5 %all-to-all-start.1 = ((f32[8,24,128]{2,1,0:T(8,128)}), f32[8,24,128]{2,1,0:T(8,128)S(1)}, u32[]{:S(2)}, u32[]{:S(2)}) async-start(f32[8,24,128]{2,1,0:T(8,128)} %bitcast.128), calls=%async_computation.1 | async-start | bytes 196608 | tf_op jit(solution)/shard_map/all_to_all | solution.py:264
  121.4 4.2 %all-to-all-done.1 = f32[8,24,128]{2,1,0:T(8,128)S(1)} async-done(((f32[8,24,128]{2,1,0:T(8,128)}), f32[8,24,128]{2,1,0:T(8,128)S(1)}, u32[]{:S(2)}, u32[]{:S(2)}) %all-to-all-start.1) | async-done | bytes 98336 | tf_op jit(solution)/shard_map/all_to_all | solution.py:264
  125.6 1.5 collective-permute-start.10
  127.0 1.6 %collective-permute-start.9 = (bf16[24,128]{1,0:T(8,128)(2,1)S(1)}, bf16[24,128]{1,0:T(8,128)(2,1)S(1)}, u32[]{:S(2)}, u32[]{:S(2)}) collective-permute-start(bf16[24,128]{1,0:T(8,128)(2,1)S(1)} %reduce_sum.9), channel_id=1, source_target_pairs={{0,248},{8,0},{16,8},{24,16},{32,24},{40,32},{48,40},{56,48},{64,5... | collective-permute-start | bytes 18440 | tf_op jit(solution)/shard_map/ppermute | solution.py:17
  128.7 3.7 %collective-permute-start.8 = (bf16[24,128]{1,0:T(8,128)(2,1)S(1)}, bf16[24,128]{1,0:T(8,128)(2,1)S(1)}, u32[]{:S(2)}, u32[]{:S(2)}) collective-permute-start(bf16[24,128]{1,0:T(8,128)(2,1)S(1)} %reduce_sum.9), channel_id=1, source_target_pairs={{0,8},{8,16},{16,24},{24,32},{32,40},{40,48},{48,56},{56,64},{64,7... | collective-permute-start | bytes 18440 | tf_op jit(solution)/shard_map/ppermute | solution.py:17
  133.2 1.4 fusion.22
  134.6 0.9 collective-permute-done.11
  135.5 0.9 convolution_convert_fusion
  136.4 2.9 %collective-permute-done.8 = bf16[24,128]{1,0:T(8,128)(2,1)S(1)} collective-permute-done((bf16[24,128]{1,0:T(8,128)(2,1)S(1)}, bf16[24,128]{1,0:T(8,128)(2,1)S(1)}, u32[]{:S(2)}, u32[]{:S(2)}) %collective-permute-start.8) | collective-permute-done | bytes 6176 | tf_op jit(solution)/shard_map/ppermute | solution.py:17
  139.3 0.9 convolution_convert_fusion.3
  140.2 0.9 convolution_convert_fusion.2
  141.2 0.9 convolution_convert_fusion.1
  142.1 7.2 %shard_map.85 = f32[12,192,128]{2,1,0:T(8,128)} custom-call(s32[96]{0:T(128)} %reshape_squeeze.17.columns_ref, s32[1]{0:T(128)} %constant.9.clone.1.send_ref, bf16[12,192,1536]{2,1,0:T(8,128)(2,1)} %bitcast.117, f32[12,192,128]{2,1,0:T(8,128)} %shard_map.83.prev_ref, bf16[12,192,128]{2,1,0:T(8,128)(2,1)} %get-tuple-element.30.local_ref, ...), custom_call_target="tpu_custom_call" | custom-call | flops 905969664 | bytes 15925248 | tf_op jit(solution)/shard_map/pallas_call | solution.py:151
  (112 shorter events, 16.2 us)
Async XLA Ops:
  0.8 4.5 %copy-start.17 = (s32[16]{0:T(128)}, s32[16]{0:T(128)S(1)}, u32[]{:S(2)}) copy-start(s32[16]{0:T(128)S(1)} %reshape_squeeze.18.send_ref) | copy-start | bytes 196
  6.6 13.9 %copy-start.15 = (s32[1,1,4,4]{3,2,1,0:T(4,128)S(1)}, s32[1,1,4,4]{3,2,1,0:T(4,128)}, u32[]{:S(2)}) copy-start(s32[1,1,4,4]{3,2,1,0:T(4,128)} %param.16) | copy-start | bytes 196
  6.6 13.9 %copy-start.13 = (bf16[1,1,3,3,768]{4,3,2,1,0:T(4,128)(2,1)S(1)}, bf16[1,1,3,3,768]{4,3,2,1,0:T(4,128)(2,1)}, u32[]{:S(2)}) copy-start(bf16[1,1,3,3,768]{4,3,2,1,0:T(4,128)(2,1)} %param.13) | copy-start | bytes 41476
  6.6 14.0 %copy-start.18 = (s32[1,1,12]{2,1,0:T(1,128)S(1)}, s32[1,1,12]{2,1,0:T(1,128)}, u32[]{:S(2)}) copy-start(s32[1,1,12]{2,1,0:T(1,128)} %param.17) | copy-start | bytes 148
  6.6 15.2 %copy-start.14 = (bf16[1,1,6,2304]{3,2,1,0:T(8,128)(2,1)S(1)}, bf16[1,1,6,2304]{3,2,1,0:T(8,128)(2,1)}, u32[]{:S(2)}) copy-start(bf16[1,1,6,2304]{3,2,1,0:T(8,128)(2,1)} %param.18) | copy-start | bytes 82948
  6.7 18.7 %copy-start.16 = (s32[1,1,12,8]{2,3,1,0:T(8,128)S(1)}, s32[1,1,12,8]{2,3,1,0:T(8,128)}, u32[]{:S(2)}) copy-start(s32[1,1,12,8]{2,3,1,0:T(8,128)} %param.15) | copy-start | bytes 1156
  6.7 23.0 %collective-permute-start.2 = (bf16[768,128]{1,0:T(8,128)(2,1)S(1)}, bf16[768,128]{1,0:T(8,128)(2,1)S(1)}, u32[]{:S(2)}, u32[]{:S(2)}) collective-permute-start(bf16[768,128]{1,0:T(8,128)(2,1)S(1)} %bitcast.132), channel_id=1, source_target_pairs={{0,1},{1,2},{2,3},{3,4},{4,5},{5,6},{6,7},{7,0},{8,9},{9,10},{10,1... | collective-permute-start | bytes 589832 | tf_op jit(solution)/shard_map/ppermute | solution.py:17
  9.8 20.0 %collective-permute-start.3 = (bf16[768,128]{1,0:T(8,128)(2,1)S(1)}, bf16[768,128]{1,0:T(8,128)(2,1)S(1)}, u32[]{:S(2)}, u32[]{:S(2)}) collective-permute-start(bf16[768,128]{1,0:T(8,128)(2,1)S(1)} %bitcast.131), channel_id=1, source_target_pairs={{0,7},{1,0},{2,1},{3,2},{4,3},{5,4},{6,5},{7,6},{8,15},{9,8},{10,9... | collective-permute-start | bytes 589832 | tf_op jit(solution)/shard_map/ppermute | solution.py:17
  10.1 19.7 %collective-permute-start.1 = (bf16[768,128]{1,0:T(8,128)(2,1)S(1)}, bf16[768,128]{1,0:T(8,128)(2,1)S(1)}, u32[]{:S(2)}, u32[]{:S(2)}) collective-permute-start(bf16[768,128]{1,0:T(8,128)(2,1)S(1)} %bitcast.130), channel_id=1, source_target_pairs={{0,248},{8,0},{16,8},{24,16},{32,24},{40,32},{48,40},{56,48},{64,5... | collective-permute-start | bytes 589832 | tf_op jit(solution)/shard_map/ppermute | solution.py:17
  20.5 18.9 %collective-permute-start = (bf16[768,128]{1,0:T(8,128)(2,1)S(1)}, bf16[768,128]{1,0:T(8,128)(2,1)S(1)}, u32[]{:S(2)}, u32[]{:S(2)}) collective-permute-start(bf16[768,128]{1,0:T(8,128)(2,1)S(1)} %bitcast.129), channel_id=1, source_target_pairs={{0,8},{8,16},{16,24},{24,32},{32,40},{40,48},{48,56},{56,64},{64,7... | collective-permute-start | bytes 589832 | tf_op jit(solution)/shard_map/ppermute | solution.py:17
  22.0 64.6 %copy-start.3 = (bf16[6,12,192]{2,1,0:T(8,128)(2,1)}, bf16[6,12,192]{2,1,0:T(8,128)(2,1)S(1)}, u32[]{:S(2)}) copy-start(bf16[6,12,192]{2,1,0:T(8,128)(2,1)S(1)} %reshape_squeeze.21) | copy-start | bytes 82948
  29.8 11.6 %copy-start.9 = (bf16[768,128]{1,0:T(8,128)(2,1)}, bf16[768,128]{1,0:T(8,128)(2,1)S(1)}, u32[]{:S(2)}) copy-start(bf16[768,128]{1,0:T(8,128)(2,1)S(1)} %collective-permute-done.2.rest_2_) | copy-start | bytes 589828
  29.8 11.6 %copy-start.10 = (bf16[768,128]{1,0:T(8,128)(2,1)}, bf16[768,128]{1,0:T(8,128)(2,1)S(1)}, u32[]{:S(2)}) copy-start(bf16[768,128]{1,0:T(8,128)(2,1)S(1)} %collective-permute-done.3.rest_3_) | copy-start | bytes 589828
  29.8 11.5 %copy-start.11 = (bf16[768,128]{1,0:T(8,128)(2,1)}, bf16[768,128]{1,0:T(8,128)(2,1)S(1)}, u32[]{:S(2)}) copy-start(bf16[768,128]{1,0:T(8,128)(2,1)S(1)} %collective-permute-done.1.rest_1_) | copy-start | bytes 589828
  49.5 14.3 %collective-permute-start.4 = (bf16[912,128]{1,0:T(8,128)(2,1)}, bf16[912,128]{1,0:T(8,128)(2,1)S(1)}, u32[]{:S(2)}, u32[]{:S(2)}) collective-permute-start(bf16[912,128]{1,0:T(8,128)(2,1)} %get-tuple-element.16), channel_id=1, source_target_pairs={{0,8},{8,16},{16,24},{24,32},{32,40},{40,48},{48,56},{56,64},{64,7... | collective-permute-start | bytes 700424 | tf_op jit(solution)/shard_map/ppermute | solution.py:17
  49.6 16.7 %collective-permute-start.5 = (bf16[912,128]{1,0:T(8,128)(2,1)}, bf16[912,128]{1,0:T(8,128)(2,1)S(1)}, u32[]{:S(2)}, u32[]{:S(2)}) collective-permute-start(bf16[912,128]{1,0:T(8,128)(2,1)} %get-tuple-element.17), channel_id=1, source_target_pairs={{0,248},{8,0},{16,8},{24,16},{32,24},{40,32},{48,40},{56,48},{64,5... | collective-permute-start | bytes 700424 | tf_op jit(solution)/shard_map/ppermute | solution.py:17
  59.2 16.4 %collective-permute-start.6 = (bf16[912,128]{1,0:T(8,128)(2,1)}, bf16[912,128]{1,0:T(8,128)(2,1)S(1)}, u32[]{:S(2)}, u32[]{:S(2)}) collective-permute-start(bf16[912,128]{1,0:T(8,128)(2,1)} %get-tuple-element.18), channel_id=1, source_target_pairs={{0,1},{1,2},{2,3},{3,4},{4,5},{5,6},{6,7},{7,0},{8,9},{9,10},{10,1... | collective-permute-start | bytes 700424 | tf_op jit(solution)/shard_map/ppermute | solution.py:17
  63.8 15.6 %collective-permute-start.7 = (bf16[912,128]{1,0:T(8,128)(2,1)}, bf16[912,128]{1,0:T(8,128)(2,1)S(1)}, u32[]{:S(2)}, u32[]{:S(2)}) collective-permute-start(bf16[912,128]{1,0:T(8,128)(2,1)} %get-tuple-element.19), channel_id=1, source_target_pairs={{0,7},{1,0},{2,1},{3,2},{4,3},{5,4},{6,5},{7,6},{8,15},{9,8},{10,9... | collective-permute-start | bytes 700424 | tf_op jit(solution)/shard_map/ppermute | solution.py:17
  63.8 15.6 %copy-start.5 = (bf16[912,128]{1,0:T(8,128)(2,1)}, bf16[912,128]{1,0:T(8,128)(2,1)S(1)}, u32[]{:S(2)}) copy-start(bf16[912,128]{1,0:T(8,128)(2,1)S(1)} %collective-permute-done.4.rest_0_) | copy-start | bytes 700420
  66.3 13.2 %copy-start.6 = (bf16[912,128]{1,0:T(8,128)(2,1)}, bf16[912,128]{1,0:T(8,128)(2,1)S(1)}, u32[]{:S(2)}) copy-start(bf16[912,128]{1,0:T(8,128)(2,1)S(1)} %collective-permute-done.5.rest_1_) | copy-start | bytes 700420
  75.5 3.9 %copy-start.7 = (bf16[912,128]{1,0:T(8,128)(2,1)}, bf16[912,128]{1,0:T(8,128)(2,1)S(1)}, u32[]{:S(2)}) copy-start(bf16[912,128]{1,0:T(8,128)(2,1)S(1)} %collective-permute-done.6.rest_2_) | copy-start | bytes 700420
  89.1 23.6 %all-to-all-start = ((bf16[32,24,128]{2,1,0:T(8,128)(2,1)}), bf16[32,24,128]{2,1,0:T(8,128)(2,1)}, u32[]{:S(2)}, u32[]{:S(2)}) async-start(bf16[32,24,128]{2,1,0:T(8,128)(2,1)} %broadcast_in_dim.56), calls=%async_computation | async-start | bytes 393216 | tf_op jit(solution)/shard_map/all_to_all | solution.py:174
  103.6 17.5 %slice-start = ((bf16[912,128]{1,0:T(8,128)(2,1)}), bf16[144,128]{1,0:T(8,128)(2,1)S(1)}, s32[]{:S(2)}) async-start(bf16[912,128]{1,0:T(8,128)(2,1)} %copy-done.6), calls=%async_computation.2 | async-start | bytes 73728 | tf_op jit(solution)/shard_map/slice | solution.py:249
  103.6 17.6 %slice-start.1 = ((bf16[912,128]{1,0:T(8,128)(2,1)}), bf16[144,128]{1,0:T(8,128)(2,1)S(1)}, s32[]{:S(2)}) async-start(bf16[912,128]{1,0:T(8,128)(2,1)} %copy-done.7), calls=%async_computation.3 | async-start | bytes 73728 | tf_op jit(solution)/shard_map/slice | solution.py:249
  103.6 17.7 %slice-start.2 = ((bf16[912,128]{1,0:T(8,128)(2,1)}), bf16[144,128]{1,0:T(8,128)(2,1)S(1)}, s32[]{:S(2)}) async-start(bf16[912,128]{1,0:T(8,128)(2,1)} %copy-done.8), calls=%async_computation.4 | async-start | bytes 73728 | tf_op jit(solution)/shard_map/slice | solution.py:249
  103.6 29.2 %copy-start.4 = (bf16[6,12,192]{2,1,0:T(8,128)(2,1)S(1)}, bf16[6,12,192]{2,1,0:T(8,128)(2,1)}, u32[]{:S(2)}) copy-start(bf16[6,12,192]{2,1,0:T(8,128)(2,1)} %copy-done.3) | copy-start | bytes 82948
  114.6 18.6 %copy-start.2 = (f32[12,192,128]{2,1,0:T(8,128)S(1)}, f32[12,192,128]{2,1,0:T(8,128)}, u32[]{:S(2)}) copy-start(f32[12,192,128]{2,1,0:T(8,128)} %get-tuple-element.20) | copy-start | bytes 3538948
  114.6 10.9 %all-to-all-start.1 = ((f32[8,24,128]{2,1,0:T(8,128)}), f32[8,24,128]{2,1,0:T(8,128)S(1)}, u32[]{:S(2)}, u32[]{:S(2)}) async-start(f32[8,24,128]{2,1,0:T(8,128)} %bitcast.128), calls=%async_computation.1 | async-start | bytes 196608 | tf_op jit(solution)/shard_map/all_to_all | solution.py:264
  125.6 15.6 %collective-permute-start.10 = (bf16[24,128]{1,0:T(8,128)(2,1)S(1)}, bf16[24,128]{1,0:T(8,128)(2,1)S(1)}, u32[]{:S(2)}, u32[]{:S(2)}) collective-permute-start(bf16[24,128]{1,0:T(8,128)(2,1)S(1)} %reduce_sum.9), channel_id=1, source_target_pairs={{0,1},{1,2},{2,3},{3,4},{4,5},{5,6},{6,7},{7,0},{8,9},{9,10},{10,1... | collective-permute-start | bytes 18440 | tf_op jit(solution)/shard_map/ppermute | solution.py:17
  127.0 13.2 %collective-permute-start.9 = (bf16[24,128]{1,0:T(8,128)(2,1)S(1)}, bf16[24,128]{1,0:T(8,128)(2,1)S(1)}, u32[]{:S(2)}, u32[]{:S(2)}) collective-permute-start(bf16[24,128]{1,0:T(8,128)(2,1)S(1)} %reduce_sum.9), channel_id=1, source_target_pairs={{0,248},{8,0},{16,8},{24,16},{32,24},{40,32},{48,40},{56,48},{64,5... | collective-permute-start | bytes 18440 | tf_op jit(solution)/shard_map/ppermute | solution.py:17
  128.7 10.6 %collective-permute-start.8 = (bf16[24,128]{1,0:T(8,128)(2,1)S(1)}, bf16[24,128]{1,0:T(8,128)(2,1)S(1)}, u32[]{:S(2)}, u32[]{:S(2)}) collective-permute-start(bf16[24,128]{1,0:T(8,128)(2,1)S(1)} %reduce_sum.9), channel_id=1, source_target_pairs={{0,8},{8,16},{16,24},{24,32},{32,40},{40,48},{48,56},{56,64},{64,7... | collective-permute-start | bytes 18440 | tf_op jit(solution)/shard_map/ppermute | solution.py:17
  132.4 3.1 %collective-permute-start.11 = (bf16[24,128]{1,0:T(8,128)(2,1)S(1)}, bf16[24,128]{1,0:T(8,128)(2,1)S(1)}, u32[]{:S(2)}, u32[]{:S(2)}) collective-permute-start(bf16[24,128]{1,0:T(8,128)(2,1)S(1)} %reduce_sum.9), channel_id=1, source_target_pairs={{0,7},{1,0},{2,1},{3,2},{4,3},{5,4},{6,5},{7,6},{8,15},{9,8},{10,9... | collective-permute-start | bytes 18440 | tf_op jit(solution)/shard_map/ppermute | solution.py:17
  (4 other events, 4.8 us)

commit v9 on v8

--- a/solution.py
+++ b/solution.py
@@ -53,6 +53,8 @@
     rest = rest[ghost_total:]
     if mode == "plain":
         (out_ref, source, picked) = rest
+    elif mode == "restrict":
+        (prolong_ref, out_ref, coarse_ref, source, picked) = rest
     elif mode == "smooth":
         (factors_ref, base_ref) = rest[:2]
         table_refs = rest[2:2 + ghost_total]
@@ -67,6 +69,8 @@
 
     @pl.when(n == 0)
     def _():
+        if mode == "restrict":
+            coarse_ref[...] = jnp.zeros_like(coarse_ref)
         source[0:block_count] = local_ref[...]
         for g, ref in enumerate(ghost_refs):
             for b in range(ghost_count):
@@ -78,6 +82,15 @@
         left = prev_ref[j] - jnp.dot(blocks_ref[j], picked[...], preferred_element_type=jnp.float32)
         if mode == "plain":
             out_ref[j] = left
+        elif mode == "restrict":
+            out_ref[j] = left
+            term = jnp.dot(
+                prolong_ref[n * rows + j], left.astype(jnp.bfloat16),
+                preferred_element_type=jnp.float32,
+            )
+            owner = send_ref[n * rows + j]
+            for a in range(coarse_ref.shape[0]):
+                coarse_ref[a] += jnp.where(owner == a, term, 0.0)
         elif mode == "smooth":
             out_ref[j] = left
             update = smoothed(factors_ref, j, left)
@@ -100,7 +113,7 @@
 
 def block_product(
     blocks, columns, prev, local, ghosts, ghost_count, mode="plain", factors=None, base=None,
-    send=None, tables=(),
+    send=None, tables=(), prolong=None, aggregates=None,
 ):
     block_count, dof, width = blocks.shape
     stored = width // dof
@@ -115,12 +128,15 @@
         whole(local.shape),
     ] + [whole(g.shape) for g in ghosts]
     operands = [blocks, prev, local] + list(ghosts)
-    if mode != "plain":
+    if mode in ("smooth", "final"):
         in_specs += [pl.BlockSpec((rows,) + factors.shape[1:], lambda n, c, s: (n, 0, 0, 0, 0)), tile]
         operands += [factors, base]
     if mode == "smooth":
         in_specs += [whole(t.shape) for t in tables]
         operands += list(tables)
+    if mode == "restrict":
+        in_specs += [whole(prolong.shape)]
+        operands += [prolong]
     scratch = [
         pltpu.VMEM((block_count + len(ghosts) * ghost_count, dof, vectors), local.dtype),
         pltpu.VMEM((width, vectors), local.dtype),
@@ -136,6 +152,10 @@
             jax.ShapeDtypeStruct(field.shape, jnp.bfloat16),
         ] + [jax.ShapeDtypeStruct(p, jnp.bfloat16) for p in payload]
         scratch.append(pltpu.VMEM((block_count, dof, vectors), jnp.bfloat16))
+    elif mode == "restrict":
+        coarse_shape = (aggregates, prolong.shape[1], vectors)
+        out_specs = [tile, whole(coarse_shape)]
+        out_shape = [field, jax.ShapeDtypeStruct(coarse_shape, jnp.float32)]
     else:
         out_specs = tile
         out_shape = field
@@ -210,11 +230,6 @@
         parts = [packed[g * ghost_rows:(g + 1) * ghost_rows] for g in range(groups)]
         return shard_low, parts
 
-    def residual(prev, shard_low, ghosts):
-        return block_product(local_blocks, columns, prev[0, 0], shard_low, ghosts, ghost_count)[
-            None, None
-        ]
-
     grains = dof_count // 3
     factors = jnp.transpose(
         smoother[0, 0].reshape((3, 3, block_count, grains)), (2, 0, 1, 3)
@@ -248,16 +263,12 @@
     neighbour_tables = [
         a[ghost_rows:].reshape((ghost_count, coarse_rows, dof_count)) for a in arrived
     ]
-    residual_second = residual(residual_first, shard_low, arrived)
-    local_terms = jnp.einsum(
-        "knd,ndr->nkr",
-        shaped,
-        residual_second[0, 0].astype(jnp.bfloat16),
-        preferred_element_type=jnp.float32,
-    )
-    coarse_residual = jnp.einsum(
-        "an,nkr->akr", onehot, local_terms, precision=lax.Precision.HIGHEST
-    )
+    residual_second, coarse_residual = block_product(
+        local_blocks, columns, residual_first[0, 0], shard_low, arrived, ghost_count,
+        mode="restrict", send=agg_id[0, 0], prolong=jnp.transpose(shaped, (1, 0, 2)),
+        aggregates=aggregates,
+    )
+    residual_second = residual_second[None, None]
     coarse_rhs = coarse_residual.astype(jnp.bfloat16).reshape((coarse_rows, vectors))
     column_part = gathered_copies(coarse_rhs, "row")
     partial = coarse_product(held, column_part)

time: 150 us -> 150 us (level)
  matrix products: 6.12 us -> 4.27 us
  Pallas kernels: 23.7 us -> 25.2 us
    dot_general x2 -> x0, matrix products: 1.8 us -> none  [the longest x1 1.53 us: cycle(): jnp.einsum('knd,ndr->nkr', shaped, residual_second[0, 0].astype(jnp.bfloa...]
    unnamed x40 -> x44, local copies, waits for them, and re-layouts: 4.08 us -> 4.1 us
where the time goes in v9:
time: 150 us
  starting transfers between devices  51.8 us (35%)
  waiting for transfers between devices  41.6 us (28%)
  Pallas kernels  25.2 us (17%)
  local copies, waits for them, and re-layouts  20.2 us (13%)
  other arithmetic  6.11 us (4%)
  matrix products  4.27 us (3%)
    ppermute x12, starting transfers between devices, passed_along(): return lax.ppermute(value, axis, pairs)  35.1 us
    ppermute x12, waiting for transfers between devices, passed_along(): return lax.ppermute(value, axis, pairs)  29 us
    pallas_call x3, Pallas kernels, block_product(): pl.pallas_call(functools.partial(product_kernel, stored, rows, mode, len(...  23.3 us
    all_to_all x1, starting transfers between devices, gathered_copies(): return lax.all_to_all(repeated, axis, 0, 0, tiled=True)  11.2 us
    all_to_all x1, waiting for transfers between devices, gathered_copies(): return lax.all_to_all(repeated, axis, 0, 0, tiled=True)  8.44 us
    all_to_all x1, starting transfers between devices, cycle(): partial = lax.all_to_all(partial, 'col', 0, 0, tiled=True)  5.54 us
    all_to_all x1, waiting for transfers between devices, cycle(): partial = lax.all_to_all(partial, 'col', 0, 0, tiled=True)  4.16 us
    unnamed x44, local copies, waits for them, and re-layouts  4.1 us
  transfers between devices with their start and end apart: 14, of which 8 were waited for; matrix products, arithmetic and copies ran while one was open for 13% of the time, Pallas kernels for 0%

profile of v9, /device:TPU:1, one launch (start us, length us, event | category | flops | bytes accessed | tf_op | source)
XLA Modules:
  0.0 149.7 jit_solution(7989726642740685658)
XLA Ops:
  1.6 0.8 reshape.222
  2.4 2.9 %multiply_add_fusion.2 = (f32[1,1,12,1,64,128]{5,4,3,2,1,0:T(8,128)S(1)}, f32[1,1,12,1,64,128]{5,4,3,2,1,0:T(8,128)S(1)}, f32[1,1,12,1,64,128]{5,4,3,2,1,0:T(8,128)S(1)}) fusion(f32[1,1,12,3,64,128]{5,4,3,2,1,0:T(8,128)} %bitcast.118, f32[12,64]{1,0:T(8,128)S(1)} %get-tuple-element.49, f32[12,64]{1,0:T(8,128)S(1)} %get-tuple-element.50, ...), kind=kLoop, calls=%fused_computation.19 | loop fusion | flops 1474560 | bytes 2386944 | tf_op jit(solution)/shard_map/add | solution.py:31
  6.7 3.1 %collective-permute-start.2 = (bf16[768,128]{1,0:T(8,128)(2,1)S(1)}, bf16[768,128]{1,0:T(8,128)(2,1)S(1)}, u32[]{:S(2)}, u32[]{:S(2)}) collective-permute-start(bf16[768,128]{1,0:T(8,128)(2,1)S(1)} %bitcast.131), channel_id=1, source_target_pairs={{0,1},{1,2},{2,3},{3,4},{4,5},{5,6},{6,7},{7,0},{8,9},{9,10},{10,1... | collective-permute-start | bytes 589832 | tf_op jit(solution)/shard_map/ppermute | solution.py:17
  10.1 10.4 %collective-permute-start.1 = (bf16[768,128]{1,0:T(8,128)(2,1)S(1)}, bf16[768,128]{1,0:T(8,128)(2,1)S(1)}, u32[]{:S(2)}, u32[]{:S(2)}) collective-permute-start(bf16[768,128]{1,0:T(8,128)(2,1)S(1)} %bitcast.129), channel_id=1, source_target_pairs={{0,248},{8,0},{16,8},{24,16},{32,24},{40,32},{48,40},{56,48},{64,5... | collective-permute-start | bytes 589832 | tf_op jit(solution)/shard_map/ppermute | solution.py:17
  29.8 9.6 %collective-permute-done.rest_0_ = bf16[768,128]{1,0:T(8,128)(2,1)S(1)} collective-permute-done((bf16[768,128]{1,0:T(8,128)(2,1)S(1)}, bf16[768,128]{1,0:T(8,128)(2,1)S(1)}, u32[]{:S(2)}, u32[]{:S(2)}) %collective-permute-start) | collective-permute-done | bytes 196640 | tf_op jit(solution)/shard_map/ppermute | solution.py:17
  39.4 2.0 %broadcast_in_dim.54.rest_4_ = bf16[12,3,3,64,128]{4,3,2,1,0:T(8,128)(2,1)} broadcast(bf16[12,3,3,64]{3,2,1,0:T(4,128)(2,1)S(1)} %bitcast.132), dimensions={0,1,2,3} | broadcast | bytes 1783296 | tf_op jit(solution)/shard_map/broadcast_in_dim | solution.py:237
  41.4 8.2 %shard_map.82 = (f32[12,192,128]{2,1,0:T(8,128)}, f32[12,192,128]{2,1,0:T(8,128)}, bf16[12,192,128]{2,1,0:T(8,128)(2,1)}, bf16[912,128]{1,0:T(8,128)(2,1)}, bf16...) custom-call(s32[96]{0:T(128)} %reshape_squeeze.17.columns_ref, s32[16]{0:T(128)} %copy-done.20, ...), custom_call_target="tpu_custom_call" | custom-call | flops 905969664 | bytes 15925248 | tf_op jit(solution)/shard_map/pallas_call | solution.py:171
  49.6 9.6 %collective-permute-start.5 = (bf16[912,128]{1,0:T(8,128)(2,1)}, bf16[912,128]{1,0:T(8,128)(2,1)S(1)}, u32[]{:S(2)}, u32[]{:S(2)}) collective-permute-start(bf16[912,128]{1,0:T(8,128)(2,1)} %get-tuple-element.19), channel_id=1, source_target_pairs={{0,248},{8,0},{16,8},{24,16},{32,24},{40,32},{48,40},{56,48},{64,5... | collective-permute-start | bytes 700424 | tf_op jit(solution)/shard_map/ppermute | solution.py:17
  59.2 4.6 %collective-permute-start.6 = (bf16[912,128]{1,0:T(8,128)(2,1)}, bf16[912,128]{1,0:T(8,128)(2,1)S(1)}, u32[]{:S(2)}, u32[]{:S(2)}) collective-permute-start(bf16[912,128]{1,0:T(8,128)(2,1)} %get-tuple-element.20), channel_id=1, source_target_pairs={{0,1},{1,2},{2,3},{3,4},{4,5},{5,6},{6,7},{7,0},{8,9},{9,10},{10,1... | collective-permute-start | bytes 700424 | tf_op jit(solution)/shard_map/ppermute | solution.py:17
  63.8 2.5 %collective-permute-done.5.rest_1_ = bf16[912,128]{1,0:T(8,128)(2,1)S(1)} collective-permute-done((bf16[912,128]{1,0:T(8,128)(2,1)}, bf16[912,128]{1,0:T(8,128)(2,1)S(1)}, u32[]{:S(2)}, u32[]{:S(2)}) %collective-permute-start.5) | collective-permute-done | bytes 233504 | tf_op jit(solution)/shard_map/ppermute | solution.py:17
  66.3 9.3 %collective-permute-done.6.rest_2_ = bf16[912,128]{1,0:T(8,128)(2,1)S(1)} collective-permute-done((bf16[912,128]{1,0:T(8,128)(2,1)}, bf16[912,128]{1,0:T(8,128)(2,1)S(1)}, u32[]{:S(2)}, u32[]{:S(2)}) %collective-permute-start.6) | collective-permute-done | bytes 233504 | tf_op jit(solution)/shard_map/ppermute | solution.py:17
  75.6 3.9 %collective-permute-done.7.rest_3_ = bf16[912,128]{1,0:T(8,128)(2,1)S(1)} collective-permute-done((bf16[912,128]{1,0:T(8,128)(2,1)}, bf16[912,128]{1,0:T(8,128)(2,1)S(1)}, u32[]{:S(2)}, u32[]{:S(2)}) %collective-permute-start.7) | collective-permute-done | bytes 233504 | tf_op jit(solution)/shard_map/ppermute | solution.py:17
  80.2 7.9 %shard_map.83 = (f32[12,192,128]{2,1,0:T(8,128)}, f32[4,6,128]{2,1,0:T(8,128)}) custom-call(s32[96]{0:T(128)} %reshape_squeeze.17.columns_ref, s32[12]{0:T(128)} %bitcast.133, bf16[12,192,1536]{2,1,0:T(8,128)(2,1)} %bitcast.114, f32[12,192,128]{2,1,0:T(8,128)} %get-tuple-element.16.prev_ref, bf16[12,192,128]{2,1,0:T(8,128)(2,1)} %get-tuple-element.17.local_ref, ...), custom_call_target="tpu_custom_call" | custom-call | flops 905969664 | bytes 15925248 | tf_op jit(solution)/shard_map/pallas_call | solution.py:171
  89.5 11.2 %all-to-all-start = ((bf16[32,24,128]{2,1,0:T(8,128)(2,1)}), bf16[32,24,128]{2,1,0:T(8,128)(2,1)}, u32[]{:S(2)}, u32[]{:S(2)}) async-start(bf16[32,24,128]{2,1,0:T(8,128)(2,1)} %broadcast_in_dim.56), calls=%async_computation | async-start | bytes 393216 | tf_op jit(solution)/shard_map/all_to_all | solution.py:194
  100.7 3.0 %copy.29 = bf16[192,6144]{0,1:T(8,128)(2,1)S(1)} copy(bf16[192,6144]{1,0:T(8,128)(2,1)} %param.19) | data formatting | bytes 4718592 | tf_op args[7]
  103.8 0.9 copy.30.held_ref
  104.7 8.4 %all-to-all-done = bf16[32,24,128]{2,1,0:T(8,128)(2,1)} async-done(((bf16[32,24,128]{2,1,0:T(8,128)(2,1)}), bf16[32,24,128]{2,1,0:T(8,128)(2,1)}, u32[]{:S(2)}, u32[]{:S(2)}) %all-to-all-start) | async-done | bytes 196640 | tf_op jit(solution)/shard_map/all_to_all | solution.py:194
  113.1 1.9 %shard_map.84 = f32[192,128]{1,0:T(8,128)} custom-call(bf16[192,768]{1,0:T(8,128)(2,1)} %copy.30.held_ref, bf16[768,128]{1,0:T(8,128)(2,1)} %bitcast.44.part_ref), custom_call_target="tpu_custom_call" | custom-call | tf_op jit(solution)/shard_map/pallas_call | solution.py:184
  115.0 5.5 %all-to-all-start.1 = ((f32[8,24,128]{2,1,0:T(8,128)}), f32[8,24,128]{2,1,0:T(8,128)S(1)}, u32[]{:S(2)}, u32[]{:S(2)}) async-start(f32[8,24,128]{2,1,0:T(8,128)} %bitcast.127), calls=%async_computation.1 | async-start | bytes 196608 | tf_op jit(solution)/shard_map/all_to_all | solution.py:275
  120.5 0.8 slice.160
  121.7 4.2 %all-to-all-done.1 = f32[8,24,128]{2,1,0:T(8,128)S(1)} async-done(((f32[8,24,128]{2,1,0:T(8,128)}), f32[8,24,128]{2,1,0:T(8,128)S(1)}, u32[]{:S(2)}, u32[]{:S(2)}) %all-to-all-start.1) | async-done | bytes 98336 | tf_op jit(solution)/shard_map/all_to_all | solution.py:275
  125.9 1.5 collective-permute-start.10
  127.4 1.6 %collective-permute-start.9 = (bf16[24,128]{1,0:T(8,128)(2,1)S(1)}, bf16[24,128]{1,0:T(8,128)(2,1)S(1)}, u32[]{:S(2)}, u32[]{:S(2)}) collective-permute-start(bf16[24,128]{1,0:T(8,128)(2,1)S(1)} %reduce_sum.9), channel_id=1, source_target_pairs={{0,248},{8,0},{16,8},{24,16},{32,24},{40,32},{48,40},{56,48},{64,5... | collective-permute-start | bytes 18440 | tf_op jit(solution)/shard_map/ppermute | solution.py:17
  129.0 3.7 %collective-permute-start.8 = (bf16[24,128]{1,0:T(8,128)(2,1)S(1)}, bf16[24,128]{1,0:T(8,128)(2,1)S(1)}, u32[]{:S(2)}, u32[]{:S(2)}) collective-permute-start(bf16[24,128]{1,0:T(8,128)(2,1)S(1)} %reduce_sum.9), channel_id=1, source_target_pairs={{0,8},{8,16},{16,24},{24,32},{32,40},{40,48},{48,56},{56,64},{64,7... | collective-permute-start | bytes 18440 | tf_op jit(solution)/shard_map/ppermute | solution.py:17
  133.6 1.4 fusion.16
  135.0 0.9 collective-permute-done.11
  135.8 0.9 convolution_convert_fusion
  136.8 2.9 %collective-permute-done.8 = bf16[24,128]{1,0:T(8,128)(2,1)S(1)} collective-permute-done((bf16[24,128]{1,0:T(8,128)(2,1)S(1)}, bf16[24,128]{1,0:T(8,128)(2,1)S(1)}, u32[]{:S(2)}, u32[]{:S(2)}) %collective-permute-start.8) | collective-permute-done | bytes 6176 | tf_op jit(solution)/shard_map/ppermute | solution.py:17
  139.7 0.9 convolution_convert_fusion.3
  140.6 0.9 convolution_convert_fusion.2
  141.5 0.9 convolution_convert_fusion.1
  142.5 7.2 %shard_map.85 = f32[12,192,128]{2,1,0:T(8,128)} custom-call(s32[96]{0:T(128)} %reshape_squeeze.17.columns_ref, s32[1]{0:T(128)} %constant.9.clone.1.send_ref, bf16[12,192,1536]{2,1,0:T(8,128)(2,1)} %bitcast.115, f32[12,192,128]{2,1,0:T(8,128)} %get-tuple-element.22.prev_ref, bf16[12,192,128]{2,1,0:T(8,128)(2,1)} %get-tuple-element.34.local_ref, ...), custom_call_target="tpu_custom_call" | custom-call | flops 905969664 | bytes 15925248 | tf_op jit(solution)/shard_map/pallas_call | solution.py:171
  (114 shorter events, 15.8 us)
Async XLA Ops:
  6.6 13.8 %copy-start.16 = (s32[1,1,4,4]{3,2,1,0:T(4,128)S(1)}, s32[1,1,4,4]{3,2,1,0:T(4,128)}, u32[]{:S(2)}) copy-start(s32[1,1,4,4]{3,2,1,0:T(4,128)} %param.16) | copy-start | bytes 196
  6.6 13.9 %copy-start.14 = (bf16[1,1,3,3,768]{4,3,2,1,0:T(4,128)(2,1)S(1)}, bf16[1,1,3,3,768]{4,3,2,1,0:T(4,128)(2,1)}, u32[]{:S(2)}) copy-start(bf16[1,1,3,3,768]{4,3,2,1,0:T(4,128)(2,1)} %param.13) | copy-start | bytes 41476
  6.6 14.0 %copy-start.18 = (s32[1,1,12]{2,1,0:T(1,128)S(1)}, s32[1,1,12]{2,1,0:T(1,128)}, u32[]{:S(2)}) copy-start(s32[1,1,12]{2,1,0:T(1,128)} %param.17) | copy-start | bytes 148
  6.6 15.2 %copy-start.15 = (bf16[1,1,6,2304]{3,2,1,0:T(8,128)(2,1)S(1)}, bf16[1,1,6,2304]{3,2,1,0:T(8,128)(2,1)}, u32[]{:S(2)}) copy-start(bf16[1,1,6,2304]{3,2,1,0:T(8,128)(2,1)} %param.18) | copy-start | bytes 82948
  6.7 18.7 %copy-start.17 = (s32[1,1,12,8]{2,3,1,0:T(8,128)S(1)}, s32[1,1,12,8]{2,3,1,0:T(8,128)}, u32[]{:S(2)}) copy-start(s32[1,1,12,8]{2,3,1,0:T(8,128)} %param.15) | copy-start | bytes 1156
  6.7 23.0 %collective-permute-start.2 = (bf16[768,128]{1,0:T(8,128)(2,1)S(1)}, bf16[768,128]{1,0:T(8,128)(2,1)S(1)}, u32[]{:S(2)}, u32[]{:S(2)}) collective-permute-start(bf16[768,128]{1,0:T(8,128)(2,1)S(1)} %bitcast.131), channel_id=1, source_target_pairs={{0,1},{1,2},{2,3},{3,4},{4,5},{5,6},{6,7},{7,0},{8,9},{9,10},{10,1... | collective-permute-start | bytes 589832 | tf_op jit(solution)/shard_map/ppermute | solution.py:17
  9.8 19.9 %collective-permute-start.3 = (bf16[768,128]{1,0:T(8,128)(2,1)S(1)}, bf16[768,128]{1,0:T(8,128)(2,1)S(1)}, u32[]{:S(2)}, u32[]{:S(2)}) collective-permute-start(bf16[768,128]{1,0:T(8,128)(2,1)S(1)} %bitcast.130), channel_id=1, source_target_pairs={{0,7},{1,0},{2,1},{3,2},{4,3},{5,4},{6,5},{7,6},{8,15},{9,8},{10,9... | collective-permute-start | bytes 589832 | tf_op jit(solution)/shard_map/ppermute | solution.py:17
  10.1 19.7 %collective-permute-start.1 = (bf16[768,128]{1,0:T(8,128)(2,1)S(1)}, bf16[768,128]{1,0:T(8,128)(2,1)S(1)}, u32[]{:S(2)}, u32[]{:S(2)}) collective-permute-start(bf16[768,128]{1,0:T(8,128)(2,1)S(1)} %bitcast.129), channel_id=1, source_target_pairs={{0,248},{8,0},{16,8},{24,16},{32,24},{40,32},{48,40},{56,48},{64,5... | collective-permute-start | bytes 589832 | tf_op jit(solution)/shard_map/ppermute | solution.py:17
  20.5 18.9 %collective-permute-start = (bf16[768,128]{1,0:T(8,128)(2,1)S(1)}, bf16[768,128]{1,0:T(8,128)(2,1)S(1)}, u32[]{:S(2)}, u32[]{:S(2)}) collective-permute-start(bf16[768,128]{1,0:T(8,128)(2,1)S(1)} %bitcast.128), channel_id=1, source_target_pairs={{0,8},{8,16},{16,24},{24,32},{32,40},{40,48},{48,56},{56,64},{64,7... | collective-permute-start | bytes 589832 | tf_op jit(solution)/shard_map/ppermute | solution.py:17
  22.0 19.4 %copy-start.4 = (bf16[6,12,192]{2,1,0:T(8,128)(2,1)}, bf16[6,12,192]{2,1,0:T(8,128)(2,1)S(1)}, u32[]{:S(2)}) copy-start(bf16[6,12,192]{2,1,0:T(8,128)(2,1)S(1)} %reshape_squeeze.21) | copy-start | bytes 82948
  22.0 19.3 %copy-start.3 = (bf16[6,12,192]{2,0,1:T(8,128)(2,1)}, bf16[6,12,192]{2,0,1:T(8,128)(2,1)S(1)}, u32[]{:S(2)}) copy-start(bf16[6,12,192]{2,0,1:T(8,128)(2,1)S(1)} %copy.47) | copy-start | bytes 82948
  29.7 11.6 %copy-start.10 = (bf16[768,128]{1,0:T(8,128)(2,1)}, bf16[768,128]{1,0:T(8,128)(2,1)S(1)}, u32[]{:S(2)}) copy-start(bf16[768,128]{1,0:T(8,128)(2,1)S(1)} %collective-permute-done.2.rest_2_) | copy-start | bytes 589828
  29.7 11.6 %copy-start.11 = (bf16[768,128]{1,0:T(8,128)(2,1)}, bf16[768,128]{1,0:T(8,128)(2,1)S(1)}, u32[]{:S(2)}) copy-start(bf16[768,128]{1,0:T(8,128)(2,1)S(1)} %collective-permute-done.3.rest_3_) | copy-start | bytes 589828
  29.8 11.6 %copy-start.12 = (bf16[768,128]{1,0:T(8,128)(2,1)}, bf16[768,128]{1,0:T(8,128)(2,1)S(1)}, u32[]{:S(2)}) copy-start(bf16[768,128]{1,0:T(8,128)(2,1)S(1)} %collective-permute-done.1.rest_1_) | copy-start | bytes 589828
  49.5 14.3 %collective-permute-start.4 = (bf16[912,128]{1,0:T(8,128)(2,1)}, bf16[912,128]{1,0:T(8,128)(2,1)S(1)}, u32[]{:S(2)}, u32[]{:S(2)}) collective-permute-start(bf16[912,128]{1,0:T(8,128)(2,1)} %get-tuple-element.18), channel_id=1, source_target_pairs={{0,8},{8,16},{16,24},{24,32},{32,40},{40,48},{48,56},{56,64},{64,7... | collective-permute-start | bytes 700424 | tf_op jit(solution)/shard_map/ppermute | solution.py:17
  49.6 16.7 %collective-permute-start.5 = (bf16[912,128]{1,0:T(8,128)(2,1)}, bf16[912,128]{1,0:T(8,128)(2,1)S(1)}, u32[]{:S(2)}, u32[]{:S(2)}) collective-permute-start(bf16[912,128]{1,0:T(8,128)(2,1)} %get-tuple-element.19), channel_id=1, source_target_pairs={{0,248},{8,0},{16,8},{24,16},{32,24},{40,32},{48,40},{56,48},{64,5... | collective-permute-start | bytes 700424 | tf_op jit(solution)/shard_map/ppermute | solution.py:17
  59.2 16.4 %collective-permute-start.6 = (bf16[912,128]{1,0:T(8,128)(2,1)}, bf16[912,128]{1,0:T(8,128)(2,1)S(1)}, u32[]{:S(2)}, u32[]{:S(2)}) collective-permute-start(bf16[912,128]{1,0:T(8,128)(2,1)} %get-tuple-element.20), channel_id=1, source_target_pairs={{0,1},{1,2},{2,3},{3,4},{4,5},{5,6},{6,7},{7,0},{8,9},{9,10},{10,1... | collective-permute-start | bytes 700424 | tf_op jit(solution)/shard_map/ppermute | solution.py:17
  63.8 15.6 %collective-permute-start.7 = (bf16[912,128]{1,0:T(8,128)(2,1)}, bf16[912,128]{1,0:T(8,128)(2,1)S(1)}, u32[]{:S(2)}, u32[]{:S(2)}) collective-permute-start(bf16[912,128]{1,0:T(8,128)(2,1)} %get-tuple-element.21), channel_id=1, source_target_pairs={{0,7},{1,0},{2,1},{3,2},{4,3},{5,4},{6,5},{7,6},{8,15},{9,8},{10,9... | collective-permute-start | bytes 700424 | tf_op jit(solution)/shard_map/ppermute | solution.py:17
  63.8 15.6 %copy-start.6 = (bf16[912,128]{1,0:T(8,128)(2,1)}, bf16[912,128]{1,0:T(8,128)(2,1)S(1)}, u32[]{:S(2)}) copy-start(bf16[912,128]{1,0:T(8,128)(2,1)S(1)} %collective-permute-done.4.rest_0_) | copy-start | bytes 700420
  66.3 13.2 %copy-start.7 = (bf16[912,128]{1,0:T(8,128)(2,1)}, bf16[912,128]{1,0:T(8,128)(2,1)S(1)}, u32[]{:S(2)}) copy-start(bf16[912,128]{1,0:T(8,128)(2,1)S(1)} %collective-permute-done.5.rest_1_) | copy-start | bytes 700420
  89.5 23.6 %all-to-all-start = ((bf16[32,24,128]{2,1,0:T(8,128)(2,1)}), bf16[32,24,128]{2,1,0:T(8,128)(2,1)}, u32[]{:S(2)}, u32[]{:S(2)}) async-start(bf16[32,24,128]{2,1,0:T(8,128)(2,1)} %broadcast_in_dim.56), calls=%async_computation | async-start | bytes 393216 | tf_op jit(solution)/shard_map/all_to_all | solution.py:194
  103.8 17.6 %slice-start = ((bf16[912,128]{1,0:T(8,128)(2,1)}), bf16[144,128]{1,0:T(8,128)(2,1)S(1)}, s32[]{:S(2)}) async-start(bf16[912,128]{1,0:T(8,128)(2,1)} %copy-done.7), calls=%async_computation.2 | async-start | bytes 73728 | tf_op jit(solution)/shard_map/slice | solution.py:264
  103.8 17.7 %slice-start.1 = ((bf16[912,128]{1,0:T(8,128)(2,1)}), bf16[144,128]{1,0:T(8,128)(2,1)S(1)}, s32[]{:S(2)}) async-start(bf16[912,128]{1,0:T(8,128)(2,1)} %copy-done.8), calls=%async_computation.3 | async-start | bytes 73728 | tf_op jit(solution)/shard_map/slice | solution.py:264
  103.8 17.8 %slice-start.2 = ((bf16[912,128]{1,0:T(8,128)(2,1)}), bf16[144,128]{1,0:T(8,128)(2,1)S(1)}, s32[]{:S(2)}) async-start(bf16[912,128]{1,0:T(8,128)(2,1)} %copy-done.9), calls=%async_computation.4 | async-start | bytes 73728 | tf_op jit(solution)/shard_map/slice | solution.py:264
  103.8 29.2 %copy-start.19 = (s32[1,1,12]{2,1,0:T(1,128)S(1)}, s32[1,1,12]{2,1,0:T(1,128)}, u32[]{:S(2)}) copy-start(s32[1,1,12]{2,1,0:T(1,128)} %param.17) | copy-start | bytes 148
  103.8 29.4 %copy-start.5 = (bf16[6,12,192]{2,1,0:T(8,128)(2,1)S(1)}, bf16[6,12,192]{2,1,0:T(8,128)(2,1)}, u32[]{:S(2)}) copy-start(bf16[6,12,192]{2,1,0:T(8,128)(2,1)} %copy-done.4) | copy-start | bytes 82948
  115.0 18.6 %copy-start.2 = (f32[12,192,128]{2,1,0:T(8,128)S(1)}, f32[12,192,128]{2,1,0:T(8,128)}, u32[]{:S(2)}) copy-start(f32[12,192,128]{2,1,0:T(8,128)} %get-tuple-element.24) | copy-start | bytes 3538948
  115.0 10.9 %all-to-all-start.1 = ((f32[8,24,128]{2,1,0:T(8,128)}), f32[8,24,128]{2,1,0:T(8,128)S(1)}, u32[]{:S(2)}, u32[]{:S(2)}) async-start(f32[8,24,128]{2,1,0:T(8,128)} %bitcast.127), calls=%async_computation.1 | async-start | bytes 196608 | tf_op jit(solution)/shard_map/all_to_all | solution.py:275
  125.9 15.6 %collective-permute-start.10 = (bf16[24,128]{1,0:T(8,128)(2,1)S(1)}, bf16[24,128]{1,0:T(8,128)(2,1)S(1)}, u32[]{:S(2)}, u32[]{:S(2)}) collective-permute-start(bf16[24,128]{1,0:T(8,128)(2,1)S(1)} %reduce_sum.9), channel_id=1, source_target_pairs={{0,1},{1,2},{2,3},{3,4},{4,5},{5,6},{6,7},{7,0},{8,9},{9,10},{10,1... | collective-permute-start | bytes 18440 | tf_op jit(solution)/shard_map/ppermute | solution.py:17
  127.4 13.2 %collective-permute-start.9 = (bf16[24,128]{1,0:T(8,128)(2,1)S(1)}, bf16[24,128]{1,0:T(8,128)(2,1)S(1)}, u32[]{:S(2)}, u32[]{:S(2)}) collective-permute-start(bf16[24,128]{1,0:T(8,128)(2,1)S(1)} %reduce_sum.9), channel_id=1, source_target_pairs={{0,248},{8,0},{16,8},{24,16},{32,24},{40,32},{48,40},{56,48},{64,5... | collective-permute-start | bytes 18440 | tf_op jit(solution)/shard_map/ppermute | solution.py:17
  129.0 10.6 %collective-permute-start.8 = (bf16[24,128]{1,0:T(8,128)(2,1)S(1)}, bf16[24,128]{1,0:T(8,128)(2,1)S(1)}, u32[]{:S(2)}, u32[]{:S(2)}) collective-permute-start(bf16[24,128]{1,0:T(8,128)(2,1)S(1)} %reduce_sum.9), channel_id=1, source_target_pairs={{0,8},{8,16},{16,24},{24,32},{32,40},{40,48},{48,56},{56,64},{64,7... | collective-permute-start | bytes 18440 | tf_op jit(solution)/shard_map/ppermute | solution.py:17
  132.8 3.1 %collective-permute-start.11 = (bf16[24,128]{1,0:T(8,128)(2,1)S(1)}, bf16[24,128]{1,0:T(8,128)(2,1)S(1)}, u32[]{:S(2)}, u32[]{:S(2)}) collective-permute-start(bf16[24,128]{1,0:T(8,128)(2,1)S(1)} %reduce_sum.9), channel_id=1, source_target_pairs={{0,7},{1,0},{2,1},{3,2},{4,3},{5,4},{6,5},{7,6},{8,15},{9,8},{10,9... | collective-permute-start | bytes 18440 | tf_op jit(solution)/shard_map/ppermute | solution.py:17
  (6 other events, 13.3 us)

commit v10 on v8

--- a/solution.py
+++ b/solution.py
@@ -245,18 +245,16 @@
     )
     held = lax.dynamic_slice_in_dim(held, lax.axis_index("col"), 1, 2)
     held = held.reshape((coarse_inverse.shape[0], row_count * coarse_rows))
+    restrict = onehot.astype(jnp.bfloat16)[:, None, :, None] * shaped[None, :, :, :]
+    restrict = restrict.reshape((coarse_rows, block_count * dof_count))
     neighbour_tables = [
         a[ghost_rows:].reshape((ghost_count, coarse_rows, dof_count)) for a in arrived
     ]
     residual_second = residual(residual_first, shard_low, arrived)
-    local_terms = jnp.einsum(
-        "knd,ndr->nkr",
-        shaped,
-        residual_second[0, 0].astype(jnp.bfloat16),
+    coarse_residual = jnp.dot(
+        restrict,
+        residual_second[0, 0].astype(jnp.bfloat16).reshape((block_count * dof_count, vectors)),
         preferred_element_type=jnp.float32,
-    )
-    coarse_residual = jnp.einsum(
-        "an,nkr->akr", onehot, local_terms, precision=lax.Precision.HIGHEST
     )
     coarse_rhs = coarse_residual.astype(jnp.bfloat16).reshape((coarse_rows, vectors))
     column_part = gathered_copies(coarse_rhs, "row")

time: 150 us -> 150 us (level)
  matrix products: 6.12 us -> 4.52 us
    dot_general x2 -> x1, matrix products: 1.8 us -> 0.2 us  [cycle(): jnp.dot(restrict, residual_second[0, 0].astype(jnp.bfloat16).reshape((blo...]
    unnamed x40 -> x38, local copies, waits for them, and re-layouts: 4.08 us -> 4.08 us
where the time goes in v10:
time: 150 us; the launch traced here: 149 us
  starting transfers between devices  51.8 us (35%)
  waiting for transfers between devices  41.2 us (27%)
  Pallas kernels  23.7 us (16%)
  local copies, waits for them, and re-layouts  20.5 us (14%)
  other arithmetic  6.84 us (5%)
  matrix products  4.52 us (3%)
    ppermute x12, starting transfers between devices, passed_along(): return lax.ppermute(value, axis, pairs)  35.1 us
    ppermute x12, waiting for transfers between devices, passed_along(): return lax.ppermute(value, axis, pairs)  28.6 us
    pallas_call x3, Pallas kernels, block_product(): pl.pallas_call(functools.partial(product_kernel, stored, rows, mode, len(...  21.9 us
    all_to_all x1, starting transfers between devices, gathered_copies(): return lax.all_to_all(repeated, axis, 0, 0, tiled=True)  11.1 us
    all_to_all x1, waiting for transfers between devices, gathered_copies(): return lax.all_to_all(repeated, axis, 0, 0, tiled=True)  8.45 us
    all_to_all x1, starting transfers between devices, cycle(): partial = lax.all_to_all(partial, 'col', 0, 0, tiled=True)  5.54 us
    all_to_all x1, waiting for transfers between devices, cycle(): partial = lax.all_to_all(partial, 'col', 0, 0, tiled=True)  4.16 us
    unnamed x38, local copies, waits for them, and re-layouts  4.08 us
  transfers between devices with their start and end apart: 14, of which 8 were waited for; matrix products, arithmetic and copies ran while one was open for 13% of the time, Pallas kernels for 0%

profile of v10, /device:TPU:1, one launch (start us, length us, event | category | flops | bytes accessed | tf_op | source)
XLA Modules:
  0.0 149.1 jit_solution(18382817956011090152)
XLA Ops:
  1.6 0.8 reshape.262
  2.4 2.9 %multiply_add_fusion.2 = (f32[1,1,12,1,64,128]{5,4,3,2,1,0:T(8,128)S(1)}, f32[1,1,12,1,64,128]{5,4,3,2,1,0:T(8,128)S(1)}, f32[1,1,12,1,64,128]{5,4,3,2,1,0:T(8,128)S(1)}) fusion(f32[1,1,12,3,64,128]{5,4,3,2,1,0:T(8,128)} %bitcast.118, f32[12,64]{1,0:T(8,128)S(1)} %get-tuple-element.45, f32[12,64]{1,0:T(8,128)S(1)} %get-tuple-element.46, ...), kind=kLoop, calls=%fused_computation.20 | loop fusion | flops 1474560 | bytes 2386944 | tf_op jit(solution)/shard_map/add | solution.py:31
  6.7 3.1 %collective-permute-start.2 = (bf16[768,128]{1,0:T(8,128)(2,1)S(1)}, bf16[768,128]{1,0:T(8,128)(2,1)S(1)}, u32[]{:S(2)}, u32[]{:S(2)}) collective-permute-start(bf16[768,128]{1,0:T(8,128)(2,1)S(1)} %bitcast.131), channel_id=1, source_target_pairs={{0,1},{1,2},{2,3},{3,4},{4,5},{5,6},{6,7},{7,0},{8,9},{9,10},{10,1... | collective-permute-start | bytes 589832 | tf_op jit(solution)/shard_map/ppermute | solution.py:17
  10.1 10.4 %collective-permute-start.1 = (bf16[768,128]{1,0:T(8,128)(2,1)S(1)}, bf16[768,128]{1,0:T(8,128)(2,1)S(1)}, u32[]{:S(2)}, u32[]{:S(2)}) collective-permute-start(bf16[768,128]{1,0:T(8,128)(2,1)S(1)} %bitcast.129), channel_id=1, source_target_pairs={{0,248},{8,0},{16,8},{24,16},{32,24},{40,32},{48,40},{56,48},{64,5... | collective-permute-start | bytes 589832 | tf_op jit(solution)/shard_map/ppermute | solution.py:17
  29.8 9.6 %collective-permute-done.rest_0_ = bf16[768,128]{1,0:T(8,128)(2,1)S(1)} collective-permute-done((bf16[768,128]{1,0:T(8,128)(2,1)S(1)}, bf16[768,128]{1,0:T(8,128)(2,1)S(1)}, u32[]{:S(2)}, u32[]{:S(2)}) %collective-permute-start) | collective-permute-done | bytes 196640 | tf_op jit(solution)/shard_map/ppermute | solution.py:17
  39.4 2.0 %broadcast_in_dim.33.rest_4_ = bf16[12,3,3,64,128]{4,3,2,1,0:T(8,128)(2,1)} broadcast(bf16[12,3,3,64]{3,2,1,0:T(4,128)(2,1)S(1)} %bitcast.132), dimensions={0,1,2,3} | broadcast | bytes 1783296 | tf_op jit(solution)/shard_map/broadcast_in_dim | solution.py:222
  41.3 8.2 %shard_map.82 = (f32[12,192,128]{2,1,0:T(8,128)}, f32[12,192,128]{2,1,0:T(8,128)}, bf16[12,192,128]{2,1,0:T(8,128)(2,1)}, bf16[912,128]{1,0:T(8,128)(2,1)}, bf16...) custom-call(s32[96]{0:T(128)} %reshape_squeeze.17.columns_ref, s32[16]{0:T(128)} %copy-done.16, ...), custom_call_target="tpu_custom_call" | custom-call | flops 905969664 | bytes 15925248 | tf_op jit(solution)/shard_map/pallas_call | solution.py:151
  49.6 9.6 %collective-permute-start.5 = (bf16[912,128]{1,0:T(8,128)(2,1)}, bf16[912,128]{1,0:T(8,128)(2,1)S(1)}, u32[]{:S(2)}, u32[]{:S(2)}) collective-permute-start(bf16[912,128]{1,0:T(8,128)(2,1)} %get-tuple-element.17), channel_id=1, source_target_pairs={{0,248},{8,0},{16,8},{24,16},{32,24},{40,32},{48,40},{56,48},{64,5... | collective-permute-start | bytes 700424 | tf_op jit(solution)/shard_map/ppermute | solution.py:17
  59.2 4.6 %collective-permute-start.6 = (bf16[912,128]{1,0:T(8,128)(2,1)}, bf16[912,128]{1,0:T(8,128)(2,1)S(1)}, u32[]{:S(2)}, u32[]{:S(2)}) collective-permute-start(bf16[912,128]{1,0:T(8,128)(2,1)} %get-tuple-element.18), channel_id=1, source_target_pairs={{0,1},{1,2},{2,3},{3,4},{4,5},{5,6},{6,7},{7,0},{8,9},{9,10},{10,1... | collective-permute-start | bytes 700424 | tf_op jit(solution)/shard_map/ppermute | solution.py:17
  64.2 2.2 %collective-permute-done.5.rest_1_ = bf16[912,128]{1,0:T(8,128)(2,1)S(1)} collective-permute-done((bf16[912,128]{1,0:T(8,128)(2,1)}, bf16[912,128]{1,0:T(8,128)(2,1)S(1)}, u32[]{:S(2)}, u32[]{:S(2)}) %collective-permute-start.5) | collective-permute-done | bytes 233504 | tf_op jit(solution)/shard_map/ppermute | solution.py:17
  66.4 9.1 %collective-permute-done.6.rest_2_ = bf16[912,128]{1,0:T(8,128)(2,1)S(1)} collective-permute-done((bf16[912,128]{1,0:T(8,128)(2,1)}, bf16[912,128]{1,0:T(8,128)(2,1)S(1)}, u32[]{:S(2)}, u32[]{:S(2)}) %collective-permute-start.6) | collective-permute-done | bytes 233504 | tf_op jit(solution)/shard_map/ppermute | solution.py:17
  75.5 3.9 %collective-permute-done.7.rest_3_ = bf16[912,128]{1,0:T(8,128)(2,1)S(1)} collective-permute-done((bf16[912,128]{1,0:T(8,128)(2,1)}, bf16[912,128]{1,0:T(8,128)(2,1)S(1)}, u32[]{:S(2)}, u32[]{:S(2)}) %collective-permute-start.7) | collective-permute-done | bytes 233504 | tf_op jit(solution)/shard_map/ppermute | solution.py:17
  80.1 6.5 %shard_map.83.prev_ref = f32[12,192,128]{2,1,0:T(8,128)} custom-call(s32[96]{0:T(128)} %reshape_squeeze.17.columns_ref, s32[1]{0:T(128)} %constant.9.clone.1.send_ref, bf16[12,192,1536]{2,1,0:T(8,128)(2,1)} %bitcast.114, f32[12,192,128]{2,1,0:T(8,128)} %get-tuple-element.14.prev_ref, bf16[12,192,128]{2,1,0:T(8,128)(2,1)} %get-tuple-element.15.local_ref, ...), custom_call_target="tpu_custom_call" | custom-call | flops 905969664 | bytes 11206656 | tf_op jit(solution)/shard_map/pallas_call | solution.py:151
  86.6 1.4 convert_element_type.73
  88.9 11.1 %all-to-all-start = ((bf16[32,24,128]{2,1,0:T(8,128)(2,1)}), bf16[32,24,128]{2,1,0:T(8,128)(2,1)}, u32[]{:S(2)}, u32[]{:S(2)}) async-start(bf16[32,24,128]{2,1,0:T(8,128)(2,1)} %broadcast_in_dim.34), calls=%async_computation | async-start | bytes 393216 | tf_op jit(solution)/shard_map/all_to_all | solution.py:174
  100.1 3.0 %copy.30 = bf16[192,6144]{0,1:T(8,128)(2,1)S(1)} copy(bf16[192,6144]{1,0:T(8,128)(2,1)} %param.19) | data formatting | bytes 4718592 | tf_op args[7]
  103.2 0.9 copy.32.held_ref
  104.0 8.5 %all-to-all-done = bf16[32,24,128]{2,1,0:T(8,128)(2,1)} async-done(((bf16[32,24,128]{2,1,0:T(8,128)(2,1)}), bf16[32,24,128]{2,1,0:T(8,128)(2,1)}, u32[]{:S(2)}, u32[]{:S(2)}) %all-to-all-start) | async-done | bytes 196640 | tf_op jit(solution)/shard_map/all_to_all | solution.py:174
  112.5 1.9 %shard_map.84 = f32[192,128]{1,0:T(8,128)} custom-call(bf16[192,768]{1,0:T(8,128)(2,1)} %copy.32.held_ref, bf16[768,128]{1,0:T(8,128)(2,1)} %bitcast.44.part_ref), custom_call_target="tpu_custom_call" | custom-call | tf_op jit(solution)/shard_map/pallas_call | solution.py:164
  114.4 5.5 %all-to-all-start.1 = ((f32[8,24,128]{2,1,0:T(8,128)}), f32[8,24,128]{2,1,0:T(8,128)S(1)}, u32[]{:S(2)}, u32[]{:S(2)}) async-start(f32[8,24,128]{2,1,0:T(8,128)} %bitcast.127), calls=%async_computation.1 | async-start | bytes 196608 | tf_op jit(solution)/shard_map/all_to_all | solution.py:262
  121.1 4.2 %all-to-all-done.1 = f32[8,24,128]{2,1,0:T(8,128)S(1)} async-done(((f32[8,24,128]{2,1,0:T(8,128)}), f32[8,24,128]{2,1,0:T(8,128)S(1)}, u32[]{:S(2)}, u32[]{:S(2)}) %all-to-all-start.1) | async-done | bytes 98336 | tf_op jit(solution)/shard_map/all_to_all | solution.py:262
  125.3 1.5 collective-permute-start.10
  126.8 1.7 %collective-permute-start.9 = (bf16[24,128]{1,0:T(8,128)(2,1)S(1)}, bf16[24,128]{1,0:T(8,128)(2,1)S(1)}, u32[]{:S(2)}, u32[]{:S(2)}) collective-permute-start(bf16[24,128]{1,0:T(8,128)(2,1)S(1)} %reduce_sum.9), channel_id=1, source_target_pairs={{0,248},{8,0},{16,8},{24,16},{32,24},{40,32},{48,40},{56,48},{64,5... | collective-permute-start | bytes 18440 | tf_op jit(solution)/shard_map/ppermute | solution.py:17
  128.4 3.7 %collective-permute-start.8 = (bf16[24,128]{1,0:T(8,128)(2,1)S(1)}, bf16[24,128]{1,0:T(8,128)(2,1)S(1)}, u32[]{:S(2)}, u32[]{:S(2)}) collective-permute-start(bf16[24,128]{1,0:T(8,128)(2,1)S(1)} %reduce_sum.9), channel_id=1, source_target_pairs={{0,8},{8,16},{16,24},{24,32},{32,40},{40,48},{48,56},{56,64},{64,7... | collective-permute-start | bytes 18440 | tf_op jit(solution)/shard_map/ppermute | solution.py:17
  133.0 1.4 fusion.16
  134.3 0.9 collective-permute-done.11
  135.2 0.9 convolution_convert_fusion
  136.1 2.9 %collective-permute-done.8 = bf16[24,128]{1,0:T(8,128)(2,1)S(1)} collective-permute-done((bf16[24,128]{1,0:T(8,128)(2,1)S(1)}, bf16[24,128]{1,0:T(8,128)(2,1)S(1)}, u32[]{:S(2)}, u32[]{:S(2)}) %collective-permute-start.8) | collective-permute-done | bytes 6176 | tf_op jit(solution)/shard_map/ppermute | solution.py:17
  139.0 0.9 convolution_convert_fusion.3
  140.0 0.9 convolution_convert_fusion.2
  140.9 0.9 convolution_convert_fusion.1
  141.9 7.2 %shard_map.85 = f32[12,192,128]{2,1,0:T(8,128)} custom-call(s32[96]{0:T(128)} %reshape_squeeze.17.columns_ref, s32[1]{0:T(128)} %constant.9.clone.1.send_ref, bf16[12,192,1536]{2,1,0:T(8,128)(2,1)} %bitcast.115, f32[12,192,128]{2,1,0:T(8,128)} %shard_map.83.prev_ref, bf16[12,192,128]{2,1,0:T(8,128)(2,1)} %get-tuple-element.30.local_ref, ...), custom_call_target="tpu_custom_call" | custom-call | flops 905969664 | bytes 15925248 | tf_op jit(solution)/shard_map/pallas_call | solution.py:151
  (111 shorter events, 16.4 us)
Async XLA Ops:
  0.8 4.5 %copy-start.16 = (s32[16]{0:T(128)}, s32[16]{0:T(128)S(1)}, u32[]{:S(2)}) copy-start(s32[16]{0:T(128)S(1)} %reshape_squeeze.18.send_ref) | copy-start | bytes 196
  6.6 13.9 %copy-start.14 = (s32[1,1,4,4]{3,2,1,0:T(4,128)S(1)}, s32[1,1,4,4]{3,2,1,0:T(4,128)}, u32[]{:S(2)}) copy-start(s32[1,1,4,4]{3,2,1,0:T(4,128)} %param.16) | copy-start | bytes 196
  6.6 13.9 %copy-start.12 = (bf16[1,1,3,3,768]{4,3,2,1,0:T(4,128)(2,1)S(1)}, bf16[1,1,3,3,768]{4,3,2,1,0:T(4,128)(2,1)}, u32[]{:S(2)}) copy-start(bf16[1,1,3,3,768]{4,3,2,1,0:T(4,128)(2,1)} %param.13) | copy-start | bytes 41476
  6.6 14.0 %copy-start.17 = (s32[1,1,12]{2,1,0:T(1,128)S(1)}, s32[1,1,12]{2,1,0:T(1,128)}, u32[]{:S(2)}) copy-start(s32[1,1,12]{2,1,0:T(1,128)} %param.17) | copy-start | bytes 148
  6.6 15.2 %copy-start.13 = (bf16[1,1,6,2304]{3,2,1,0:T(8,128)(2,1)S(1)}, bf16[1,1,6,2304]{3,2,1,0:T(8,128)(2,1)}, u32[]{:S(2)}) copy-start(bf16[1,1,6,2304]{3,2,1,0:T(8,128)(2,1)} %param.18) | copy-start | bytes 82948
  6.7 18.7 %copy-start.15 = (s32[1,1,12,8]{2,3,1,0:T(8,128)S(1)}, s32[1,1,12,8]{2,3,1,0:T(8,128)}, u32[]{:S(2)}) copy-start(s32[1,1,12,8]{2,3,1,0:T(8,128)} %param.15) | copy-start | bytes 1156
  6.7 23.0 %collective-permute-start.2 = (bf16[768,128]{1,0:T(8,128)(2,1)S(1)}, bf16[768,128]{1,0:T(8,128)(2,1)S(1)}, u32[]{:S(2)}, u32[]{:S(2)}) collective-permute-start(bf16[768,128]{1,0:T(8,128)(2,1)S(1)} %bitcast.131), channel_id=1, source_target_pairs={{0,1},{1,2},{2,3},{3,4},{4,5},{5,6},{6,7},{7,0},{8,9},{9,10},{10,1... | collective-permute-start | bytes 589832 | tf_op jit(solution)/shard_map/ppermute | solution.py:17
  9.8 20.0 %collective-permute-start.3 = (bf16[768,128]{1,0:T(8,128)(2,1)S(1)}, bf16[768,128]{1,0:T(8,128)(2,1)S(1)}, u32[]{:S(2)}, u32[]{:S(2)}) collective-permute-start(bf16[768,128]{1,0:T(8,128)(2,1)S(1)} %bitcast.130), channel_id=1, source_target_pairs={{0,7},{1,0},{2,1},{3,2},{4,3},{5,4},{6,5},{7,6},{8,15},{9,8},{10,9... | collective-permute-start | bytes 589832 | tf_op jit(solution)/shard_map/ppermute | solution.py:17
  10.1 19.7 %collective-permute-start.1 = (bf16[768,128]{1,0:T(8,128)(2,1)S(1)}, bf16[768,128]{1,0:T(8,128)(2,1)S(1)}, u32[]{:S(2)}, u32[]{:S(2)}) collective-permute-start(bf16[768,128]{1,0:T(8,128)(2,1)S(1)} %bitcast.129), channel_id=1, source_target_pairs={{0,248},{8,0},{16,8},{24,16},{32,24},{40,32},{48,40},{56,48},{64,5... | collective-permute-start | bytes 589832 | tf_op jit(solution)/shard_map/ppermute | solution.py:17
  20.5 18.9 %collective-permute-start = (bf16[768,128]{1,0:T(8,128)(2,1)S(1)}, bf16[768,128]{1,0:T(8,128)(2,1)S(1)}, u32[]{:S(2)}, u32[]{:S(2)}) collective-permute-start(bf16[768,128]{1,0:T(8,128)(2,1)S(1)} %bitcast.128), channel_id=1, source_target_pairs={{0,8},{8,16},{16,24},{24,32},{32,40},{40,48},{48,56},{56,64},{64,7... | collective-permute-start | bytes 589832 | tf_op jit(solution)/shard_map/ppermute | solution.py:17
  22.0 42.0 %copy-start.3 = (bf16[6,12,192]{2,1,0:T(8,128)(2,1)}, bf16[6,12,192]{2,1,0:T(8,128)(2,1)S(1)}, u32[]{:S(2)}) copy-start(bf16[6,12,192]{2,1,0:T(8,128)(2,1)S(1)} %reshape_squeeze.21) | copy-start | bytes 82948
  29.8 11.6 %copy-start.8 = (bf16[768,128]{1,0:T(8,128)(2,1)}, bf16[768,128]{1,0:T(8,128)(2,1)S(1)}, u32[]{:S(2)}) copy-start(bf16[768,128]{1,0:T(8,128)(2,1)S(1)} %collective-permute-done.2.rest_2_) | copy-start | bytes 589828
  29.8 11.6 %copy-start.9 = (bf16[768,128]{1,0:T(8,128)(2,1)}, bf16[768,128]{1,0:T(8,128)(2,1)S(1)}, u32[]{:S(2)}) copy-start(bf16[768,128]{1,0:T(8,128)(2,1)S(1)} %collective-permute-done.3.rest_3_) | copy-start | bytes 589828
  29.8 11.5 %copy-start.10 = (bf16[768,128]{1,0:T(8,128)(2,1)}, bf16[768,128]{1,0:T(8,128)(2,1)S(1)}, u32[]{:S(2)}) copy-start(bf16[768,128]{1,0:T(8,128)(2,1)S(1)} %collective-permute-done.1.rest_1_) | copy-start | bytes 589828
  39.4 2.0 %copy-start.11 = (bf16[768,128]{1,0:T(8,128)(2,1)}, bf16[768,128]{1,0:T(8,128)(2,1)S(1)}, u32[]{:S(2)}) copy-start(bf16[768,128]{1,0:T(8,128)(2,1)S(1)} %collective-permute-done.rest_0_) | copy-start | bytes 589828
  49.5 14.7 %collective-permute-start.4 = (bf16[912,128]{1,0:T(8,128)(2,1)}, bf16[912,128]{1,0:T(8,128)(2,1)}, u32[]{:S(2)}, u32[]{:S(2)}) collective-permute-start(bf16[912,128]{1,0:T(8,128)(2,1)} %get-tuple-element.16), channel_id=1, source_target_pairs={{0,8},{8,16},{16,24},{24,32},{32,40},{40,48},{48,56},{56,64},{64,7... | collective-permute-start | bytes 700424 | tf_op jit(solution)/shard_map/ppermute | solution.py:17
  49.6 16.8 %collective-permute-start.5 = (bf16[912,128]{1,0:T(8,128)(2,1)}, bf16[912,128]{1,0:T(8,128)(2,1)S(1)}, u32[]{:S(2)}, u32[]{:S(2)}) collective-permute-start(bf16[912,128]{1,0:T(8,128)(2,1)} %get-tuple-element.17), channel_id=1, source_target_pairs={{0,248},{8,0},{16,8},{24,16},{32,24},{40,32},{48,40},{56,48},{64,5... | collective-permute-start | bytes 700424 | tf_op jit(solution)/shard_map/ppermute | solution.py:17
  59.2 16.3 %collective-permute-start.6 = (bf16[912,128]{1,0:T(8,128)(2,1)}, bf16[912,128]{1,0:T(8,128)(2,1)S(1)}, u32[]{:S(2)}, u32[]{:S(2)}) collective-permute-start(bf16[912,128]{1,0:T(8,128)(2,1)} %get-tuple-element.18), channel_id=1, source_target_pairs={{0,1},{1,2},{2,3},{3,4},{4,5},{5,6},{6,7},{7,0},{8,9},{9,10},{10,1... | collective-permute-start | bytes 700424 | tf_op jit(solution)/shard_map/ppermute | solution.py:17
  63.8 15.6 %collective-permute-start.7 = (bf16[912,128]{1,0:T(8,128)(2,1)}, bf16[912,128]{1,0:T(8,128)(2,1)S(1)}, u32[]{:S(2)}, u32[]{:S(2)}) collective-permute-start(bf16[912,128]{1,0:T(8,128)(2,1)} %get-tuple-element.19), channel_id=1, source_target_pairs={{0,7},{1,0},{2,1},{3,2},{4,3},{5,4},{6,5},{7,6},{8,15},{9,8},{10,9... | collective-permute-start | bytes 700424 | tf_op jit(solution)/shard_map/ppermute | solution.py:17
  66.4 13.1 %copy-start.5 = (bf16[912,128]{1,0:T(8,128)(2,1)}, bf16[912,128]{1,0:T(8,128)(2,1)S(1)}, u32[]{:S(2)}) copy-start(bf16[912,128]{1,0:T(8,128)(2,1)S(1)} %collective-permute-done.5.rest_1_) | copy-start | bytes 700420
  75.5 3.9 %copy-start.6 = (bf16[912,128]{1,0:T(8,128)(2,1)}, bf16[912,128]{1,0:T(8,128)(2,1)S(1)}, u32[]{:S(2)}) copy-start(bf16[912,128]{1,0:T(8,128)(2,1)S(1)} %collective-permute-done.6.rest_2_) | copy-start | bytes 700420
  88.9 23.6 %all-to-all-start = ((bf16[32,24,128]{2,1,0:T(8,128)(2,1)}), bf16[32,24,128]{2,1,0:T(8,128)(2,1)}, u32[]{:S(2)}, u32[]{:S(2)}) async-start(bf16[32,24,128]{2,1,0:T(8,128)(2,1)} %broadcast_in_dim.34), calls=%async_computation | async-start | bytes 393216 | tf_op jit(solution)/shard_map/all_to_all | solution.py:174
  103.1 17.7 %slice-start = ((bf16[912,128]{1,0:T(8,128)(2,1)}), bf16[144,128]{1,0:T(8,128)(2,1)S(1)}, s32[]{:S(2)}) async-start(bf16[912,128]{1,0:T(8,128)(2,1)} %copy-done.5), calls=%async_computation.2 | async-start | bytes 73728 | tf_op jit(solution)/shard_map/slice | solution.py:251
  103.1 17.8 %slice-start.1 = ((bf16[912,128]{1,0:T(8,128)(2,1)}), bf16[144,128]{1,0:T(8,128)(2,1)S(1)}, s32[]{:S(2)}) async-start(bf16[912,128]{1,0:T(8,128)(2,1)} %copy-done.6), calls=%async_computation.3 | async-start | bytes 73728 | tf_op jit(solution)/shard_map/slice | solution.py:251
  103.2 17.9 %slice-start.2 = ((bf16[912,128]{1,0:T(8,128)(2,1)}), bf16[144,128]{1,0:T(8,128)(2,1)S(1)}, s32[]{:S(2)}) async-start(bf16[912,128]{1,0:T(8,128)(2,1)} %copy-done.7), calls=%async_computation.4 | async-start | bytes 73728 | tf_op jit(solution)/shard_map/slice | solution.py:251
  103.2 29.4 %copy-start.4 = (bf16[6,12,192]{2,1,0:T(8,128)(2,1)S(1)}, bf16[6,12,192]{2,1,0:T(8,128)(2,1)}, u32[]{:S(2)}) copy-start(bf16[6,12,192]{2,1,0:T(8,128)(2,1)} %copy-done.3) | copy-start | bytes 82948
  114.4 18.6 %copy-start.2 = (f32[12,192,128]{2,1,0:T(8,128)S(1)}, f32[12,192,128]{2,1,0:T(8,128)}, u32[]{:S(2)}) copy-start(f32[12,192,128]{2,1,0:T(8,128)} %get-tuple-element.20) | copy-start | bytes 3538948
  114.4 10.9 %all-to-all-start.1 = ((f32[8,24,128]{2,1,0:T(8,128)}), f32[8,24,128]{2,1,0:T(8,128)S(1)}, u32[]{:S(2)}, u32[]{:S(2)}) async-start(f32[8,24,128]{2,1,0:T(8,128)} %bitcast.127), calls=%async_computation.1 | async-start | bytes 196608 | tf_op jit(solution)/shard_map/all_to_all | solution.py:262
  125.3 15.6 %collective-permute-start.10 = (bf16[24,128]{1,0:T(8,128)(2,1)S(1)}, bf16[24,128]{1,0:T(8,128)(2,1)S(1)}, u32[]{:S(2)}, u32[]{:S(2)}) collective-permute-start(bf16[24,128]{1,0:T(8,128)(2,1)S(1)} %reduce_sum.9), channel_id=1, source_target_pairs={{0,1},{1,2},{2,3},{3,4},{4,5},{5,6},{6,7},{7,0},{8,9},{9,10},{10,1... | collective-permute-start | bytes 18440 | tf_op jit(solution)/shard_map/ppermute | solution.py:17
  126.8 13.2 %collective-permute-start.9 = (bf16[24,128]{1,0:T(8,128)(2,1)S(1)}, bf16[24,128]{1,0:T(8,128)(2,1)S(1)}, u32[]{:S(2)}, u32[]{:S(2)}) collective-permute-start(bf16[24,128]{1,0:T(8,128)(2,1)S(1)} %reduce_sum.9), channel_id=1, source_target_pairs={{0,248},{8,0},{16,8},{24,16},{32,24},{40,32},{48,40},{56,48},{64,5... | collective-permute-start | bytes 18440 | tf_op jit(solution)/shard_map/ppermute | solution.py:17
  128.4 10.6 %collective-permute-start.8 = (bf16[24,128]{1,0:T(8,128)(2,1)S(1)}, bf16[24,128]{1,0:T(8,128)(2,1)S(1)}, u32[]{:S(2)}, u32[]{:S(2)}) collective-permute-start(bf16[24,128]{1,0:T(8,128)(2,1)S(1)} %reduce_sum.9), channel_id=1, source_target_pairs={{0,8},{8,16},{16,24},{24,32},{32,40},{40,48},{48,56},{56,64},{64,7... | collective-permute-start | bytes 18440 | tf_op jit(solution)/shard_map/ppermute | solution.py:17
  132.2 3.1 %collective-permute-start.11 = (bf16[24,128]{1,0:T(8,128)(2,1)S(1)}, bf16[24,128]{1,0:T(8,128)(2,1)S(1)}, u32[]{:S(2)}, u32[]{:S(2)}) collective-permute-start(bf16[24,128]{1,0:T(8,128)(2,1)S(1)} %reduce_sum.9), channel_id=1, source_target_pairs={{0,7},{1,0},{2,1},{3,2},{4,3},{5,4},{6,5},{7,6},{8,15},{9,8},{10,9... | collective-permute-start | bytes 18440 | tf_op jit(solution)/shard_map/ppermute | solution.py:17
  (3 other events, 2.8 us)
